TPU v7x, 256 devices: a whole 4x4x8 slice. The times are simulated.
256 devices in a mesh: dp: 4 (over y_lo, core), block: 64 (over x, y_hi, z).
Axes of the slice: x: 4, y: 4 (y_hi: 2, y_lo: 2; y = y_hi * 2 + y_lo), z: 8, core: 2. Of those that a mesh axis runs over, the one named last changes fastest.
Arguments:
- tokens: bfloat16 [4096, 16384], P('dp', 'block'), may hold values from -6 to 6
- cotangent: bfloat16 [4096, 16384], P('dp', 'block'), may hold values from -6 to 6
- up_width: bfloat16 [64, 256, 1024], P('block'), may hold values from -0.375 to 0.375
- up_hidden: bfloat16 [256, 256, 256], P('block'), may hold values from -0.375 to 0.375
- down_hidden: bfloat16 [256, 256, 256], P('block'), may hold values from -0.375 to 0.375
- down_width: bfloat16 [64, 1024, 256], P('block'), may hold values from -0.1875 to 0.1875
Outputs:
- layer_out: bfloat16 [4096, 16384], P('dp', 'block')
- tokens_grad: bfloat16 [4096, 16384], P('dp', 'block')
- up_width_grad: float32 [64, 256, 1024], P('block')
- up_hidden_grad: float32 [256, 256, 256], P('block')
- down_hidden_grad: float32 [256, 256, 256], P('block')
- down_width_grad: float32 [64, 1024, 256], P('block')
All inputs are finite; a program needn't handle non-finite values.
Results may differ from a plain program's by a relative error of at most 0.014.
Values may be sent and summed in bfloat16 or wider, within the bound.
No kernel may reach another device: no remote copies, remote signals or barrier semaphores. Data moves between devices by JAX's collectives and lax.ppermute only.
A program may use at most 64 MiB of HBM per device.

v0:
```python
import math

import jax
import jax.numpy as jnp
from jax import lax
from jax.sharding import PartitionSpec as P


def gelu_exact(value):
    return 0.5 * value * (1.0 + jax.scipy.special.erf(value / math.sqrt(2.0)))


def gelu_slope(value):
    return 0.5 * (1.0 + jax.scipy.special.erf(value / math.sqrt(2.0))) + value * jnp.exp(
        -0.5 * value * value
    ) / math.sqrt(2.0 * math.pi)


def contract_rows(left, right):
    return lax.dot_general(
        left, right, (((0,), (0,)), ((), ())), preferred_element_type=jnp.float32
    )


def contract_cols(left, right):
    return lax.dot_general(
        left, right, (((1,), (1,)), ((), ())), preferred_element_type=jnp.float32
    )


def shards(tokens, cotangent, up_width, up_hidden, down_hidden, down_width):
    row_count = tokens.shape[0]
    block_size = tokens.shape[1]
    expand = up_width.shape[2] // block_size
    grad_scale = 1.0 / math.sqrt(row_count * lax.axis_size("dp"))
    expanded = jnp.dot(tokens, up_width[0], preferred_element_type=jnp.float32).astype(jnp.bfloat16)
    hidden_tiles = lax.all_to_all(
        expanded.reshape(row_count, block_size, expand),
        "block",
        split_axis=1,
        concat_axis=2,
        tiled=True,
    )
    pre_act = jnp.einsum(
        "tkg,kgm->tkm", hidden_tiles, up_hidden, preferred_element_type=jnp.float32
    )
    active = gelu_exact(pre_act).astype(jnp.bfloat16)
    back_rows = jnp.einsum(
        "tkm,kmn->tkn", active, down_hidden, preferred_element_type=jnp.float32
    ).astype(jnp.bfloat16)
    portion = lax.all_to_all(back_rows, "block", split_axis=2, concat_axis=1, tiled=True)
    flattened = portion.reshape(portion.shape[0], block_size * expand)
    gathered_rows = flattened
    layer_out = jnp.dot(flattened, down_width[0], preferred_element_type=jnp.float32).astype(
        jnp.bfloat16
    )
    out_rows_grad = contract_cols(cotangent, down_width[0]).astype(jnp.bfloat16)
    down_width_grad = contract_rows(gathered_rows, cotangent)[None]
    grad_tiles = lax.all_to_all(
        out_rows_grad.reshape(row_count, block_size, expand),
        "block",
        split_axis=1,
        concat_axis=2,
        tiled=True,
    )
    down_hidden_grad = jnp.einsum(
        "tkm,tkn->kmn", active, grad_tiles, preferred_element_type=jnp.float32
    )
    act_grad = jnp.einsum(
        "tkn,kmn->tkm", grad_tiles, down_hidden, preferred_element_type=jnp.float32
    )
    pre_grad = (act_grad * gelu_slope(pre_act)).astype(jnp.bfloat16)
    up_hidden_grad = jnp.einsum(
        "tkg,tkm->kgm", hidden_tiles, pre_grad, preferred_element_type=jnp.float32
    )
    tile_grad = jnp.einsum(
        "tkm,kgm->tkg", pre_grad, up_hidden, preferred_element_type=jnp.float32
    ).astype(jnp.bfloat16)
    portion = lax.all_to_all(tile_grad, "block", split_axis=2, concat_axis=1, tiled=True)
    flattened = portion.reshape(portion.shape[0], block_size * expand)
    tokens_grad = contract_cols(flattened, up_width[0]).astype(jnp.bfloat16)
    up_width_grad = contract_rows(tokens, flattened)[None]
    summed = (
        lax.psum(up_width_grad.astype(jnp.bfloat16), "dp").astype(jnp.float32),
        lax.psum(up_hidden_grad.astype(jnp.bfloat16), "dp").astype(jnp.float32),
        lax.psum(down_hidden_grad.astype(jnp.bfloat16), "dp").astype(jnp.float32),
        lax.psum(down_width_grad.astype(jnp.bfloat16), "dp").astype(jnp.float32),
    )
    results = tuple((member * grad_scale for member in summed))
    return (layer_out, tokens_grad, results[0], results[1], results[2], results[3])


def solution(mesh):
    in_specs = (
        P("dp", "block"),
        P("dp", "block"),
        P("block", None, None),
        P("block", None, None),
        P("block", None, None),
        P("block", None, None),
    )
    out_specs = (
        P("dp", "block"),
        P("dp", "block"),
        P("block", None, None),
        P("block", None, None),
        P("block", None, None),
        P("block", None, None),
    )
    return jax.shard_map(shards, mesh=mesh, in_specs=in_specs, out_specs=out_specs, check_vma=False)
```

profile of v0, /device:TPU:1, one launch (start us, length us, event | category | flops | bytes accessed | tf_op | source)
XLA Modules:
  0.0 333.6 jit_solution(801734257422933790)
XLA Ops:
  7.2 2.0 convolution_convert_fusion.1
  9.2 2.2 reshape.28
  11.4 15.5 %all-to-all-start = ((bf16[1024,256,4]{0,2,1:T(4,128)(2,1)}), bf16[1024,256,4]{0,2,1:T(4,128)(2,1)}, u32[]{:S(2)}, u32[]{:S(2)}) async-start(bf16[1024,256,4]{0,2,1:T(4,128)(2,1)} %reshape.28), calls=%async_computation | async-start | bytes 4194304 | tf_op jit(solution)/shard_map/all_to_all | solution.py:37
  26.9 1.8 convolution_convert_fusion
  28.7 2.3 reshape.30
  31.0 44.8 %all-to-all-done = bf16[1024,256,4]{0,2,1:T(4,128)(2,1)} async-done(((bf16[1024,256,4]{0,2,1:T(4,128)(2,1)}), bf16[1024,256,4]{0,2,1:T(4,128)(2,1)}, u32[]{:S(2)}, u32[]{:S(2)}) %all-to-all-start) | async-done | bytes 2097184 | tf_op jit(solution)/shard_map/all_to_all | solution.py:37
  75.8 9.5 %all-to-all-start.2 = ((bf16[1024,256,4]{0,2,1:T(4,128)(2,1)}), bf16[1024,256,4]{0,2,1:T(4,128)(2,1)}, u32[]{:S(2)}, u32[]{:S(2)}) async-start(bf16[1024,256,4]{0,2,1:T(4,128)(2,1)} %reshape.30), calls=%async_computation.2 | async-start | bytes 4194304 | tf_op jit(solution)/shard_map/all_to_all | solution.py:59
  85.2 2.7 copy.39
  87.9 3.7 %fusion.7 = (bf16[1024,4,256]{2,0,1:T(8,128)(2,1)S(1)}, f32[4,1024,256]{2,1,0:T(8,128)}) fusion(bf16[4,256,256]{2,1,0:T(8,128)(2,1)S(1)} %copy-done, bf16[1024,4,256]{0,1,2:T(4,128)(2,1)S(1)} %bitcast.78), kind=kOutput, calls=%fused_computation.10 | convolution fusion | flops 542113792 | bytes 8912896 | tf_op jit(solution)/shard_map/tkg,kgm->tkm/dot_general | solution.py:44
  91.6 2.0 convert_bitcast_fusion.1
  93.7 4.6 %copy.41 = bf16[1024,4,256]{0,1,2:T(4,128)(2,1)} copy(bf16[1024,4,256]{2,0,1:T(8,128)(2,1)} %convert_bitcast_fusion.1) | data formatting | bytes 4194304 | tf_op jit(solution)/shard_map/convert_element_type | solution.py:50
  98.3 35.2 %all-to-all-done.2 = bf16[1024,256,4]{0,2,1:T(4,128)(2,1)} async-done(((bf16[1024,256,4]{0,2,1:T(4,128)(2,1)}), bf16[1024,256,4]{0,2,1:T(4,128)(2,1)}, u32[]{:S(2)}, u32[]{:S(2)}) %all-to-all-start.2) | async-done | bytes 2097184 | tf_op jit(solution)/shard_map/all_to_all | solution.py:59
  133.4 10.2 %all-to-all-start.1 = ((bf16[1024,4,256]{0,1,2:T(4,128)(2,1)}), bf16[1024,4,256]{0,1,2:T(4,128)(2,1)}, u32[]{:S(2)}, u32[]{:S(2)}) async-start(bf16[1024,4,256]{0,1,2:T(4,128)(2,1)} %copy.41), calls=%async_computation.1 | async-start | bytes 4194304 | tf_op jit(solution)/shard_map/all_to_all | solution.py:51
  143.7 4.0 %copy.43 = bf16[1024,4,64,4]{0,1,3,2:T(4,128)(2,1)} copy(bf16[1024,4,64,4]{0,3,1,2:T(4,128)(2,1)} %bitcast.10) | data formatting | bytes 4194304 | tf_op jit(solution)/shard_map/all_to_all | solution.py:59
  147.6 4.3 %copy.44 = bf16[1024,4,256]{2,0,1:T(8,128)(2,1)} copy(bf16[1024,4,256]{0,1,2:T(4,128)(2,1)} %bitcast.80) | data formatting | bytes 4194304 | tf_op jit(solution)/shard_map/all_to_all | solution.py:59
  151.9 4.0 %fusion.5 = bf16[1024,4,256]{2,0,1:T(8,128)(2,1)S(1)} fusion(f32[4,1024,256]{2,1,0:T(8,128)} %get-tuple-element.35, bf16[1024,4,256]{2,0,1:T(8,128)(2,1)} %copy.44, bf16[4,256,256]{2,1,0:T(8,128)(2,1)} %param.10), kind=kOutput, calls=%fused_computation.6 | convolution fusion | flops 547356672 | bytes 8912896 | tf_op jit(solution)/shard_map/tkn,kmn->tkm/dot_general | solution.py:69
  157.3 2.1 convert_bitcast_fusion
  159.3 4.5 %copy.45 = bf16[1024,4,256]{0,1,2:T(4,128)(2,1)} copy(bf16[1024,4,256]{2,0,1:T(8,128)(2,1)} %convert_bitcast_fusion) | data formatting | bytes 4194304 | tf_op jit(solution)/shard_map/convert_element_type | solution.py:78
  163.9 27.8 %all-to-all-done.1 = bf16[1024,4,256]{0,1,2:T(4,128)(2,1)} async-done(((bf16[1024,4,256]{0,1,2:T(4,128)(2,1)}), bf16[1024,4,256]{0,1,2:T(4,128)(2,1)}, u32[]{:S(2)}, u32[]{:S(2)}) %all-to-all-start.1) | async-done | bytes 2097184 | tf_op jit(solution)/shard_map/all_to_all | solution.py:51
  191.6 10.0 %all-to-all-start.3 = ((bf16[1024,4,256]{0,1,2:T(4,128)(2,1)}), bf16[1024,4,256]{0,1,2:T(4,128)(2,1)}, u32[]{:S(2)}, u32[]{:S(2)}) async-start(bf16[1024,4,256]{0,1,2:T(4,128)(2,1)} %copy.45), calls=%async_computation.3 | async-start | bytes 4194304 | tf_op jit(solution)/shard_map/all_to_all | solution.py:79
  201.7 3.4 %convolution_convert_fusion.6 = bf16[4,256,256]{2,1,0:T(8,128)(2,1)} fusion(bf16[1024,4,256]{2,0,1:T(8,128)(2,1)S(1)} %get-tuple-element.34, bf16[1024,4,256]{2,0,1:T(8,128)(2,1)} %copy.44), kind=kOutput, calls=%fused_computation.26 | convolution fusion | flops 537133056 | bytes 4718592 | tf_op jit(solution)/shard_map/tkm,tkn->kmn/dot_general | solution.py:66
  205.1 1.6 fusion.14
  206.8 2.7 copy.42
  209.4 2.0 reshape.29
  211.5 38.4 %all-to-all-done.3 = bf16[1024,4,256]{0,1,2:T(4,128)(2,1)} async-done(((bf16[1024,4,256]{0,1,2:T(4,128)(2,1)}), bf16[1024,4,256]{0,1,2:T(4,128)(2,1)}, u32[]{:S(2)}, u32[]{:S(2)}) %all-to-all-start.3) | async-done | bytes 2097184 | tf_op jit(solution)/shard_map/all_to_all | solution.py:79
  249.8 2.7 copy.46
  252.5 2.1 reshape.31
  254.6 3.3 fusion.17
  260.4 3.2 convolution_convert_fusion.4
  263.7 1.6 convolution_convert_fusion.5
  265.2 56.5 %all-reduce.3.cloned.1.call-done = (bf16[1,256,1024]{1,2,0:T(8,128)(2,1)}, bf16[4,256,256]{2,1,0:T(8,128)(2,1)}, bf16[4,256,256]{2,1,0:T(8,128)(2,1)}, bf16[1,1024,256]{2,1,0:T(8,128)(2,1)}) async-done(((bf16[1,256,1024]{1,2,0:T(8,128)(2,1)}, bf16[4,256,256]{2,1,0:T(8,128)(2,1)}, bf16[4,256,256]{2,1,0:T(8,128)(2,1)}, bf16[1,1024,256]{2,1,0:T(8,128)(2,1)}), (bf16[1,256,1024]{1,2,0:T(8,128)(2,1)}, ...) | async-done | bytes 2097168 | tf_op jit(solution)/shard_map/psum | solution.py:84
  325.2 1.5 convert_multiply_fusion.1
  (32 shorter events, 7.4 us)
Async XLA Ops:
  7.2 80.8 %copy-start = (bf16[4,256,256]{2,1,0:T(8,128)(2,1)S(1)}, bf16[4,256,256]{2,1,0:T(8,128)(2,1)}, u32[]{:S(2)}) copy-start(bf16[4,256,256]{2,1,0:T(8,128)(2,1)} %param.9) | copy-start | bytes 1572868
  11.4 15.5 %copy-start.6 = (bf16[1024,256]{1,0:T(8,128)(2,1)S(1)}, bf16[1024,256]{1,0:T(8,128)(2,1)}, u32[]{:S(2)}) copy-start(bf16[1024,256]{1,0:T(8,128)(2,1)} %param.7) | copy-start | bytes 1572868
  11.4 64.3 %all-to-all-start = ((bf16[1024,256,4]{0,2,1:T(4,128)(2,1)}), bf16[1024,256,4]{0,2,1:T(4,128)(2,1)}, u32[]{:S(2)}, u32[]{:S(2)}) async-start(bf16[1024,256,4]{0,2,1:T(4,128)(2,1)} %reshape.28), calls=%async_computation | async-start | bytes 4194304 | tf_op jit(solution)/shard_map/all_to_all | solution.py:37
  75.8 57.7 %all-to-all-start.2 = ((bf16[1024,256,4]{0,2,1:T(4,128)(2,1)}), bf16[1024,256,4]{0,2,1:T(4,128)(2,1)}, u32[]{:S(2)}, u32[]{:S(2)}) async-start(bf16[1024,256,4]{0,2,1:T(4,128)(2,1)} %reshape.30), calls=%async_computation.2 | async-start | bytes 4194304 | tf_op jit(solution)/shard_map/all_to_all | solution.py:59
  87.9 3.7 %copy-start.1 = (bf16[1024,4,64,4]{0,1,3,2:T(4,128)(2,1)}, bf16[1024,4,64,4]{0,1,3,2:T(4,128)(2,1)S(1)}, u32[]{:S(2)}) copy-start(bf16[1024,4,64,4]{0,1,3,2:T(4,128)(2,1)S(1)} %copy.39) | copy-start | bytes 6291460
  87.9 3.7 %copy-start.7 = (bf16[4,256,256]{2,1,0:T(8,128)(2,1)S(1)}, bf16[4,256,256]{2,1,0:T(8,128)(2,1)}, u32[]{:S(2)}) copy-start(bf16[4,256,256]{2,1,0:T(8,128)(2,1)} %param.10) | copy-start | bytes 1572868
  133.4 58.2 %all-to-all-start.1 = ((bf16[1024,4,256]{0,1,2:T(4,128)(2,1)}), bf16[1024,4,256]{0,1,2:T(4,128)(2,1)}, u32[]{:S(2)}, u32[]{:S(2)}) async-start(bf16[1024,4,256]{0,1,2:T(4,128)(2,1)} %copy.41), calls=%async_computation.1 | async-start | bytes 4194304 | tf_op jit(solution)/shard_map/all_to_all | solution.py:51
  156.0 1.3 copy-start.4
  191.6 58.2 %all-to-all-start.3 = ((bf16[1024,4,256]{0,1,2:T(4,128)(2,1)}), bf16[1024,4,256]{0,1,2:T(4,128)(2,1)}, u32[]{:S(2)}, u32[]{:S(2)}) async-start(bf16[1024,4,256]{0,1,2:T(4,128)(2,1)} %copy.45), calls=%async_computation.3 | async-start | bytes 4194304 | tf_op jit(solution)/shard_map/all_to_all | solution.py:79
  201.7 120.0 %all-reduce.3.cloned.1.call-start = ((), (), s32[]{:S(2)}) async-start(), calls=%async_computation.4 | async-start | bytes 4194304 | tf_op jit(solution)/shard_map/psum | solution.py:84
  201.7 3.4 %copy-start.2 = (bf16[1024,4,64,4]{0,1,3,2:T(4,128)(2,1)S(1)}, bf16[1024,4,64,4]{0,1,3,2:T(4,128)(2,1)}, u32[]{:S(2)}) copy-start(bf16[1024,4,64,4]{0,1,3,2:T(4,128)(2,1)} %copy-done.1) | copy-start | bytes 6291460
  201.7 3.4 %copy-start.5 = (bf16[1024,4,256]{2,0,1:T(8,128)(2,1)S(1)}, bf16[1024,4,256]{2,0,1:T(8,128)(2,1)}, u32[]{:S(2)}) copy-start(bf16[1024,4,256]{2,0,1:T(8,128)(2,1)} %copy-done.4) | copy-start | bytes 6291460
  254.6 3.3 copy-start.3
  259.4 1.0 copy-start.10
  260.4 3.2 copy-start.8
  321.7 2.5 copy-start.9
  322.9 2.4 copy-start.11
  322.9 2.4 copy-start.12
Sparse Core Ops, SparseCore 0:
  259.6 62.0 all-reduce.2
where the time goes:
time: 335 us; the launch traced here: 334 us
  waiting for transfers between devices  203 us (61%)
  starting transfers between devices  45.3 us (14%)
  local copies, waits for them, and re-layouts  37.7 us (11%)
  matrix products  30.2 us (9%)
  between operations  14.2 us (4%)
  other arithmetic  3.72 us (1%)
    psum x1, waiting for transfers between devices, shards(): lax.psum(up_width_grad.astype(jnp.bfloat16), 'dp').astype(jnp.float32)  56.5 us
    all_to_all x1, waiting for transfers between devices, shards(): lax.all_to_all(expanded.reshape(row_count, block_size, expand), 'block',...  44.8 us
    all_to_all x1, waiting for transfers between devices, shards(): lax.all_to_all(tile_grad, 'block', split_axis=2, concat_axis=1, tiled=True)  38.4 us
    all_to_all x1, waiting for transfers between devices, shards(): lax.all_to_all(out_rows_grad.reshape(row_count, block_size, expand), 'blo...  35.2 us
    all_to_all x1, waiting for transfers between devices, shards(): lax.all_to_all(back_rows, 'block', split_axis=2, concat_axis=1, tiled=True)  27.8 us
    all_to_all x1, starting transfers between devices, shards(): lax.all_to_all(expanded.reshape(row_count, block_size, expand), 'block',...  15.5 us
    all_to_all x1, starting transfers between devices, shards(): lax.all_to_all(back_rows, 'block', split_axis=2, concat_axis=1, tiled=True)  10.2 us
    all_to_all x1, starting transfers between devices, shards(): lax.all_to_all(tile_grad, 'block', split_axis=2, concat_axis=1, tiled=True)  10 us
  transfers between devices with their start and end apart: 5, of which 5 were waited for; matrix products, arithmetic and copies ran while one was open for 15% of the time, Pallas kernels for 0%

commit v1 on v0

v1 whole, which is shorter than its diff:
```python
import math

import jax
import jax.numpy as jnp
from jax import lax
from jax.sharding import PartitionSpec as P


def gelu_exact(value):
    return 0.5 * value * (1.0 + jax.scipy.special.erf(value / math.sqrt(2.0)))


def gelu_slope(value):
    return 0.5 * (1.0 + jax.scipy.special.erf(value / math.sqrt(2.0))) + value * jnp.exp(
        -0.5 * value * value
    ) / math.sqrt(2.0 * math.pi)


def dot(left, right, left_dims, right_dims, batch=((), ())):
    return lax.dot_general(
        left, right, ((left_dims, right_dims), batch), preferred_element_type=jnp.float32
    )


def shards(tokens, cotangent, up_width, up_hidden, down_hidden, down_width):
    row_count, block_size = tokens.shape
    nb = lax.axis_size("block")
    local_blocks, hidden_size, _ = up_hidden.shape
    expand = up_width.shape[2] // block_size
    chunk = local_blocks * expand
    grad_scale = 1.0 / math.sqrt(row_count * lax.axis_size("dp"))
    uw = up_width[0]
    dw = down_width[0]

    expanded_t = dot(uw, tokens, (0,), (1,)).astype(jnp.bfloat16)
    out_grad_t = dot(dw, cotangent, (1,), (1,)).astype(jnp.bfloat16)
    send = jnp.stack(
        [expanded_t.reshape(nb, chunk, row_count), out_grad_t.reshape(nb, chunk, row_count)], axis=1
    )
    recv = lax.all_to_all(send, "block", 0, 0, tiled=True)
    recv = recv.reshape(nb, 2, local_blocks, expand, row_count)
    hidden_t = recv[:, 0].transpose(1, 0, 2, 3).reshape(local_blocks, nb * expand, row_count)
    grad_t = recv[:, 1].transpose(1, 0, 2, 3).reshape(local_blocks, nb * expand, row_count)

    pre_act = dot(up_hidden, hidden_t, (1,), (1,), ((0,), (0,)))
    active = gelu_exact(pre_act).astype(jnp.bfloat16)
    back_t = dot(down_hidden, active, (1,), (1,), ((0,), (0,))).astype(jnp.bfloat16)
    act_grad = dot(down_hidden, grad_t, (2,), (1,), ((0,), (0,)))
    pre_grad = (act_grad * gelu_slope(pre_act)).astype(jnp.bfloat16)
    tile_grad_t = dot(up_hidden, pre_grad, (2,), (1,), ((0,), (0,))).astype(jnp.bfloat16)
    down_hidden_grad = dot(active, grad_t, (2,), (2,), ((0,), (0,)))
    up_hidden_grad = dot(hidden_t, pre_grad, (2,), (2,), ((0,), (0,)))
    dhg = lax.psum(down_hidden_grad.astype(jnp.bfloat16), "dp").astype(jnp.float32)
    uhg = lax.psum(up_hidden_grad.astype(jnp.bfloat16), "dp").astype(jnp.float32)

    send2 = jnp.stack([back_t, tile_grad_t], axis=0).reshape(2, local_blocks, nb, expand, row_count)
    send2 = send2.transpose(2, 0, 1, 3, 4)
    recv2 = lax.all_to_all(send2, "block", 0, 0, tiled=True)
    rows_t = recv2[:, 0].reshape(nb * chunk, row_count)
    rows_grad_t = recv2[:, 1].reshape(nb * chunk, row_count)

    layer_out = dot(rows_t, dw, (0,), (0,)).astype(jnp.bfloat16)
    down_width_grad = dot(rows_t, cotangent, (1,), (0,))
    tokens_grad = dot(rows_grad_t, uw, (0,), (1,)).astype(jnp.bfloat16)
    up_width_grad = dot(tokens, rows_grad_t, (0,), (1,))
    dwg = lax.psum(down_width_grad.astype(jnp.bfloat16), "dp").astype(jnp.float32)
    uwg = lax.psum(up_width_grad.astype(jnp.bfloat16), "dp").astype(jnp.float32)
    return (
        layer_out,
        tokens_grad,
        (uwg * grad_scale)[None],
        uhg * grad_scale,
        dhg * grad_scale,
        (dwg * grad_scale)[None],
    )


def solution(mesh):
    in_specs = (
        P("dp", "block"),
        P("dp", "block"),
        P("block", None, None),
        P("block", None, None),
        P("block", None, None),
        P("block", None, None),
    )
    out_specs = in_specs
    return jax.shard_map(shards, mesh=mesh, in_specs=in_specs, out_specs=out_specs, check_vma=False)
```

time: 335 us -> 348 us (1.039)
  blocking collectives: 0 us -> 109 us
  waiting for transfers between devices: 203 us -> 144 us
  starting transfers between devices: 45.3 us -> 9.5 us
  local copies, waits for them, and re-layouts: 37.7 us -> 29.8 us
  other arithmetic: 3.72 us -> 9.94 us
    all_to_all x0 -> x1, blocking collectives: none -> 109 us  [shards(): recv = lax.all_to_all(send, 'block', 0, 0, tiled=True)]
    all_to_all x4 -> x1, waiting for transfers between devices: 146 us -> 86.2 us  [shards(): recv2 = lax.all_to_all(send2, 'block', 0, 0, tiled=True)]
    all_to_all x4 -> x1, starting transfers between devices: 45.2 us -> 9.46 us  [shards(): recv2 = lax.all_to_all(send2, 'block', 0, 0, tiled=True)]
    another operation x0 -> x4, local copies, waits for them, and re-layouts: none -> 14.3 us  [the longest x2 8.29 us: shards(): jnp.stack([back_t, tile_grad_t], axis=0)]
    all_to_all x5 -> x1, local copies, waits for them, and re-layouts: 16.3 us -> 2.33 us  [shards(): recv = lax.all_to_all(send, 'block', 0, 0, tiled=True)]
    convert_element_type x2 -> x0, local copies, waits for them, and re-layouts: 9.13 us -> none  [the longest x1 4.61 us: shards(): back_rows = jnp.einsum('tkm,kmn->tkn', active, down_hidden, preferred_ele...]
    reshape x4 -> x0, local copies, waits for them, and re-layouts: 8.59 us -> none  [the longest x2 4.1 us: shards(): flattened = portion.reshape(portion.shape[0], block_size * expand)]
    transpose x0 -> x1, other arithmetic: none -> 5.82 us  [shards(): send2 = send2.transpose(2, 0, 1, 3, 4)]
  transfers between devices with their start and end apart: 5 -> 2, of which waited for: 5 -> 2; matrix products, arithmetic and copies ran while one was open for 15% -> 3% of each run, Pallas kernels for 0% -> 0%
where the time goes in v1:
time: 348 us
  waiting for transfers between devices  144 us (41%)
  blocking collectives  109 us (31%)
  matrix products  31 us (9%)
  local copies, waits for them, and re-layouts  29.8 us (9%)
  between operations  14.2 us (4%)
  other arithmetic  9.94 us (3%)
  starting transfers between devices  9.5 us (3%)
    all_to_all x1, blocking collectives, shards(): recv = lax.all_to_all(send, 'block', 0, 0, tiled=True)  109 us
    all_to_all x1, waiting for transfers between devices, shards(): recv2 = lax.all_to_all(send2, 'block', 0, 0, tiled=True)  86.2 us
    psum x1, waiting for transfers between devices, shards(): uwg = lax.psum(up_width_grad.astype(jnp.bfloat16), 'dp').astype(jnp.float32)  58.1 us
    dot_general x12, matrix products, dot(): lax.dot_general(left, right, ((left_dims, right_dims), batch), preferred_...  31 us
    all_to_all x1, starting transfers between devices, shards(): recv2 = lax.all_to_all(send2, 'block', 0, 0, tiled=True)  9.46 us
    another operation x2, local copies, waits for them, and re-layouts, shards(): jnp.stack([back_t, tile_grad_t], axis=0)  8.29 us
  transfers between devices with their start and end apart: 2, of which 2 were waited for; matrix products, arithmetic and copies ran while one was open for 3% of the time, Pallas kernels for 0%

profile of v1, /device:TPU:1, one launch (start us, length us, event | category | flops | bytes accessed | tf_op | source)
XLA Modules:
  0.0 347.7 jit_solution(13198589442776961454)
XLA Ops:
  7.2 2.1 convolution_convert_fusion.1
  9.3 0.7 convolution_convert_fusion
  10.5 108.8 %all_to_all.10 = bf16[64,2,16,1024]{3,2,1,0:T(8,128)(2,1)S(1)} all-to-all(bf16[64,2,16,1024]{3,2,1,0:T(8,128)(2,1)S(1)} %pad_maximum_fusion), channel_id=1, replica_groups=mesh['dp'=4,'block'=64] {'block'}, dimensions={0} | all-to-all | bytes 8388608 | tf_op jit(solution)/shard_map/all_to_all | solution.py:40
  119.3 2.3 copy.52
  121.6 0.6 slice_bitcast_fusion
  122.2 1.6 copy.57
  123.9 1.6 copy.53
  125.5 3.4 fusion.7
  129.0 3.3 fusion.5
  132.2 1.3 copy-done.3
  133.6 2.1 convert_bitcast_fusion
  135.7 4.1 %stack.14 = bf16[1,4,64,4,1024]{4,3,2,1,0:T(4,128)(2,1)} reshape(bf16[4,256,1024]{2,1,0:T(8,128)(2,1)} %convert_bitcast_fusion) | data formatting | bytes 4194304 | tf_op jit(solution)/shard_map/stack | solution.py:56
  139.8 3.7 %convert_bitcast_fusion.1 = bf16[4,256,1024]{2,1,0:T(8,128)(2,1)} fusion(bf16[4,256,1024]{1,2,0:T(8,128)(2,1)} %get-tuple-element.38, bf16[4,256,256]{2,1,0:T(8,128)(2,1)S(1)} %copy-done.7), kind=kOutput, calls=%fused_computation.19 | convolution fusion | flops 537919488 | bytes 4718592 | tf_op jit(solution)/shard_map/dot_general | solution.py:20
  143.5 4.2 %stack.13 = bf16[1,4,64,4,1024]{4,3,2,1,0:T(4,128)(2,1)} reshape(bf16[4,256,1024]{2,1,0:T(8,128)(2,1)} %convert_bitcast_fusion.1) | data formatting | bytes 4194304 | tf_op jit(solution)/shard_map/stack | solution.py:56
  147.7 5.8 %copy_bitcast_fusion = bf16[64,2,4,4,1024]{4,3,2,1,0:T(4,128)(2,1)} fusion(bf16[1,4,64,4,1024]{4,3,2,1,0:T(4,128)(2,1)} %stack.14, bf16[1,4,64,4,1024]{4,3,2,1,0:T(4,128)(2,1)} %stack.13), kind=kLoop, calls=%fused_computation.9 | loop fusion | flops 2097152 | bytes 8388608 | tf_op jit(solution)/shard_map/transpose | solution.py:57
  153.5 9.5 %all-to-all-start.1 = ((bf16[64,2,4,4,1024]{4,3,2,1,0:T(4,128)(2,1)}), bf16[64,2,4,4,1024]{4,3,2,1,0:T(4,128)(2,1)}, u32[]{:S(2)}, u32[]{:S(2)}) async-start(bf16[64,2,4,4,1024]{4,3,2,1,0:T(4,128)(2,1)} %copy_bitcast_fusion), calls=%async_computation.1 | async-start | bytes 8388608 | tf_op jit(solution)/shard_map/all_to_all | solution.py:58
  163.0 4.8 %fusion.20 = bf16[4,256,256]{2,1,0:T(8,128)(2,1)} fusion(bf16[4,256,1024]{1,2,0:T(8,128)(2,1)} %get-tuple-element.38, bf16[4,256,1024]{2,0,1:T(4,128)(2,1)} %bitcast.79), kind=kOutput, calls=%fused_computation.34 | convolution fusion | flops 537133056 | bytes 4718592 | tf_op jit(solution)/shard_map/dot_general | solution.py:20
  167.8 1.6 fusion.17
  169.4 86.2 %all-to-all-done.1 = bf16[64,2,4,4,1024]{4,3,2,1,0:T(4,128)(2,1)} async-done(((bf16[64,2,4,4,1024]{4,3,2,1,0:T(4,128)(2,1)}), bf16[64,2,4,4,1024]{4,3,2,1,0:T(4,128)(2,1)}, u32[]{:S(2)}, u32[]{:S(2)}) %all-to-all-start.1) | async-done | bytes 4194336 | tf_op jit(solution)/shard_map/all_to_all | solution.py:58
  255.6 4.9 %fusion.28 = (bf16[64,1,4,4,1024]{4,3,2,1,0:T(4,128)(2,1)}, bf16[64,1,4,4,1024]{4,3,2,1,0:T(4,128)(2,1)S(1)}) fusion(bf16[64,2,4,4,1024]{4,3,2,1,0:T(4,128)(2,1)} %all-to-all-done.1), kind=kLoop, calls=%fused_computation.44 | loop fusion | bytes 8388608 | tf_op jit(solution)/shard_map/slice | solution.py:60
  260.5 4.0 %reshape_squeeze.7 = bf16[1024,1024]{1,0:T(8,128)(2,1)} reshape(bf16[64,1,4,4,1024]{4,3,2,1,0:T(4,128)(2,1)} %get-tuple-element.34) | data formatting | bytes 4194304 | tf_op jit(solution)/shard_map/reshape;squeeze | solution.py:60
  264.6 3.1 fusion.23
  267.7 2.0 reshape_squeeze.6
  269.7 3.2 convolution_convert_fusion.2
  272.9 1.6 copy-done.5
  274.4 1.6 convolution_convert_fusion.4
  276.1 1.6 convolution_convert_fusion.5
  277.7 58.1 %all-reduce.3.cloned.1.call-done = (bf16[256,1024]{0,1:T(8,128)(2,1)}, bf16[4,256,256]{2,1,0:T(8,128)(2,1)}, bf16[4,256,256]{2,1,0:T(8,128)(2,1)}, bf16[1024,256]{1,0:T(8,128)(2,1)}) async-done(((bf16[256,1024]{0,1:T(8,128)(2,1)}, bf16[4,256,256]{2,1,0:T(8,128)(2,1)}, bf16[4,256,256]{2,1,0:T(8,128)(2,1)}, bf16[1024,256]{1,0:T(8,128)(2,1)}), (bf16[256,1024]{0,1:T(8,128)(2,1)}, ...) | async-done | bytes 2097168 | tf_op jit(solution)/shard_map/psum | solution.py:67
  335.8 1.2 multiply_bitcast_fusion.1
  337.0 1.3 copy.66
  338.3 1.0 multiply_bitcast_fusion
  339.3 1.5 convert_multiply_fusion
  (35 shorter events, 0.7 us)
Async XLA Ops:
  7.2 118.3 %copy-start = (bf16[4,256,256]{2,1,0:T(8,128)(2,1)S(1)}, bf16[4,256,256]{2,1,0:T(8,128)(2,1)}, u32[]{:S(2)}) copy-start(bf16[4,256,256]{2,1,0:T(8,128)(2,1)} %param.9) | copy-start | bytes 1572868
  7.2 2.1 copy-start.13
  7.2 2.1 copy-start.10
  123.9 5.1 %copy-start.2 = (bf16[4,64,4,1024]{3,0,2,1:T(4,128)(2,1)}, bf16[4,64,4,1024]{3,0,2,1:T(4,128)(2,1)S(1)}, u32[]{:S(2)}) copy-start(bf16[4,64,4,1024]{3,0,2,1:T(4,128)(2,1)S(1)} %copy.57) | copy-start | bytes 6291460
  125.5 3.4 copy-start.7
  132.2 1.3 copy-start.3
  153.5 102.1 %all-to-all-start.1 = ((bf16[64,2,4,4,1024]{4,3,2,1,0:T(4,128)(2,1)}), bf16[64,2,4,4,1024]{4,3,2,1,0:T(4,128)(2,1)}, u32[]{:S(2)}, u32[]{:S(2)}) async-start(bf16[64,2,4,4,1024]{4,3,2,1,0:T(4,128)(2,1)} %copy_bitcast_fusion), calls=%async_computation.1 | async-start | bytes 8388608 | tf_op jit(solution)/shard_map/all_to_all | solution.py:58
  162.9 172.8 %all-reduce.3.cloned.1.call-start = ((), (), s32[]{:S(2)}) async-start(), calls=%async_computation.2 | async-start | bytes 4194304 | tf_op jit(solution)/shard_map/psum | solution.py:67
  163.0 4.8 %copy-start.4 = (bf16[4,256,1024]{1,2,0:T(8,128)(2,1)S(1)}, bf16[4,256,1024]{1,2,0:T(8,128)(2,1)}, u32[]{:S(2)}) copy-start(bf16[4,256,1024]{1,2,0:T(8,128)(2,1)} %copy-done.3) | copy-start | bytes 6291460
  260.5 4.0 %copy-start.9 = (bf16[1024,256]{1,0:T(8,128)(2,1)S(1)}, bf16[1024,256]{1,0:T(8,128)(2,1)}, u32[]{:S(2)}) copy-start(bf16[1024,256]{1,0:T(8,128)(2,1)} %param.6) | copy-start | bytes 1572868
  267.7 2.0 copy-start.11
  269.7 3.2 copy-start.12
  272.8 1.6 copy-start.5
  274.4 1.6 copy-start.6
  274.4 1.7 copy-start.14
  335.8 2.5 copy-start.8
  336.9 2.4 copy-start.15
  337.0 2.4 copy-start.16
  338.3 2.6 copy-start.1
Sparse Core Ops, SparseCore 0:
  273.0 62.7 all-reduce.2

commit v2 on v1

v2 whole, which is shorter than its diff:
```python
import math

import jax
import jax.numpy as jnp
from jax import lax
from jax.sharding import PartitionSpec as P

CHUNKS = 2


def gelu_exact(value):
    return 0.5 * value * (1.0 + jax.scipy.special.erf(value / math.sqrt(2.0)))


def gelu_slope(value):
    return 0.5 * (1.0 + jax.scipy.special.erf(value / math.sqrt(2.0))) + value * jnp.exp(
        -0.5 * value * value
    ) / math.sqrt(2.0 * math.pi)


def dot(left, right, left_dims, right_dims, batch=((), ())):
    return lax.dot_general(
        left, right, ((left_dims, right_dims), batch), preferred_element_type=jnp.float32
    )


def pick(pair, index):
    return lax.dynamic_index_in_dim(pair, index, axis=0, keepdims=False)


def dp_sum(grad):
    size = lax.axis_size("dp")
    index = lax.axis_index("dp")
    core = index % 2
    row = index // 2
    core_swap = [(i, i ^ 1) for i in range(size)]
    row_swap = [(i, i ^ 2) for i in range(size)]
    parts = grad.astype(jnp.bfloat16).reshape(2, 2, -1)
    got = lax.ppermute(pick(parts, 1 - core), "dp", core_swap)
    half = pick(parts, core).astype(jnp.float32) + got.astype(jnp.float32)
    got = lax.ppermute(pick(half, 1 - row).astype(jnp.bfloat16), "dp", row_swap)
    quarter = (pick(half, row) + got.astype(jnp.float32)).astype(jnp.bfloat16)
    got = lax.ppermute(quarter, "dp", row_swap)
    half = jnp.where(row == 0, jnp.stack([quarter, got]), jnp.stack([got, quarter]))
    got = lax.ppermute(half, "dp", core_swap)
    full = jnp.where(core == 0, jnp.stack([half, got]), jnp.stack([got, half]))
    return full.reshape(grad.shape).astype(jnp.float32)


def shards(tokens, cotangent, up_width, up_hidden, down_hidden, down_width):
    total_rows, block_size = tokens.shape
    nb = lax.axis_size("block")
    local_blocks = up_hidden.shape[0]
    expand = up_width.shape[2] // block_size
    chunk = local_blocks * expand
    grad_scale = 1.0 / math.sqrt(total_rows * lax.axis_size("dp"))
    uw = up_width[0]
    dw = down_width[0]
    rows = total_rows // CHUNKS

    outs, tgrads = [], []
    dhg = uhg = dwg = uwg = None
    for step in range(CHUNKS):
        x = tokens[step * rows:(step + 1) * rows]
        c = cotangent[step * rows:(step + 1) * rows]
        expanded_t = dot(uw, x, (0,), (1,)).astype(jnp.bfloat16)
        out_grad_t = dot(dw, c, (1,), (1,)).astype(jnp.bfloat16)
        send = jnp.stack(
            [expanded_t.reshape(nb, chunk, rows), out_grad_t.reshape(nb, chunk, rows)], axis=1
        )
        recv = lax.all_to_all(send, "block", 0, 0, tiled=True)
        recv = recv.reshape(nb, 2, local_blocks, expand, rows)
        hidden_t = recv[:, 0].transpose(1, 0, 2, 3).reshape(local_blocks, nb * expand, rows)
        grad_t = recv[:, 1].transpose(1, 0, 2, 3).reshape(local_blocks, nb * expand, rows)

        pre_act = dot(up_hidden, hidden_t, (1,), (1,), ((0,), (0,)))
        active = gelu_exact(pre_act).astype(jnp.bfloat16)
        back_t = dot(down_hidden, active, (1,), (1,), ((0,), (0,))).astype(jnp.bfloat16)
        act_grad = dot(down_hidden, grad_t, (2,), (1,), ((0,), (0,)))
        pre_grad = (act_grad * gelu_slope(pre_act)).astype(jnp.bfloat16)
        tile_grad_t = dot(up_hidden, pre_grad, (2,), (1,), ((0,), (0,))).astype(jnp.bfloat16)
        g_dh = dot(active, grad_t, (2,), (2,), ((0,), (0,)))
        g_uh = dot(hidden_t, pre_grad, (2,), (2,), ((0,), (0,)))
        dhg = g_dh if dhg is None else dhg + g_dh
        uhg = g_uh if uhg is None else uhg + g_uh

        send2 = jnp.stack([back_t, tile_grad_t], axis=0).reshape(2, local_blocks, nb, expand, rows)
        send2 = send2.transpose(2, 0, 1, 3, 4)
        recv2 = lax.all_to_all(send2, "block", 0, 0, tiled=True)
        rows_t = recv2[:, 0].reshape(nb * chunk, rows)
        rows_grad_t = recv2[:, 1].reshape(nb * chunk, rows)

        outs.append(dot(rows_t, dw, (0,), (0,)).astype(jnp.bfloat16))
        tgrads.append(dot(rows_grad_t, uw, (0,), (1,)).astype(jnp.bfloat16))
        g_dw = dot(rows_t, c, (1,), (0,))
        g_uw = dot(x, rows_grad_t, (0,), (1,))
        dwg = g_dw if dwg is None else dwg + g_dw
        uwg = g_uw if uwg is None else uwg + g_uw

    dhg = dp_sum(dhg)
    uhg = dp_sum(uhg)
    dwg = dp_sum(dwg)
    uwg = dp_sum(uwg)
    return (
        jnp.concatenate(outs, axis=0),
        jnp.concatenate(tgrads, axis=0),
        (uwg * grad_scale)[None],
        uhg * grad_scale,
        dhg * grad_scale,
        (dwg * grad_scale)[None],
    )


def solution(mesh):
    in_specs = (
        P("dp", "block"),
        P("dp", "block"),
        P("block", None, None),
        P("block", None, None),
        P("block", None, None),
        P("block", None, None),
    )
    out_specs = in_specs
    return jax.shard_map(shards, mesh=mesh, in_specs=in_specs, out_specs=out_specs, check_vma=False)
```

time: 348 us -> 321 us (0.922); the launches traced: 348 us -> 316 us
  blocking collectives: 109 us -> 0 us
  starting transfers between devices: 9.5 us -> 66.3 us
  local copies, waits for them, and re-layouts: 29.8 us -> 56.5 us
  other arithmetic: 9.94 us -> 28.9 us
  waiting for transfers between devices: 144 us -> 126 us
  between operations: 14.2 us -> 1.59 us
  matrix products: 31 us -> 36.7 us
    all_to_all x1 -> x0, blocking collectives: 109 us -> none  [shards(): recv = lax.all_to_all(send, 'block', 0, 0, tiled=True)]
    all_to_all x0 -> x2, waiting for transfers between devices: none -> 79.7 us  [shards(): recv = lax.all_to_all(send, 'block', 0, 0, tiled=True)]
    all_to_all x1 -> x2, waiting for transfers between devices: 86.2 us -> 26.3 us  [shards(): recv2 = lax.all_to_all(send2, 'block', 0, 0, tiled=True)]
    psum x1 -> x0, waiting for transfers between devices: 58.1 us -> none  [shards(): uwg = lax.psum(up_width_grad.astype(jnp.bfloat16), 'dp').astype(jnp.float32)]
    all_to_all x0 -> x2, starting transfers between devices: none -> 24.6 us  [shards(): recv = lax.all_to_all(send, 'block', 0, 0, tiled=True)]
    ppermute x0 -> x16, waiting for transfers between devices: none -> 20.4 us  [the longest x4 12.8 us: dp_sum(): got = lax.ppermute(pick(half, 1 - row).astype(jnp.bfloat16), 'dp', row_swap)]
    ppermute x0 -> x16, starting transfers between devices: none -> 19.4 us  [the longest x4 6.62 us: dp_sum(): got = lax.ppermute(pick(parts, 1 - core), 'dp', core_swap)]
    all_to_all x1 -> x2, starting transfers between devices: 9.46 us -> 22.2 us  [shards(): recv2 = lax.all_to_all(send2, 'block', 0, 0, tiled=True)]
  transfers between devices with their start and end apart: 2 -> 20, of which waited for: 2 -> 10; matrix products, arithmetic and copies ran while one was open for 3% -> 28% of each run, Pallas kernels for 0% -> 0%
where the time goes in v2:
time: 321 us; the launch traced here: 316 us
  waiting for transfers between devices  126 us (39%)
  starting transfers between devices  66.3 us (21%)
  local copies, waits for them, and re-layouts  56.5 us (18%)
  matrix products  36.7 us (11%)
  other arithmetic  28.9 us (9%)
    all_to_all x2, waiting for transfers between devices, shards(): recv = lax.all_to_all(send, 'block', 0, 0, tiled=True)  79.7 us
    dot_general x24, matrix products, dot(): lax.dot_general(left, right, ((left_dims, right_dims), batch), preferred_...  36.7 us
    all_to_all x2, waiting for transfers between devices, shards(): recv2 = lax.all_to_all(send2, 'block', 0, 0, tiled=True)  26.3 us
    all_to_all x2, starting transfers between devices, shards(): recv = lax.all_to_all(send, 'block', 0, 0, tiled=True)  24.6 us
    all_to_all x2, starting transfers between devices, shards(): recv2 = lax.all_to_all(send2, 'block', 0, 0, tiled=True)  22.2 us
    ppermute x4, waiting for transfers between devices, dp_sum(): got = lax.ppermute(pick(half, 1 - row).astype(jnp.bfloat16), 'dp', row_swap)  12.8 us
    select_n x8, other arithmetic, dp_sum(): jnp.where(row == 0, jnp.stack([quarter, got]), jnp.stack([got, quarter]))  9.39 us
    ppermute x4, waiting for transfers between devices, dp_sum(): got = lax.ppermute(quarter, 'dp', row_swap)  7.54 us
  transfers between devices with their start and end apart: 20, of which 10 were waited for; matrix products, arithmetic and copies ran while one was open for 28% of the time, Pallas kernels for 0%

profile of v2, /device:TPU:1, one launch (start us, length us, event | category | flops | bytes accessed | tf_op | source)
XLA Modules:
  0.0 316.2 jit_solution(17283289771490873347)
XLA Ops:
  5.3 15.2 %all-to-all-start = ((bf16[64,2,16,512]{3,2,1,0:T(8,128)(2,1)}), bf16[64,2,16,512]{3,2,1,0:T(8,128)(2,1)S(1)}, u32[]{:S(2)}, u32[]{:S(2)}) async-start(bf16[64,2,16,512]{3,2,1,0:T(8,128)(2,1)} %pad_maximum_fusion), calls=%async_computation | async-start | bytes 4194304 | tf_op jit(solution)/shard_map/all_to_all | solution.py:71
  25.1 44.5 %all-to-all-done = bf16[64,2,16,512]{3,2,1,0:T(8,128)(2,1)S(1)} async-done(((bf16[64,2,16,512]{3,2,1,0:T(8,128)(2,1)}), bf16[64,2,16,512]{3,2,1,0:T(8,128)(2,1)S(1)}, u32[]{:S(2)}, u32[]{:S(2)}) %all-to-all-start) | async-done | bytes 2097184 | tf_op jit(solution)/shard_map/all_to_all | solution.py:71
  70.9 9.4 %all-to-all-start.2 = ((bf16[64,2,16,512]{3,2,1,0:T(8,128)(2,1)}), bf16[64,2,16,512]{3,2,1,0:T(8,128)(2,1)S(1)}, u32[]{:S(2)}, u32[]{:S(2)}) async-start(bf16[64,2,16,512]{3,2,1,0:T(8,128)(2,1)} %pad_maximum_fusion.2), calls=%async_computation.2 | async-start | bytes 4194304 | tf_op jit(solution)/shard_map/all_to_all | solution.py:71
  80.3 2.8 copy.86
  93.6 35.2 %all-to-all-done.2 = bf16[64,2,16,512]{3,2,1,0:T(8,128)(2,1)S(1)} async-done(((bf16[64,2,16,512]{3,2,1,0:T(8,128)(2,1)}), bf16[64,2,16,512]{3,2,1,0:T(8,128)(2,1)S(1)}, u32[]{:S(2)}, u32[]{:S(2)}) %all-to-all-start.2) | async-done | bytes 2097184 | tf_op jit(solution)/shard_map/all_to_all | solution.py:71
  130.1 1.8 copy.103
  133.8 2.2 stack.162
  136.0 3.3 %copy_bitcast_fusion.1 = bf16[64,2,4,4,512]{4,3,2,1,0:T(4,128)(2,1)} fusion(bf16[1,4,64,4,512]{4,3,2,1,0:T(4,128)(2,1)} %stack.162, bf16[1,4,64,4,512]{4,3,2,1,0:T(4,128)(2,1)S(1)} %copy-done.15), kind=kLoop, calls=%fused_computation.25 | loop fusion | flops 1048576 | bytes 4194304 | tf_op jit(solution)/shard_map/transpose | solution.py:88
  139.4 10.1 %all-to-all-start.1 = ((bf16[64,2,4,4,512]{4,3,2,1,0:T(4,128)(2,1)}), bf16[64,2,4,4,512]{4,3,2,1,0:T(4,128)(2,1)}, u32[]{:S(2)}, u32[]{:S(2)}) async-start(bf16[64,2,4,4,512]{4,3,2,1,0:T(4,128)(2,1)} %copy_bitcast_fusion.1), calls=%async_computation.1 | async-start | bytes 4194304 | tf_op jit(solution)/shard_map/all_to_all | solution.py:89
  155.1 2.1 fusion.25
  159.3 1.8 dynamic-slice_bitcast_fusion.2
  167.6 3.3 %copy_bitcast_fusion = bf16[64,2,4,4,512]{4,3,2,1,0:T(4,128)(2,1)} fusion(bf16[1,4,64,4,512]{4,3,2,1,0:T(4,128)(2,1)S(1)} %copy-done.13, bf16[1,4,64,4,512]{4,3,2,1,0:T(4,128)(2,1)} %stack.165), kind=kLoop, calls=%fused_computation.18 | loop fusion | flops 1048576 | bytes 4194304 | tf_op jit(solution)/shard_map/transpose | solution.py:88
  176.1 5.8 %collective-permute-done.5 = bf16[65536]{0:T(1024)(128)(2,1)S(1)} collective-permute-done((bf16[65536]{0:T(1024)(128)(2,1)S(1)}, bf16[65536]{0:T(1024)(128)(2,1)S(1)}, u32[]{:S(2)}, u32[]{:S(2)}) %collective-permute-start.5) | collective-permute-done | bytes 131104 | tf_op jit(solution)/shard_map/ppermute | solution.py:41
  183.0 2.7 collective-permute-done.9
  187.8 3.0 collective-permute-done.6
  193.2 3.2 %collective-permute-done.10 = bf16[65536]{0:T(1024)(128)(2,1)S(1)} collective-permute-done((bf16[65536]{0:T(1024)(128)(2,1)S(1)}, bf16[65536]{0:T(1024)(128)(2,1)S(1)}, u32[]{:S(2)}, u32[]{:S(2)}) %collective-permute-start.10) | collective-permute-done | bytes 131104 | tf_op jit(solution)/shard_map/ppermute | solution.py:43
  201.1 1.8 convert_multiply_fusion.1
  202.9 12.1 %all-to-all-start.3 = ((bf16[64,2,4,4,512]{4,3,2,1,0:T(4,128)(2,1)}), bf16[64,2,4,4,512]{4,3,2,1,0:T(4,128)(2,1)S(1)}, u32[]{:S(2)}, u32[]{:S(2)}) async-start(bf16[64,2,4,4,512]{4,3,2,1,0:T(4,128)(2,1)} %copy_bitcast_fusion), calls=%async_computation.3 | async-start | bytes 4194304 | tf_op jit(solution)/shard_map/all_to_all | solution.py:89
  216.7 2.7 mul.104
  219.5 2.7 mul.102
  222.2 3.9 %fusion.59 = (bf16[64,1,4,4,512]{4,3,2,1,0:T(4,128)(2,1)}, bf16[64,1,4,4,512]{4,3,2,1,0:T(4,128)(2,1)}) fusion(bf16[64,2,4,4,512]{4,3,2,1,0:T(4,128)(2,1)} %all-to-all-done.1), kind=kLoop, calls=%fused_computation.129 | loop fusion | bytes 4194304 | tf_op jit(solution)/shard_map/slice | solution.py:91
  226.1 2.2 reshape_squeeze.14
  228.3 2.2 reshape_squeeze.12
  230.5 2.5 convolution_convert_fusion.9
  233.1 2.5 convolution_convert_fusion.11
  238.4 26.3 %all-to-all-done.3 = bf16[64,2,4,4,512]{4,3,2,1,0:T(4,128)(2,1)S(1)} async-done(((bf16[64,2,4,4,512]{4,3,2,1,0:T(4,128)(2,1)}), bf16[64,2,4,4,512]{4,3,2,1,0:T(4,128)(2,1)S(1)}, u32[]{:S(2)}, u32[]{:S(2)}) %all-to-all-start.3) | async-done | bytes 2097184 | tf_op jit(solution)/shard_map/all_to_all | solution.py:89
  264.8 2.5 fusion.60
  273.6 2.2 reshape.384
  277.0 4.7 %collective-permute-start = (bf16[2,65536]{1,0:T(2,128)(2,1)S(1)}, bf16[2,65536]{1,0:T(2,128)(2,1)}, u32[]{:S(2)}, u32[]{:S(2)}) collective-permute-start(bf16[2,65536]{1,0:T(2,128)(2,1)S(1)} %dynamic-slice_bitcast_fusion.3), channel_id=1, source_target_pairs={{0,64},{64,0},{128,192},{192,128},{1,65},{65,1},{129,193},{193,129... | collective-permute-start | bytes 786440 | tf_op jit(solution)/shard_map/ppermute | solution.py:39
  282.8 2.5 fusion.27
  296.4 2.5 collective-permute-done.13
  302.3 3.6 %collective-permute-start.3 = (bf16[2,65536]{1,0:T(2,128)(2,1)S(1)}, bf16[2,65536]{1,0:T(2,128)(2,1)S(1)}, u32[]{:S(2)}, u32[]{:S(2)}) collective-permute-start(bf16[2,65536]{1,0:T(2,128)(2,1)S(1)} %broadcast_select_fusion.7), channel_id=1, source_target_pairs={{0,64},{64,0},{128,192},{192,128},{1,65},{65,1},{129,193},{193,129... | collective-permute-start | bytes 786440 | tf_op jit(solution)/shard_map/ppermute | solution.py:45
  (179 shorter events, 91.1 us)
Async XLA Ops:
  0.6 84.3 %copy-start = (bf16[4,256,256]{2,1,0:T(8,128)(2,1)S(1)}, bf16[4,256,256]{2,1,0:T(8,128)(2,1)}, u32[]{:S(2)}) copy-start(bf16[4,256,256]{2,1,0:T(8,128)(2,1)} %param.9) | copy-start | bytes 1572868
  5.3 15.3 %copy-start.18 = (bf16[1,256,1024]{2,1,0:T(8,128)(2,1)S(1)}, bf16[1,256,1024]{2,1,0:T(8,128)(2,1)}, u32[]{:S(2)}) copy-start(bf16[1,256,1024]{2,1,0:T(8,128)(2,1)} %param.8) | copy-start | bytes 1572868
  5.3 64.2 %all-to-all-start = ((bf16[64,2,16,512]{3,2,1,0:T(8,128)(2,1)}), bf16[64,2,16,512]{3,2,1,0:T(8,128)(2,1)S(1)}, u32[]{:S(2)}, u32[]{:S(2)}) async-start(bf16[64,2,16,512]{3,2,1,0:T(8,128)(2,1)} %pad_maximum_fusion), calls=%async_computation | async-start | bytes 4194304 | tf_op jit(solution)/shard_map/all_to_all | solution.py:71
  70.9 57.8 %all-to-all-start.2 = ((bf16[64,2,16,512]{3,2,1,0:T(8,128)(2,1)}), bf16[64,2,16,512]{3,2,1,0:T(8,128)(2,1)S(1)}, u32[]{:S(2)}, u32[]{:S(2)}) async-start(bf16[64,2,16,512]{3,2,1,0:T(8,128)(2,1)} %pad_maximum_fusion.2), calls=%async_computation.2 | async-start | bytes 4194304 | tf_op jit(solution)/shard_map/all_to_all | solution.py:71
  139.4 63.5 %all-to-all-start.1 = ((bf16[64,2,4,4,512]{4,3,2,1,0:T(4,128)(2,1)}), bf16[64,2,4,4,512]{4,3,2,1,0:T(4,128)(2,1)}, u32[]{:S(2)}, u32[]{:S(2)}) async-start(bf16[64,2,4,4,512]{4,3,2,1,0:T(4,128)(2,1)} %copy_bitcast_fusion.1), calls=%async_computation.1 | async-start | bytes 4194304 | tf_op jit(solution)/shard_map/all_to_all | solution.py:89
  158.1 6.3 %copy-start.6 = (bf16[4,256,512]{2,1,0:T(8,128)(2,1)S(1)}, bf16[4,256,512]{2,1,0:T(8,128)(2,1)}, u32[]{:S(2)}) copy-start(bf16[4,256,512]{2,1,0:T(8,128)(2,1)} %fusion.23) | copy-start | bytes 3145732
  161.2 9.7 %collective-permute-start.4 = (bf16[2,65536]{1,0:T(2,128)(2,1)}, bf16[2,65536]{1,0:T(2,128)(2,1)}, u32[]{:S(2)}, u32[]{:S(2)}) collective-permute-start(bf16[2,65536]{1,0:T(2,128)(2,1)} %dynamic-slice_bitcast_fusion.2), channel_id=1, source_target_pairs={{0,64},{64,0},{128,192},{192,128},{1,65},{65,1},{129,193},{193,129... | collective-permute-start | bytes 786440 | tf_op jit(solution)/shard_map/ppermute | solution.py:39
  167.1 6.5 %copy-start.27 = (bf16[2,2,65536]{2,1,0:T(2,128)(2,1)S(1)}, bf16[2,2,65536]{2,1,0:T(2,128)(2,1)}, u32[]{:S(2)}) copy-start(bf16[2,2,65536]{2,1,0:T(2,128)(2,1)} %reshape.386) | copy-start | bytes 1572868
  167.1 6.5 %collective-permute-start.8 = (bf16[2,65536]{1,0:T(2,128)(2,1)S(1)}, bf16[2,65536]{1,0:T(2,128)(2,1)S(1)}, u32[]{:S(2)}, u32[]{:S(2)}) collective-permute-start(bf16[2,65536]{1,0:T(2,128)(2,1)S(1)} %dynamic-slice_bitcast_fusion.1), channel_id=1, source_target_pairs={{0,64},{64,0},{128,192},{192,128},{1,65},{65,1},{129,193},{193,129... | collective-permute-start | bytes 786440 | tf_op jit(solution)/shard_map/ppermute | solution.py:39
  173.1 8.7 %collective-permute-start.5 = (bf16[65536]{0:T(1024)(128)(2,1)S(1)}, bf16[65536]{0:T(1024)(128)(2,1)S(1)}, u32[]{:S(2)}, u32[]{:S(2)}) collective-permute-start(bf16[65536]{0:T(1024)(128)(2,1)S(1)} %convert_reduce_fusion.2), channel_id=1, source_target_pairs={{0,128},{64,192},{128,0},{192,64},{1,129},{65,193},{129,1},{193,65... | collective-permute-start | bytes 393224 | tf_op jit(solution)/shard_map/ppermute | solution.py:41
  174.9 10.8 %collective-permute-start.9 = (bf16[65536]{0:T(1024)(128)(2,1)S(1)}, bf16[65536]{0:T(1024)(128)(2,1)S(1)}, u32[]{:S(2)}, u32[]{:S(2)}) collective-permute-start(bf16[65536]{0:T(1024)(128)(2,1)S(1)} %convert_reduce_fusion.1), channel_id=1, source_target_pairs={{0,128},{64,192},{128,0},{192,64},{1,129},{65,193},{129,1},{193,65... | collective-permute-start | bytes 393224 | tf_op jit(solution)/shard_map/ppermute | solution.py:41
  181.9 8.9 %collective-permute-start.6 = (bf16[65536]{0:T(1024)(128)(2,1)S(1)}, bf16[65536]{0:T(1024)(128)(2,1)S(1)}, u32[]{:S(2)}, u32[]{:S(2)}) collective-permute-start(bf16[65536]{0:T(1024)(128)(2,1)S(1)} %add_convert_fusion.2), channel_id=1, source_target_pairs={{0,128},{64,192},{128,0},{192,64},{1,129},{65,193},{129,1},{193,65... | collective-permute-start | bytes 393224 | tf_op jit(solution)/shard_map/ppermute | solution.py:43
  186.0 10.4 %collective-permute-start.10 = (bf16[65536]{0:T(1024)(128)(2,1)S(1)}, bf16[65536]{0:T(1024)(128)(2,1)S(1)}, u32[]{:S(2)}, u32[]{:S(2)}) collective-permute-start(bf16[65536]{0:T(1024)(128)(2,1)S(1)} %add_convert_fusion.1), channel_id=1, source_target_pairs={{0,128},{64,192},{128,0},{192,64},{1,129},{65,193},{129,1},{193,65... | collective-permute-start | bytes 393224 | tf_op jit(solution)/shard_map/ppermute | solution.py:43
  192.1 22.9 %collective-permute-start.7 = (bf16[2,65536]{1,0:T(2,128)(2,1)S(1)}, bf16[2,65536]{1,0:T(2,128)(2,1)S(1)}, u32[]{:S(2)}, u32[]{:S(2)}) collective-permute-start(bf16[2,65536]{1,0:T(2,128)(2,1)S(1)} %broadcast_select_fusion.6), channel_id=1, source_target_pairs={{0,64},{64,0},{128,192},{192,128},{1,65},{65,1},{129,193},{193,129... | collective-permute-start | bytes 786440 | tf_op jit(solution)/shard_map/ppermute | solution.py:45
  197.7 3.4 %collective-permute-start.11 = (bf16[2,65536]{1,0:T(2,128)(2,1)S(1)}, bf16[2,65536]{1,0:T(2,128)(2,1)S(1)}, u32[]{:S(2)}, u32[]{:S(2)}) collective-permute-start(bf16[2,65536]{1,0:T(2,128)(2,1)S(1)} %broadcast_select_fusion.5), channel_id=1, source_target_pairs={{0,64},{64,0},{128,192},{192,128},{1,65},{65,1},{129,193},{193,129... | collective-permute-start | bytes 786440 | tf_op jit(solution)/shard_map/ppermute | solution.py:45
  202.9 61.9 %all-to-all-start.3 = ((bf16[64,2,4,4,512]{4,3,2,1,0:T(4,128)(2,1)}), bf16[64,2,4,4,512]{4,3,2,1,0:T(4,128)(2,1)S(1)}, u32[]{:S(2)}, u32[]{:S(2)}) async-start(bf16[64,2,4,4,512]{4,3,2,1,0:T(4,128)(2,1)} %copy_bitcast_fusion), calls=%async_computation.3 | async-start | bytes 4194304 | tf_op jit(solution)/shard_map/all_to_all | solution.py:89
  226.1 4.4 %copy-start.19 = (bf16[1,256,1024]{2,1,0:T(8,128)(2,1)S(1)}, bf16[1,256,1024]{2,1,0:T(8,128)(2,1)}, u32[]{:S(2)}) copy-start(bf16[1,256,1024]{2,1,0:T(8,128)(2,1)} %param.8) | copy-start | bytes 1572868
  228.3 4.8 %copy-start.22 = (bf16[1,1024,256]{2,1,0:T(8,128)(2,1)S(1)}, bf16[1,1024,256]{2,1,0:T(8,128)(2,1)}, u32[]{:S(2)}) copy-start(bf16[1,1024,256]{2,1,0:T(8,128)(2,1)} %param.11) | copy-start | bytes 1572868
  230.5 5.1 %copy-start.7 = (bf16[1024,512]{1,0:T(8,128)(2,1)S(1)}, bf16[1024,512]{1,0:T(8,128)(2,1)}, u32[]{:S(2)}) copy-start(bf16[1024,512]{1,0:T(8,128)(2,1)} %reshape_squeeze.14) | copy-start | bytes 3145732
  230.5 5.1 %copy-start.23 = (bf16[1024,256]{1,0:T(8,128)(2,1)S(1)}, bf16[1024,256]{1,0:T(8,128)(2,1)}, u32[]{:S(2)}) copy-start(bf16[1024,256]{1,0:T(8,128)(2,1)} %param.6) | copy-start | bytes 1572868
  270.9 10.8 %copy-start.11 = (bf16[64,1,4,4,512]{4,3,2,1,0:T(4,128)(2,1)S(1)}, bf16[64,1,4,4,512]{4,3,2,1,0:T(4,128)(2,1)}, u32[]{:S(2)}) copy-start(bf16[64,1,4,4,512]{4,3,2,1,0:T(4,128)(2,1)} %get-tuple-element.9) | copy-start | bytes 3145732
  273.6 9.1 %copy-start.10 = (f32[1024,256]{1,0:T(8,128)S(1)}, f32[1024,256]{1,0:T(8,128)}, u32[]{:S(2)}) copy-start(f32[1024,256]{1,0:T(8,128)} %fusion.53) | copy-start | bytes 3145732
  273.6 9.1 %copy-start.26 = (bf16[1024,256]{1,0:T(8,128)(2,1)S(1)}, bf16[1024,256]{1,0:T(8,128)(2,1)}, u32[]{:S(2)}) copy-start(bf16[1024,256]{1,0:T(8,128)(2,1)} %param.7) | copy-start | bytes 1572868
  277.0 12.1 %collective-permute-start = (bf16[2,65536]{1,0:T(2,128)(2,1)S(1)}, bf16[2,65536]{1,0:T(2,128)(2,1)}, u32[]{:S(2)}, u32[]{:S(2)}) collective-permute-start(bf16[2,65536]{1,0:T(2,128)(2,1)S(1)} %dynamic-slice_bitcast_fusion.3), channel_id=1, source_target_pairs={{0,64},{64,0},{128,192},{192,128},{1,65},{65,1},{129,193},{193,129... | collective-permute-start | bytes 786440 | tf_op jit(solution)/shard_map/ppermute | solution.py:39
  287.2 4.5 %collective-permute-start.12 = (bf16[2,65536]{1,0:T(2,128)(2,1)S(1)}, bf16[2,65536]{1,0:T(2,128)(2,1)S(1)}, u32[]{:S(2)}, u32[]{:S(2)}) collective-permute-start(bf16[2,65536]{1,0:T(2,128)(2,1)S(1)} %dynamic-slice_bitcast_fusion), channel_id=1, source_target_pairs={{0,64},{64,0},{128,192},{192,128},{1,65},{65,1},{129,193},{193,129... | collective-permute-start | bytes 786440 | tf_op jit(solution)/shard_map/ppermute | solution.py:39
  291.3 4.9 %collective-permute-start.1 = (bf16[65536]{0:T(1024)(128)(2,1)S(1)}, bf16[65536]{0:T(1024)(128)(2,1)S(1)}, u32[]{:S(2)}, u32[]{:S(2)}) collective-permute-start(bf16[65536]{0:T(1024)(128)(2,1)S(1)} %convert_reduce_fusion.3), channel_id=1, source_target_pairs={{0,128},{64,192},{128,0},{192,64},{1,129},{65,193},{129,1},{193,65... | collective-permute-start | bytes 393224 | tf_op jit(solution)/shard_map/ppermute | solution.py:41
  293.0 5.9 %collective-permute-start.13 = (bf16[65536]{0:T(1024)(128)(2,1)S(1)}, bf16[65536]{0:T(1024)(128)(2,1)S(1)}, u32[]{:S(2)}, u32[]{:S(2)}) collective-permute-start(bf16[65536]{0:T(1024)(128)(2,1)S(1)} %convert_reduce_fusion), channel_id=1, source_target_pairs={{0,128},{64,192},{128,0},{192,64},{1,129},{65,193},{129,1},{193,65... | collective-permute-start | bytes 393224 | tf_op jit(solution)/shard_map/ppermute | solution.py:41
  296.2 4.8 %collective-permute-start.2 = (bf16[65536]{0:T(1024)(128)(2,1)S(1)}, bf16[65536]{0:T(1024)(128)(2,1)S(1)}, u32[]{:S(2)}, u32[]{:S(2)}) collective-permute-start(bf16[65536]{0:T(1024)(128)(2,1)S(1)} %add_convert_fusion.3), channel_id=1, source_target_pairs={{0,128},{64,192},{128,0},{192,64},{1,129},{65,193},{129,1},{193,65... | collective-permute-start | bytes 393224 | tf_op jit(solution)/shard_map/ppermute | solution.py:43
  299.3 6.6 %collective-permute-start.14 = (bf16[65536]{0:T(1024)(128)(2,1)S(1)}, bf16[65536]{0:T(1024)(128)(2,1)S(1)}, u32[]{:S(2)}, u32[]{:S(2)}) collective-permute-start(bf16[65536]{0:T(1024)(128)(2,1)S(1)} %add_convert_fusion), channel_id=1, source_target_pairs={{0,128},{64,192},{128,0},{192,64},{1,129},{65,193},{129,1},{193,65... | collective-permute-start | bytes 393224 | tf_op jit(solution)/shard_map/ppermute | solution.py:43
  302.3 8.6 %collective-permute-start.3 = (bf16[2,65536]{1,0:T(2,128)(2,1)S(1)}, bf16[2,65536]{1,0:T(2,128)(2,1)S(1)}, u32[]{:S(2)}, u32[]{:S(2)}) collective-permute-start(bf16[2,65536]{1,0:T(2,128)(2,1)S(1)} %broadcast_select_fusion.7), channel_id=1, source_target_pairs={{0,64},{64,0},{128,192},{192,128},{1,65},{65,1},{129,193},{193,129... | collective-permute-start | bytes 786440 | tf_op jit(solution)/shard_map/ppermute | solution.py:45
  307.2 6.2 %collective-permute-start.15 = (bf16[2,65536]{1,0:T(2,128)(2,1)S(1)}, bf16[2,65536]{1,0:T(2,128)(2,1)S(1)}, u32[]{:S(2)}, u32[]{:S(2)}) collective-permute-start(bf16[2,65536]{1,0:T(2,128)(2,1)S(1)} %broadcast_select_fusion.4), channel_id=1, source_target_pairs={{0,64},{64,0},{128,192},{192,128},{1,65},{65,1},{129,193},{193,129... | collective-permute-start | bytes 786440 | tf_op jit(solution)/shard_map/ppermute | solution.py:45
  311.7 4.3 %copy-start.1 = (bf16[4,256,256]{2,1,0:T(8,128)(2,1)S(1)}, bf16[4,256,256]{2,1,0:T(8,128)(2,1)}, u32[]{:S(2)}) copy-start(bf16[4,256,256]{2,1,0:T(8,128)(2,1)} %param.9) | copy-start | bytes 1572868
  (21 other events, 46.0 us)

commit v3 on v2

v3 whole, which is shorter than its diff:
```python
import math

import jax
import jax.numpy as jnp
from jax import lax
from jax.sharding import PartitionSpec as P

GROUPS = 2


def gelu_exact(value):
    return 0.5 * value * (1.0 + jax.scipy.special.erf(value / math.sqrt(2.0)))


def gelu_slope(value):
    return 0.5 * (1.0 + jax.scipy.special.erf(value / math.sqrt(2.0))) + value * jnp.exp(
        -0.5 * value * value
    ) / math.sqrt(2.0 * math.pi)


def dot(left, right, left_dims, right_dims, batch=((), ())):
    return lax.dot_general(
        left, right, ((left_dims, right_dims), batch), preferred_element_type=jnp.float32
    )


def pick(pair, index):
    return lax.dynamic_index_in_dim(pair, index, axis=0, keepdims=False)


def dp_sum(flat):
    size = lax.axis_size("dp")
    index = lax.axis_index("dp")
    core = index % 2
    row = index // 2
    core_swap = [(i, i ^ 1) for i in range(size)]
    row_swap = [(i, i ^ 2) for i in range(size)]
    parts = flat.reshape(2, 2, -1)
    got = lax.ppermute(pick(parts, 1 - core), "dp", core_swap)
    half = pick(parts, core).astype(jnp.float32) + got.astype(jnp.float32)
    got = lax.ppermute(pick(half, 1 - row).astype(jnp.bfloat16), "dp", row_swap)
    quarter = (pick(half, row) + got.astype(jnp.float32)).astype(jnp.bfloat16)
    got = lax.ppermute(quarter, "dp", row_swap)
    half = jnp.where(row == 0, jnp.stack([quarter, got]), jnp.stack([got, quarter]))
    got = lax.ppermute(half, "dp", core_swap)
    full = jnp.where(core == 0, jnp.stack([half, got]), jnp.stack([got, half]))
    return full.reshape(-1)


def summed(scale, *grads):
    flat = jnp.concatenate([(g * scale).astype(jnp.bfloat16).reshape(-1) for g in grads])
    total = dp_sum(flat).astype(jnp.float32)
    out, start = [], 0
    for g in grads:
        out.append(total[start:start + g.size].reshape(g.shape))
        start += g.size
    return out


def shards(tokens, cotangent, up_width, up_hidden, down_hidden, down_width):
    rows, block_size = tokens.shape
    nb = lax.axis_size("block")
    local_blocks, hidden_size, _ = up_hidden.shape
    expand = up_width.shape[2] // block_size
    per = local_blocks // GROUPS
    grad_scale = 1.0 / math.sqrt(rows * lax.axis_size("dp"))
    uw = up_width[0].reshape(block_size, nb, GROUPS, per * expand)
    dw = down_width[0].reshape(nb, GROUPS, per * expand, block_size)

    out_acc = tg_acc = None
    dhg, uhg, dwg, uwg = [], [], [], []
    for grp in range(GROUPS):
        uw_g = uw[:, :, grp].reshape(block_size, nb * per * expand)
        dw_g = dw[:, grp].reshape(nb * per * expand, block_size)
        expanded_t = dot(uw_g, tokens, (0,), (1,)).astype(jnp.bfloat16)
        out_grad_t = dot(dw_g, cotangent, (1,), (1,)).astype(jnp.bfloat16)
        send = jnp.stack(
            [expanded_t.reshape(nb, per * expand, rows), out_grad_t.reshape(nb, per * expand, rows)],
            axis=1,
        )
        recv = lax.all_to_all(send, "block", 0, 0, tiled=True)
        recv = recv.reshape(nb, 2, per, expand, rows)
        hidden_t = recv[:, 0].transpose(1, 0, 2, 3).reshape(per, nb * expand, rows)
        grad_t = recv[:, 1].transpose(1, 0, 2, 3).reshape(per, nb * expand, rows)

        uh = up_hidden[grp * per:(grp + 1) * per]
        dh = down_hidden[grp * per:(grp + 1) * per]
        pre_act = dot(uh, hidden_t, (1,), (1,), ((0,), (0,)))
        active = gelu_exact(pre_act).astype(jnp.bfloat16)
        back_t = dot(dh, active, (1,), (1,), ((0,), (0,))).astype(jnp.bfloat16)
        act_grad = dot(dh, grad_t, (2,), (1,), ((0,), (0,)))
        pre_grad = (act_grad * gelu_slope(pre_act)).astype(jnp.bfloat16)
        tile_grad_t = dot(uh, pre_grad, (2,), (1,), ((0,), (0,))).astype(jnp.bfloat16)
        g_dh = dot(active, grad_t, (2,), (2,), ((0,), (0,)))
        g_uh = dot(hidden_t, pre_grad, (2,), (2,), ((0,), (0,)))
        s_dh, s_uh = summed(grad_scale, g_dh, g_uh)
        dhg.append(s_dh)
        uhg.append(s_uh)

        send2 = jnp.stack([back_t, tile_grad_t], axis=0).reshape(2, per, nb, expand, rows)
        send2 = send2.transpose(2, 0, 1, 3, 4).reshape(nb, 2, per * expand, rows)
        recv2 = lax.all_to_all(send2, "block", 0, 0, tiled=True)
        rows_t = recv2[:, 0].reshape(nb * per * expand, rows)
        rows_grad_t = recv2[:, 1].reshape(nb * per * expand, rows)

        part_out = dot(rows_t, dw_g, (0,), (0,))
        part_tg = dot(rows_grad_t, uw_g, (0,), (1,))
        out_acc = part_out if out_acc is None else out_acc + part_out
        tg_acc = part_tg if tg_acc is None else tg_acc + part_tg
        g_dw = dot(rows_t, cotangent, (1,), (0,))
        g_uw = dot(tokens, rows_grad_t, (0,), (1,))
        s_dw, s_uw = summed(grad_scale, g_dw, g_uw)
        dwg.append(s_dw.reshape(nb, 1, per * expand, block_size))
        uwg.append(s_uw.reshape(block_size, nb, 1, per * expand))

    return (
        out_acc.astype(jnp.bfloat16),
        tg_acc.astype(jnp.bfloat16),
        jnp.concatenate(uwg, axis=2).reshape(1, block_size, -1),
        jnp.concatenate(uhg, axis=0),
        jnp.concatenate(dhg, axis=0),
        jnp.concatenate(dwg, axis=1).reshape(1, -1, block_size),
    )


def solution(mesh):
    in_specs = (
        P("dp", "block"),
        P("dp", "block"),
        P("block", None, None),
        P("block", None, None),
        P("block", None, None),
        P("block", None, None),
    )
    out_specs = in_specs
    return jax.shard_map(shards, mesh=mesh, in_specs=in_specs, out_specs=out_specs, check_vma=False)
```

time: 321 us -> 354 us (1.10)
  local copies, waits for them, and re-layouts: 56.5 us -> 84.9 us
  waiting for transfers between devices: 126 us -> 136 us
  matrix products: 36.7 us -> 32.7 us
    slice x2 -> x16, local copies, waits for them, and re-layouts: 6.4 us -> 29.3 us  [the longest x12 24.8 us: summed(): out.append(total[start:start + g.size].reshape(g.shape))]
    all_to_all x2, waiting for transfers between devices: 26.3 us -> 41 us  [shards(): recv2 = lax.all_to_all(send2, 'block', 0, 0, tiled=True)]
    concatenate x0 -> x12, local copies, waits for them, and re-layouts: none -> 9.48 us  [summed(): jnp.concatenate([(g * scale).astype(jnp.bfloat16).reshape(-1) for g in gr...]
    mul x4 -> x0, local copies, waits for them, and re-layouts: 8.95 us -> none  [the longest x1 2.75 us: shards(): dhg * grad_scale]
    unnamed x66 -> x54, local copies, waits for them, and re-layouts: 3.54 us -> 10.6 us
    another operation x8 -> x4, local copies, waits for them, and re-layouts: 12.4 us -> 6.89 us  [shards(): jnp.stack([back_t, tile_grad_t], axis=0).reshape(2, per, nb, expand, rows)]
    mul x4 -> x0, other arithmetic: 5.1 us -> none  [the longest x1 1.76 us: shards(): dhg * grad_scale]
    transpose x6 -> x8, local copies, waits for them, and re-layouts: 4.6 us -> 8.71 us  [the longest x2 3.92 us: shards(): send2 = send2.transpose(2, 0, 1, 3, 4).reshape(nb, 2, per * expand, rows)]
  transfers between devices with their start and end apart: 20 -> 20, of which waited for: 10 -> 9; matrix products, arithmetic and copies ran while one was open for 28% -> 26% of each run, Pallas kernels for 0% -> 0%
where the time goes in v3:
time: 354 us; the launch traced here: 349 us
  waiting for transfers between devices  136 us (38%)
  local copies, waits for them, and re-layouts  84.9 us (24%)
  starting transfers between devices  66.2 us (19%)
  matrix products  32.7 us (9%)
  other arithmetic  27.5 us (8%)
    all_to_all x2, waiting for transfers between devices, shards(): recv = lax.all_to_all(send, 'block', 0, 0, tiled=True)  77.7 us
    all_to_all x2, waiting for transfers between devices, shards(): recv2 = lax.all_to_all(send2, 'block', 0, 0, tiled=True)  41 us
    dot_general x24, matrix products, dot(): lax.dot_general(left, right, ((left_dims, right_dims), batch), preferred_...  32.7 us
    slice x12, local copies, waits for them, and re-layouts, summed(): out.append(total[start:start + g.size].reshape(g.shape))  24.8 us
    all_to_all x2, starting transfers between devices, shards(): recv = lax.all_to_all(send, 'block', 0, 0, tiled=True)  24.5 us
    all_to_all x2, starting transfers between devices, shards(): recv2 = lax.all_to_all(send2, 'block', 0, 0, tiled=True)  21.9 us
    ppermute x4, waiting for transfers between devices, dp_sum(): got = lax.ppermute(pick(half, 1 - row).astype(jnp.bfloat16), 'dp', row_swap)  11.7 us
    unnamed x54, local copies, waits for them, and re-layouts  10.6 us
  transfers between devices with their start and end apart: 20, of which 9 were waited for; matrix products, arithmetic and copies ran while one was open for 26% of the time, Pallas kernels for 0%

profile of v3, /device:TPU:1, one launch (start us, length us, event | category | flops | bytes accessed | tf_op | source)
XLA Modules:
  0.0 348.7 jit_solution(15020624653704459767)
XLA Ops:
  4.5 15.1 %all-to-all-start = ((bf16[64,2,8,1024]{3,2,1,0:T(8,128)(2,1)}), bf16[64,2,8,1024]{3,2,1,0:T(8,128)(2,1)S(1)}, u32[]{:S(2)}, u32[]{:S(2)}) async-start(bf16[64,2,8,1024]{3,2,1,0:T(8,128)(2,1)} %pad_maximum_fusion), calls=%async_computation | async-start | bytes 4194304 | tf_op jit(solution)/shard_map/all_to_all | solution.py:81
  23.6 45.0 %all-to-all-done = bf16[64,2,8,1024]{3,2,1,0:T(8,128)(2,1)S(1)} async-done(((bf16[64,2,8,1024]{3,2,1,0:T(8,128)(2,1)}), bf16[64,2,8,1024]{3,2,1,0:T(8,128)(2,1)S(1)}, u32[]{:S(2)}, u32[]{:S(2)}) %all-to-all-start) | async-done | bytes 2097184 | tf_op jit(solution)/shard_map/all_to_all | solution.py:81
  70.0 9.4 %all-to-all-start.2 = ((bf16[64,2,8,1024]{3,2,1,0:T(8,128)(2,1)}), bf16[64,2,8,1024]{3,2,1,0:T(8,128)(2,1)S(1)}, u32[]{:S(2)}, u32[]{:S(2)}) async-start(bf16[64,2,8,1024]{3,2,1,0:T(8,128)(2,1)} %pad_maximum_fusion.1), calls=%async_computation.2 | async-start | bytes 4194304 | tf_op jit(solution)/shard_map/all_to_all | solution.py:81
  80.2 1.8 fusion.85
  82.0 2.7 copy.133
  95.1 32.7 %all-to-all-done.2 = bf16[64,2,8,1024]{3,2,1,0:T(8,128)(2,1)S(1)} async-done(((bf16[64,2,8,1024]{3,2,1,0:T(8,128)(2,1)}), bf16[64,2,8,1024]{3,2,1,0:T(8,128)(2,1)S(1)}, u32[]{:S(2)}, u32[]{:S(2)}) %all-to-all-start.2) | async-done | bytes 2097184 | tf_op jit(solution)/shard_map/all_to_all | solution.py:81
  139.9 2.8 maximum_bitcast_fusion
  144.0 2.1 reshape.503
  146.8 9.7 %all-to-all-start.1 = ((bf16[64,2,8,1024]{3,2,1,0:T(8,128)(2,1)}), bf16[64,2,8,1024]{3,2,1,0:T(8,128)(2,1)S(1)}, u32[]{:S(2)}, u32[]{:S(2)}) async-start(bf16[64,2,8,1024]{3,2,1,0:T(8,128)(2,1)} %reshape.503), calls=%async_computation.1 | async-start | bytes 4194304 | tf_op jit(solution)/shard_map/all_to_all | solution.py:102
  158.7 1.8 collective-permute-start.8
  160.5 2.8 fusion.38
  168.5 2.4 fusion.26
  170.9 2.2 stack.166
  173.2 2.2 stack.165
  175.4 3.1 maximum_bitcast_fusion.1
  178.5 2.6 copy.159
  181.2 4.0 %reshape.509 = bf16[64,2,8,1024]{3,2,1,0:T(8,128)(2,1)} reshape(bf16[64,2,2,4,1024]{4,3,2,1,0:T(4,128)(2,1)} %copy.159) | data formatting | bytes 4194304 | tf_op jit(solution)/shard_map/reshape | solution.py:101
  190.7 2.6 collective-permute-done.9
  193.8 4.8 %collective-permute-done.13 = bf16[65536]{0:T(1024)(128)(2,1)S(1)} collective-permute-done((bf16[65536]{0:T(1024)(128)(2,1)S(1)}, bf16[65536]{0:T(1024)(128)(2,1)S(1)}, u32[]{:S(2)}, u32[]{:S(2)}) %collective-permute-start.13) | collective-permute-done | bytes 131104 | tf_op jit(solution)/shard_map/ppermute | solution.py:41
  199.6 4.6 %collective-permute-done.10 = bf16[65536]{0:T(1024)(128)(2,1)S(1)} collective-permute-done((bf16[65536]{0:T(1024)(128)(2,1)S(1)}, bf16[65536]{0:T(1024)(128)(2,1)S(1)}, u32[]{:S(2)}, u32[]{:S(2)}) %collective-permute-start.10) | collective-permute-done | bytes 131104 | tf_op jit(solution)/shard_map/ppermute | solution.py:43
  205.5 2.2 collective-permute-start.11
  216.8 12.3 %all-to-all-start.3 = ((bf16[64,2,8,1024]{3,2,1,0:T(8,128)(2,1)}), bf16[64,2,8,1024]{3,2,1,0:T(8,128)(2,1)}, u32[]{:S(2)}, u32[]{:S(2)}) async-start(bf16[64,2,8,1024]{3,2,1,0:T(8,128)(2,1)} %reshape.509), calls=%async_computation.3 | async-start | bytes 4194304 | tf_op jit(solution)/shard_map/all_to_all | solution.py:102
  237.8 41.0 %all-to-all-done.3 = bf16[64,2,8,1024]{3,2,1,0:T(8,128)(2,1)} async-done(((bf16[64,2,8,1024]{3,2,1,0:T(8,128)(2,1)}), bf16[64,2,8,1024]{3,2,1,0:T(8,128)(2,1)}, u32[]{:S(2)}, u32[]{:S(2)}) %all-to-all-start.3) | async-done | bytes 2097184 | tf_op jit(solution)/shard_map/all_to_all | solution.py:102
  282.4 2.4 fusion.34
  286.4 4.9 %collective-permute-start.4 = (bf16[2,65536]{1,0:T(2,128)(2,1)S(1)}, bf16[2,65536]{1,0:T(2,128)(2,1)S(1)}, u32[]{:S(2)}, u32[]{:S(2)}) collective-permute-start(bf16[2,65536]{1,0:T(2,128)(2,1)S(1)} %dynamic-slice_bitcast_fusion.2), channel_id=1, source_target_pairs={{0,64},{64,0},{128,192},{192,128},{1,65},{65,1},{129,193},{193,129... | collective-permute-start | bytes 786440 | tf_op jit(solution)/shard_map/ppermute | solution.py:39
  304.4 2.2 collective-permute-done.1
  307.2 2.2 collective-permute-done.5
  312.6 2.4 collective-permute-start.3
  323.9 6.8 %slice.127 = bf16[256,64,1,8]{3,1,0,2:T(8,128)(2,1)} reshape(bf16[1,2,65536]{2,1,0:T(2,128)(2,1)S(1)} %get-tuple-element.39) | data formatting | bytes 524288 | tf_op jit(solution)/shard_map/slice | solution.py:55
  330.7 5.0 %copy.170 = bf16[256,64,1,8]{0,3,2,1:T(8,128)(2,1)S(1)} copy(bf16[256,64,1,8]{3,1,0,2:T(8,128)(2,1)} %slice.127) | data formatting | bytes 524288 | tf_op jit(solution)/shard_map/slice | solution.py:55
  335.7 6.8 %slice.125 = bf16[256,64,1,8]{3,1,0,2:T(8,128)(2,1)} reshape(bf16[1,2,65536]{2,1,0:T(2,128)(2,1)S(1)} %get-tuple-element.37) | data formatting | bytes 524288 | tf_op jit(solution)/shard_map/slice | solution.py:55
  342.5 4.8 %copy.169 = bf16[256,64,1,8]{0,3,2,1:T(8,128)(2,1)S(1)} copy(bf16[256,64,1,8]{3,1,0,2:T(8,128)(2,1)} %slice.125) | data formatting | bytes 524288 | tf_op jit(solution)/shard_map/slice | solution.py:55
  (189 shorter events, 99.7 us)
Async XLA Ops:
  0.6 1.9 copy-start.7
  0.7 1.9 copy-start.10
  4.5 64.1 %all-to-all-start = ((bf16[64,2,8,1024]{3,2,1,0:T(8,128)(2,1)}), bf16[64,2,8,1024]{3,2,1,0:T(8,128)(2,1)S(1)}, u32[]{:S(2)}, u32[]{:S(2)}) async-start(bf16[64,2,8,1024]{3,2,1,0:T(8,128)(2,1)} %pad_maximum_fusion), calls=%async_computation | async-start | bytes 4194304 | tf_op jit(solution)/shard_map/all_to_all | solution.py:81
  70.0 57.8 %all-to-all-start.2 = ((bf16[64,2,8,1024]{3,2,1,0:T(8,128)(2,1)}), bf16[64,2,8,1024]{3,2,1,0:T(8,128)(2,1)S(1)}, u32[]{:S(2)}, u32[]{:S(2)}) async-start(bf16[64,2,8,1024]{3,2,1,0:T(8,128)(2,1)} %pad_maximum_fusion.1), calls=%async_computation.2 | async-start | bytes 4194304 | tf_op jit(solution)/shard_map/all_to_all | solution.py:81
  85.0 2.2 copy-start.6
  130.3 2.8 copy-start.15
  134.8 2.6 copy-start.3
  135.9 2.7 copy-start.4
  144.0 2.1 copy-start.18
  146.8 70.0 %all-to-all-start.1 = ((bf16[64,2,8,1024]{3,2,1,0:T(8,128)(2,1)}), bf16[64,2,8,1024]{3,2,1,0:T(8,128)(2,1)S(1)}, u32[]{:S(2)}, u32[]{:S(2)}) async-start(bf16[64,2,8,1024]{3,2,1,0:T(8,128)(2,1)} %reshape.503), calls=%async_computation.1 | async-start | bytes 4194304 | tf_op jit(solution)/shard_map/all_to_all | solution.py:102
  158.7 26.8 %collective-permute-start.8 = (bf16[2,65536]{1,0:T(2,128)(2,1)}, bf16[2,65536]{1,0:T(2,128)(2,1)}, u32[]{:S(2)}, u32[]{:S(2)}) collective-permute-start(bf16[2,65536]{1,0:T(2,128)(2,1)} %dynamic-slice_bitcast_fusion.1), channel_id=1, source_target_pairs={{0,64},{64,0},{128,192},{192,128},{1,65},{65,1},{129,193},{193,129... | collective-permute-start | bytes 786440 | tf_op jit(solution)/shard_map/ppermute | solution.py:39
  166.1 2.4 copy-start.2
  185.1 3.1 copy-start.12
  185.1 3.1 collective-permute-start.12
  187.8 5.5 %collective-permute-start.9 = (bf16[65536]{0:T(1024)(128)(2,1)S(1)}, bf16[65536]{0:T(1024)(128)(2,1)S(1)}, u32[]{:S(2)}, u32[]{:S(2)}) collective-permute-start(bf16[65536]{0:T(1024)(128)(2,1)S(1)} %convert_reduce_fusion.1), channel_id=1, source_target_pairs={{0,128},{64,192},{128,0},{192,64},{1,129},{65,193},{129,1},{193,65... | collective-permute-start | bytes 393224 | tf_op jit(solution)/shard_map/ppermute | solution.py:41
  189.5 9.0 %collective-permute-start.13 = (bf16[65536]{0:T(1024)(128)(2,1)S(1)}, bf16[65536]{0:T(1024)(128)(2,1)S(1)}, u32[]{:S(2)}, u32[]{:S(2)}) collective-permute-start(bf16[65536]{0:T(1024)(128)(2,1)S(1)} %convert_reduce_fusion), channel_id=1, source_target_pairs={{0,128},{64,192},{128,0},{192,64},{1,129},{65,193},{129,1},{193,65... | collective-permute-start | bytes 393224 | tf_op jit(solution)/shard_map/ppermute | solution.py:41
  193.3 10.9 %collective-permute-start.10 = (bf16[65536]{0:T(1024)(128)(2,1)S(1)}, bf16[65536]{0:T(1024)(128)(2,1)S(1)}, u32[]{:S(2)}, u32[]{:S(2)}) collective-permute-start(bf16[65536]{0:T(1024)(128)(2,1)S(1)} %add_convert_fusion.1), channel_id=1, source_target_pairs={{0,128},{64,192},{128,0},{192,64},{1,129},{65,193},{129,1},{193,65... | collective-permute-start | bytes 393224 | tf_op jit(solution)/shard_map/ppermute | solution.py:43
  198.8 8.9 %collective-permute-start.14 = (bf16[65536]{0:T(1024)(128)(2,1)S(1)}, bf16[65536]{0:T(1024)(128)(2,1)S(1)}, u32[]{:S(2)}, u32[]{:S(2)}) collective-permute-start(bf16[65536]{0:T(1024)(128)(2,1)S(1)} %add_convert_fusion), channel_id=1, source_target_pairs={{0,128},{64,192},{128,0},{192,64},{1,129},{65,193},{129,1},{193,65... | collective-permute-start | bytes 393224 | tf_op jit(solution)/shard_map/ppermute | solution.py:43
  205.5 7.5 %collective-permute-start.11 = (bf16[2,65536]{1,0:T(2,128)(2,1)S(1)}, bf16[2,65536]{1,0:T(2,128)(2,1)S(1)}, u32[]{:S(2)}, u32[]{:S(2)}) collective-permute-start(bf16[2,65536]{1,0:T(2,128)(2,1)S(1)} %broadcast_select_fusion.5), channel_id=1, source_target_pairs={{0,64},{64,0},{128,192},{192,128},{1,65},{65,1},{129,193},{193,129... | collective-permute-start | bytes 786440 | tf_op jit(solution)/shard_map/ppermute | solution.py:45
  209.1 4.7 %collective-permute-start.15 = (bf16[2,65536]{1,0:T(2,128)(2,1)S(1)}, bf16[2,65536]{1,0:T(2,128)(2,1)S(1)}, u32[]{:S(2)}, u32[]{:S(2)}) collective-permute-start(bf16[2,65536]{1,0:T(2,128)(2,1)S(1)} %broadcast_select_fusion.4), channel_id=1, source_target_pairs={{0,64},{64,0},{128,192},{192,128},{1,65},{65,1},{129,193},{193,129... | collective-permute-start | bytes 786440 | tf_op jit(solution)/shard_map/ppermute | solution.py:45
  216.8 61.9 %all-to-all-start.3 = ((bf16[64,2,8,1024]{3,2,1,0:T(8,128)(2,1)}), bf16[64,2,8,1024]{3,2,1,0:T(8,128)(2,1)}, u32[]{:S(2)}, u32[]{:S(2)}) async-start(bf16[64,2,8,1024]{3,2,1,0:T(8,128)(2,1)} %reshape.509), calls=%async_computation.3 | async-start | bytes 4194304 | tf_op jit(solution)/shard_map/all_to_all | solution.py:102
  229.1 2.5 copy-start.9
  237.5 61.8 %collective-permute-start = (bf16[2,65536]{1,0:T(2,128)(2,1)}, bf16[2,65536]{1,0:T(2,128)(2,1)}, u32[]{:S(2)}, u32[]{:S(2)}) collective-permute-start(bf16[2,65536]{1,0:T(2,128)(2,1)} %dynamic-slice_bitcast_fusion.3), channel_id=1, source_target_pairs={{0,64},{64,0},{128,192},{192,128},{1,65},{65,1},{129,193},{193,129... | collective-permute-start | bytes 786440 | tf_op jit(solution)/shard_map/ppermute | solution.py:39
  286.4 6.6 %copy-start.22 = (bf16[256,64,1,8]{0,3,2,1:T(8,128)(2,1)S(1)}, bf16[256,64,1,8]{0,3,2,1:T(8,128)(2,1)}, u32[]{:S(2)}) copy-start(bf16[256,64,1,8]{0,3,2,1:T(8,128)(2,1)} %get-tuple-element.41) | copy-start | bytes 786436
  286.4 15.7 %collective-permute-start.4 = (bf16[2,65536]{1,0:T(2,128)(2,1)S(1)}, bf16[2,65536]{1,0:T(2,128)(2,1)S(1)}, u32[]{:S(2)}, u32[]{:S(2)}) collective-permute-start(bf16[2,65536]{1,0:T(2,128)(2,1)S(1)} %dynamic-slice_bitcast_fusion.2), channel_id=1, source_target_pairs={{0,64},{64,0},{128,192},{192,128},{1,65},{65,1},{129,193},{193,129... | collective-permute-start | bytes 786440 | tf_op jit(solution)/shard_map/ppermute | solution.py:39
  295.0 2.5 copy-start.20
  301.5 5.1 %collective-permute-start.1 = (bf16[65536]{0:T(1024)(128)(2,1)S(1)}, bf16[65536]{0:T(1024)(128)(2,1)S(1)}, u32[]{:S(2)}, u32[]{:S(2)}) collective-permute-start(bf16[65536]{0:T(1024)(128)(2,1)S(1)} %convert_reduce_fusion.3), channel_id=1, source_target_pairs={{0,128},{64,192},{128,0},{192,64},{1,129},{65,193},{129,1},{193,65... | collective-permute-start | bytes 393224 | tf_op jit(solution)/shard_map/ppermute | solution.py:41
  303.4 6.0 %collective-permute-start.5 = (bf16[65536]{0:T(1024)(128)(2,1)S(1)}, bf16[65536]{0:T(1024)(128)(2,1)S(1)}, u32[]{:S(2)}, u32[]{:S(2)}) collective-permute-start(bf16[65536]{0:T(1024)(128)(2,1)S(1)} %convert_reduce_fusion.2), channel_id=1, source_target_pairs={{0,128},{64,192},{128,0},{192,64},{1,129},{65,193},{129,1},{193,65... | collective-permute-start | bytes 393224 | tf_op jit(solution)/shard_map/ppermute | solution.py:41
  306.6 4.7 %collective-permute-start.2 = (bf16[65536]{0:T(1024)(128)(2,1)S(1)}, bf16[65536]{0:T(1024)(128)(2,1)S(1)}, u32[]{:S(2)}, u32[]{:S(2)}) collective-permute-start(bf16[65536]{0:T(1024)(128)(2,1)S(1)} %add_convert_fusion.3), channel_id=1, source_target_pairs={{0,128},{64,192},{128,0},{192,64},{1,129},{65,193},{129,1},{193,65... | collective-permute-start | bytes 393224 | tf_op jit(solution)/shard_map/ppermute | solution.py:43
  309.7 5.3 %collective-permute-start.6 = (bf16[65536]{0:T(1024)(128)(2,1)S(1)}, bf16[65536]{0:T(1024)(128)(2,1)S(1)}, u32[]{:S(2)}, u32[]{:S(2)}) collective-permute-start(bf16[65536]{0:T(1024)(128)(2,1)S(1)} %add_convert_fusion.2), channel_id=1, source_target_pairs={{0,128},{64,192},{128,0},{192,64},{1,129},{65,193},{129,1},{193,65... | collective-permute-start | bytes 393224 | tf_op jit(solution)/shard_map/ppermute | solution.py:43
  312.6 7.5 %collective-permute-start.3 = (bf16[2,65536]{1,0:T(2,128)(2,1)S(1)}, bf16[2,65536]{1,0:T(2,128)(2,1)S(1)}, u32[]{:S(2)}, u32[]{:S(2)}) collective-permute-start(bf16[2,65536]{1,0:T(2,128)(2,1)S(1)} %broadcast_select_fusion.7), channel_id=1, source_target_pairs={{0,64},{64,0},{128,192},{192,128},{1,65},{65,1},{129,193},{193,129... | collective-permute-start | bytes 786440 | tf_op jit(solution)/shard_map/ppermute | solution.py:45
  316.4 5.1 %collective-permute-start.7 = (bf16[2,65536]{1,0:T(2,128)(2,1)S(1)}, bf16[2,65536]{1,0:T(2,128)(2,1)S(1)}, u32[]{:S(2)}, u32[]{:S(2)}) collective-permute-start(bf16[2,65536]{1,0:T(2,128)(2,1)S(1)} %broadcast_select_fusion.6), channel_id=1, source_target_pairs={{0,64},{64,0},{128,192},{192,128},{1,65},{65,1},{129,193},{193,129... | collective-permute-start | bytes 786440 | tf_op jit(solution)/shard_map/ppermute | solution.py:45
  (12 other events, 14.3 us)

commit v4 on v2

--- a/solution.py
+++ b/solution.py
@@ -28,22 +28,21 @@
     return lax.dynamic_index_in_dim(pair, index, axis=0, keepdims=False)
 
 
-def dp_sum(grad):
+def dp_sum(grad, scale):
     size = lax.axis_size("dp")
     index = lax.axis_index("dp")
     core = index % 2
     row = index // 2
     core_swap = [(i, i ^ 1) for i in range(size)]
     row_swap = [(i, i ^ 2) for i in range(size)]
-    parts = grad.astype(jnp.bfloat16).reshape(2, 2, -1)
-    got = lax.ppermute(pick(parts, 1 - core), "dp", core_swap)
-    half = pick(parts, core).astype(jnp.float32) + got.astype(jnp.float32)
-    got = lax.ppermute(pick(half, 1 - row).astype(jnp.bfloat16), "dp", row_swap)
-    quarter = (pick(half, row) + got.astype(jnp.float32)).astype(jnp.bfloat16)
-    got = lax.ppermute(quarter, "dp", row_swap)
-    half = jnp.where(row == 0, jnp.stack([quarter, got]), jnp.stack([got, quarter]))
-    got = lax.ppermute(half, "dp", core_swap)
-    full = jnp.where(core == 0, jnp.stack([half, got]), jnp.stack([got, half]))
+    own = (grad * scale).astype(jnp.bfloat16)
+    got = lax.ppermute(own, "dp", core_swap)
+    pair = (own.astype(jnp.float32) + got.astype(jnp.float32)).astype(jnp.bfloat16).reshape(2, -1)
+    mine = pick(pair, core)
+    got = lax.ppermute(mine, "dp", row_swap)
+    total = (mine.astype(jnp.float32) + got.astype(jnp.float32)).astype(jnp.bfloat16)
+    got = lax.ppermute(total, "dp", core_swap)
+    full = jnp.where(core == 0, jnp.stack([total, got]), jnp.stack([got, total]))
     return full.reshape(grad.shape).astype(jnp.float32)
 
 
@@ -85,7 +84,7 @@
         uhg = g_uh if uhg is None else uhg + g_uh
 
         send2 = jnp.stack([back_t, tile_grad_t], axis=0).reshape(2, local_blocks, nb, expand, rows)
-        send2 = send2.transpose(2, 0, 1, 3, 4)
+        send2 = send2.transpose(2, 0, 1, 3, 4).reshape(nb, 2, chunk, rows)
         recv2 = lax.all_to_all(send2, "block", 0, 0, tiled=True)
         rows_t = recv2[:, 0].reshape(nb * chunk, rows)
         rows_grad_t = recv2[:, 1].reshape(nb * chunk, rows)
@@ -97,17 +96,17 @@
         dwg = g_dw if dwg is None else dwg + g_dw
         uwg = g_uw if uwg is None else uwg + g_uw
 
-    dhg = dp_sum(dhg)
-    uhg = dp_sum(uhg)
-    dwg = dp_sum(dwg)
-    uwg = dp_sum(uwg)
+    dhg = dp_sum(dhg, grad_scale)
+    uhg = dp_sum(uhg, grad_scale)
+    dwg = dp_sum(dwg, grad_scale)
+    uwg = dp_sum(uwg, grad_scale)
     return (
         jnp.concatenate(outs, axis=0),
         jnp.concatenate(tgrads, axis=0),
-        (uwg * grad_scale)[None],
-        uhg * grad_scale,
-        dhg * grad_scale,
-        (dwg * grad_scale)[None],
+        uwg[None],
+        uhg,
+        dhg,
+        dwg[None],
     )
 
 

time: 321 us -> 311 us (0.969)
  waiting for transfers between devices: 126 us -> 142 us
  matrix products: 36.7 us -> 26.9 us
  other arithmetic: 28.9 us -> 19.6 us
  starting transfers between devices: 66.3 us -> 61.3 us
    convert_element_type x4 -> x12, other arithmetic: 0.1 us -> 14.5 us  [the longest x4 10.6 us: dp_sum(): return full.reshape(grad.shape).astype(jnp.float32)]
    all_to_all x2, waiting for transfers between devices: 26.3 us -> 39.2 us  [shards(): recv2 = lax.all_to_all(send2, 'block', 0, 0, tiled=True)]
    another operation x4 -> x8, local copies, waits for them, and re-layouts: 5.51 us -> 16.3 us  [shards(): jnp.stack([back_t, tile_grad_t], axis=0)]
    dot_general x24, matrix products: 36.7 us -> 26.9 us  [dot(): lax.dot_general(left, right, ((left_dims, right_dims), batch), preferred_...]
    select_n x8 -> x0, other arithmetic: 9.39 us -> none  [dp_sum(): jnp.where(row == 0, jnp.stack([quarter, got]), jnp.stack([got, quarter]))]
    mul x4 -> x0, local copies, waits for them, and re-layouts: 8.95 us -> none  [the longest x1 2.75 us: shards(): dhg * grad_scale]
    another operation x20 -> x8, local copies, waits for them, and re-layouts: 9.1 us -> 2.18 us  [dp_sum(): jnp.stack([total, got])]
    all_to_all x2, starting transfers between devices: 22.2 us -> 15.4 us  [shards(): recv2 = lax.all_to_all(send2, 'block', 0, 0, tiled=True)]
  transfers between devices with their start and end apart: 20 -> 16, of which waited for: 10 -> 8; matrix products, arithmetic and copies ran while one was open for 28% -> 23% of each run, Pallas kernels for 0% -> 0%
where the time goes in v4:
time: 311 us; the launch traced here: 306 us
  waiting for transfers between devices  142 us (46%)
  starting transfers between devices  61.3 us (20%)
  local copies, waits for them, and re-layouts  54.3 us (17%)
  matrix products  26.9 us (9%)
  other arithmetic  19.6 us (6%)
    all_to_all x2, waiting for transfers between devices, shards(): recv = lax.all_to_all(send, 'block', 0, 0, tiled=True)  79.7 us
    all_to_all x2, waiting for transfers between devices, shards(): recv2 = lax.all_to_all(send2, 'block', 0, 0, tiled=True)  39.2 us
    dot_general x24, matrix products, dot(): lax.dot_general(left, right, ((left_dims, right_dims), batch), preferred_...  26.9 us
    all_to_all x2, starting transfers between devices, shards(): recv = lax.all_to_all(send, 'block', 0, 0, tiled=True)  24.6 us
    ppermute x4, waiting for transfers between devices, dp_sum(): got = lax.ppermute(mine, 'dp', row_swap)  23.5 us
    another operation x8, local copies, waits for them, and re-layouts, shards(): jnp.stack([back_t, tile_grad_t], axis=0)  16.3 us
    all_to_all x2, starting transfers between devices, shards(): recv2 = lax.all_to_all(send2, 'block', 0, 0, tiled=True)  15.4 us
    ppermute x4, starting transfers between devices, dp_sum(): got = lax.ppermute(own, 'dp', core_swap)  11 us
  transfers between devices with their start and end apart: 16, of which 8 were waited for; matrix products, arithmetic and copies ran while one was open for 23% of the time, Pallas kernels for 0%

profile of v4, /device:TPU:1, one launch (start us, length us, event | category | flops | bytes accessed | tf_op | source)
XLA Modules:
  0.0 305.9 jit_solution(12004184694973254715)
XLA Ops:
  5.3 15.2 %all-to-all-start = ((bf16[64,2,16,512]{3,2,1,0:T(8,128)(2,1)}), bf16[64,2,16,512]{3,2,1,0:T(8,128)(2,1)S(1)}, u32[]{:S(2)}, u32[]{:S(2)}) async-start(bf16[64,2,16,512]{3,2,1,0:T(8,128)(2,1)} %pad_maximum_fusion), calls=%async_computation | async-start | bytes 4194304 | tf_op jit(solution)/shard_map/all_to_all | solution.py:70
  25.1 44.5 %all-to-all-done = bf16[64,2,16,512]{3,2,1,0:T(8,128)(2,1)S(1)} async-done(((bf16[64,2,16,512]{3,2,1,0:T(8,128)(2,1)}), bf16[64,2,16,512]{3,2,1,0:T(8,128)(2,1)S(1)}, u32[]{:S(2)}, u32[]{:S(2)}) %all-to-all-start) | async-done | bytes 2097184 | tf_op jit(solution)/shard_map/all_to_all | solution.py:70
  70.9 9.4 %all-to-all-start.2 = ((bf16[64,2,16,512]{3,2,1,0:T(8,128)(2,1)}), bf16[64,2,16,512]{3,2,1,0:T(8,128)(2,1)S(1)}, u32[]{:S(2)}, u32[]{:S(2)}) async-start(bf16[64,2,16,512]{3,2,1,0:T(8,128)(2,1)} %pad_maximum_fusion.2), calls=%async_computation.2 | async-start | bytes 4194304 | tf_op jit(solution)/shard_map/all_to_all | solution.py:70
  80.3 2.8 copy.90
  93.5 35.2 %all-to-all-done.2 = bf16[64,2,16,512]{3,2,1,0:T(8,128)(2,1)S(1)} async-done(((bf16[64,2,16,512]{3,2,1,0:T(8,128)(2,1)}), bf16[64,2,16,512]{3,2,1,0:T(8,128)(2,1)S(1)}, u32[]{:S(2)}, u32[]{:S(2)}) %all-to-all-start.2) | async-done | bytes 2097184 | tf_op jit(solution)/shard_map/all_to_all | solution.py:70
  131.7 2.1 stack.81
  133.8 2.4 copy.98
  136.3 2.1 stack.82
  145.7 5.1 %collective-permute-start.3 = (bf16[4,256,256]{2,1,0:T(8,128)(2,1)}, bf16[4,256,256]{2,1,0:T(8,128)(2,1)}, u32[]{:S(2)}, u32[]{:S(2)}) collective-permute-start(bf16[4,256,256]{2,1,0:T(8,128)(2,1)} %fusion.30), channel_id=1, source_target_pairs={{0,64},{64,0},{128,192},{192,128},{1,65},{65,1},{129,193},{193,129... | collective-permute-start | bytes 1572872 | tf_op jit(solution)/shard_map/ppermute | solution.py:39
  153.2 2.5 copy.100
  155.7 6.0 %all-to-all-start.1 = ((bf16[64,2,16,512]{3,2,1,0:T(8,128)(2,1)}), bf16[64,2,16,512]{3,2,1,0:T(8,128)(2,1)S(1)}, u32[]{:S(2)}, u32[]{:S(2)}) async-start(bf16[64,2,16,512]{3,2,1,0:T(8,128)(2,1)} %copy.100), calls=%async_computation.1 | async-start | bytes 4194304 | tf_op jit(solution)/shard_map/all_to_all | solution.py:88
  161.7 2.1 stack.86
  163.9 2.4 copy.113
  166.3 2.1 stack.85
  170.2 2.5 copy.114
  174.9 2.6 dynamic-slice_reduce_fusion.2
  182.0 8.0 %collective-permute-done.4 = bf16[131072]{0:T(1024)(128)(2,1)} collective-permute-done((bf16[131072]{0:T(1024)(128)(2,1)S(1)}, bf16[131072]{0:T(1024)(128)(2,1)}, u32[]{:S(2)}, u32[]{:S(2)}) %collective-permute-start.4) | collective-permute-done | bytes 262176 | tf_op jit(solution)/shard_map/ppermute | solution.py:42
  191.0 2.3 collective-permute-start.5
  193.3 7.4 %collective-permute-done.7 = bf16[131072]{0:T(1024)(128)(2,1)S(1)} collective-permute-done((bf16[131072]{0:T(1024)(128)(2,1)S(1)}, bf16[131072]{0:T(1024)(128)(2,1)S(1)}, u32[]{:S(2)}, u32[]{:S(2)}) %collective-permute-start.7) | collective-permute-done | bytes 262176 | tf_op jit(solution)/shard_map/ppermute | solution.py:42
  201.0 2.0 collective-permute-start.8
  203.6 3.1 %fusion.46 = f32[2,131072]{1,0:T(2,128)} fusion(pred[]{:T(512)S(6)} %eq.11, bf16[1,131072]{1,0:T(2,128)(2,1)S(1)} %stack.93, bf16[1,131072]{1,0:T(2,128)(2,1)S(1)} %stack.92), kind=kLoop, calls=%fused_computation.84 | loop fusion | flops 2621440 | bytes 1572865 | tf_op jit(solution)/shard_map/convert_element_type | solution.py:46
  207.1 3.9 %all-to-all-done.1 = bf16[64,2,16,512]{3,2,1,0:T(8,128)(2,1)S(1)} async-done(((bf16[64,2,16,512]{3,2,1,0:T(8,128)(2,1)}), bf16[64,2,16,512]{3,2,1,0:T(8,128)(2,1)S(1)}, u32[]{:S(2)}, u32[]{:S(2)}) %all-to-all-start.1) | async-done | bytes 2097184 | tf_op jit(solution)/shard_map/all_to_all | solution.py:88
  210.9 9.4 %all-to-all-start.3 = ((bf16[64,2,16,512]{3,2,1,0:T(8,128)(2,1)}), bf16[64,2,16,512]{3,2,1,0:T(8,128)(2,1)}, u32[]{:S(2)}, u32[]{:S(2)}) async-start(bf16[64,2,16,512]{3,2,1,0:T(8,128)(2,1)} %copy.114), calls=%async_computation.3 | async-start | bytes 4194304 | tf_op jit(solution)/shard_map/all_to_all | solution.py:88
  220.4 3.1 %fusion.47 = f32[2,131072]{1,0:T(2,128)} fusion(pred[]{:T(512)S(6)} %eq.11, bf16[1,131072]{1,0:T(2,128)(2,1)S(1)} %stack.97, bf16[1,131072]{1,0:T(2,128)(2,1)S(1)} %stack.96), kind=kLoop, calls=%fused_computation.85 | loop fusion | flops 2621440 | bytes 1572865 | tf_op jit(solution)/shard_map/convert_element_type | solution.py:46
  223.5 3.1 %reshape.139 = f32[4,256,256]{2,1,0:T(8,128)} reshape(f32[2,131072]{1,0:T(2,128)} %fusion.46) | data formatting | bytes 2097152 | tf_op jit(solution)/shard_map/convert_element_type | solution.py:46
  226.6 3.1 %reshape.140 = f32[4,256,256]{2,1,0:T(8,128)} reshape(f32[2,131072]{1,0:T(2,128)} %fusion.47) | data formatting | bytes 2097152 | tf_op jit(solution)/shard_map/convert_element_type | solution.py:46
  233.4 35.3 %all-to-all-done.3 = bf16[64,2,16,512]{3,2,1,0:T(8,128)(2,1)} async-done(((bf16[64,2,16,512]{3,2,1,0:T(8,128)(2,1)}), bf16[64,2,16,512]{3,2,1,0:T(8,128)(2,1)}, u32[]{:S(2)}, u32[]{:S(2)}) %all-to-all-start.3) | async-done | bytes 2097184 | tf_op jit(solution)/shard_map/all_to_all | solution.py:88
  270.9 5.2 %collective-permute-start.9 = (bf16[1024,256]{1,0:T(8,128)(2,1)S(1)}, bf16[1024,256]{1,0:T(8,128)(2,1)S(1)}, u32[]{:S(2)}, u32[]{:S(2)}) collective-permute-start(bf16[1024,256]{1,0:T(8,128)(2,1)S(1)} %fusion.29), channel_id=1, source_target_pairs={{0,64},{64,0},{128,192},{192,128},{1,65},{65,1},{129,193},{193,129... | collective-permute-start | bytes 1572872 | tf_op jit(solution)/shard_map/ppermute | solution.py:39
  285.8 4.0 %collective-permute-done.10 = bf16[131072]{0:T(1024)(128)(2,1)S(1)} collective-permute-done((bf16[131072]{0:T(1024)(128)(2,1)S(1)}, bf16[131072]{0:T(1024)(128)(2,1)S(1)}, u32[]{:S(2)}, u32[]{:S(2)}) %collective-permute-start.10) | collective-permute-done | bytes 262176 | tf_op jit(solution)/shard_map/ppermute | solution.py:42
  291.3 4.1 %collective-permute-done.1 = bf16[131072]{0:T(1024)(128)(2,1)S(1)} collective-permute-done((bf16[131072]{0:T(1024)(128)(2,1)S(1)}, bf16[131072]{0:T(1024)(128)(2,1)S(1)}, u32[]{:S(2)}, u32[]{:S(2)}) %collective-permute-start.1) | collective-permute-done | bytes 262176 | tf_op jit(solution)/shard_map/ppermute | solution.py:42
  297.3 2.2 fusion.48
  301.6 2.2 fusion.45
  (119 shorter events, 66.9 us)
Async XLA Ops:
  0.6 84.2 %copy-start = (bf16[4,256,256]{2,1,0:T(8,128)(2,1)S(1)}, bf16[4,256,256]{2,1,0:T(8,128)(2,1)}, u32[]{:S(2)}) copy-start(bf16[4,256,256]{2,1,0:T(8,128)(2,1)} %param.9) | copy-start | bytes 1572868
  0.6 1.7 copy-start.10
  5.3 15.2 %copy-start.8 = (bf16[1,256,1024]{2,1,0:T(8,128)(2,1)S(1)}, bf16[1,256,1024]{2,1,0:T(8,128)(2,1)}, u32[]{:S(2)}) copy-start(bf16[1,256,1024]{2,1,0:T(8,128)(2,1)} %param.8) | copy-start | bytes 1572868
  5.3 64.2 %all-to-all-start = ((bf16[64,2,16,512]{3,2,1,0:T(8,128)(2,1)}), bf16[64,2,16,512]{3,2,1,0:T(8,128)(2,1)S(1)}, u32[]{:S(2)}, u32[]{:S(2)}) async-start(bf16[64,2,16,512]{3,2,1,0:T(8,128)(2,1)} %pad_maximum_fusion), calls=%async_computation | async-start | bytes 4194304 | tf_op jit(solution)/shard_map/all_to_all | solution.py:70
  20.6 1.5 copy-start.11
  69.5 1.3 copy-start.2
  70.9 57.8 %all-to-all-start.2 = ((bf16[64,2,16,512]{3,2,1,0:T(8,128)(2,1)}), bf16[64,2,16,512]{3,2,1,0:T(8,128)(2,1)S(1)}, u32[]{:S(2)}, u32[]{:S(2)}) async-start(bf16[64,2,16,512]{3,2,1,0:T(8,128)(2,1)} %pad_maximum_fusion.2), calls=%async_computation.2 | async-start | bytes 4194304 | tf_op jit(solution)/shard_map/all_to_all | solution.py:70
  84.9 1.1 copy-start.7
  142.9 1.5 copy-start.4
  144.4 6.4 %copy-start.3 = (f32[4,256,256]{2,1,0:T(8,128)S(1)}, f32[4,256,256]{2,1,0:T(8,128)}, u32[]{:S(2)}) copy-start(f32[4,256,256]{2,1,0:T(8,128)} %fusion.36) | copy-start | bytes 3145732
  145.7 27.0 %collective-permute-start.3 = (bf16[4,256,256]{2,1,0:T(8,128)(2,1)}, bf16[4,256,256]{2,1,0:T(8,128)(2,1)}, u32[]{:S(2)}, u32[]{:S(2)}) collective-permute-start(bf16[4,256,256]{2,1,0:T(8,128)(2,1)} %fusion.30), channel_id=1, source_target_pairs={{0,64},{64,0},{128,192},{192,128},{1,65},{65,1},{129,193},{193,129... | collective-permute-start | bytes 1572872 | tf_op jit(solution)/shard_map/ppermute | solution.py:39
  151.4 1.6 copy-start.5
  151.4 26.6 %collective-permute-start.6 = (bf16[4,256,256]{2,1,0:T(8,128)(2,1)S(1)}, bf16[4,256,256]{2,1,0:T(8,128)(2,1)}, u32[]{:S(2)}, u32[]{:S(2)}) collective-permute-start(bf16[4,256,256]{2,1,0:T(8,128)(2,1)S(1)} %fusion.31), channel_id=1, source_target_pairs={{0,64},{64,0},{128,192},{192,128},{1,65},{65,1},{129,193},{193,129... | collective-permute-start | bytes 1572872 | tf_op jit(solution)/shard_map/ppermute | solution.py:39
  155.7 55.2 %all-to-all-start.1 = ((bf16[64,2,16,512]{3,2,1,0:T(8,128)(2,1)}), bf16[64,2,16,512]{3,2,1,0:T(8,128)(2,1)S(1)}, u32[]{:S(2)}, u32[]{:S(2)}) async-start(bf16[64,2,16,512]{3,2,1,0:T(8,128)(2,1)} %copy.100), calls=%async_computation.1 | async-start | bytes 4194304 | tf_op jit(solution)/shard_map/all_to_all | solution.py:88
  168.4 1.5 copy-start.6
  177.5 12.5 %collective-permute-start.4 = (bf16[131072]{0:T(1024)(128)(2,1)S(1)}, bf16[131072]{0:T(1024)(128)(2,1)}, u32[]{:S(2)}, u32[]{:S(2)}) collective-permute-start(bf16[131072]{0:T(1024)(128)(2,1)S(1)} %dynamic-slice_reduce_fusion.2), channel_id=1, source_target_pairs={{0,128},{64,192},{128,0},{192,64},{1,129},{65,193},{129,1},{193,65... | collective-permute-start | bytes 786440 | tf_op jit(solution)/shard_map/ppermute | solution.py:42
  180.9 19.8 %collective-permute-start.7 = (bf16[131072]{0:T(1024)(128)(2,1)S(1)}, bf16[131072]{0:T(1024)(128)(2,1)S(1)}, u32[]{:S(2)}, u32[]{:S(2)}) collective-permute-start(bf16[131072]{0:T(1024)(128)(2,1)S(1)} %dynamic-slice_reduce_fusion.1), channel_id=1, source_target_pairs={{0,128},{64,192},{128,0},{192,64},{1,129},{65,193},{129,1},{193,65... | collective-permute-start | bytes 786440 | tf_op jit(solution)/shard_map/ppermute | solution.py:42
  191.0 12.3 %collective-permute-start.5 = (bf16[131072]{0:T(1024)(128)(2,1)S(1)}, bf16[131072]{0:T(1024)(128)(2,1)S(1)}, u32[]{:S(2)}, u32[]{:S(2)}) collective-permute-start(bf16[131072]{0:T(1024)(128)(2,1)S(1)} %add_convert_fusion.6), channel_id=1, source_target_pairs={{0,64},{64,0},{128,192},{192,128},{1,65},{65,1},{129,193},{193,129... | collective-permute-start | bytes 786440 | tf_op jit(solution)/shard_map/ppermute | solution.py:44
  201.0 5.7 %collective-permute-start.8 = (bf16[131072]{0:T(1024)(128)(2,1)S(1)}, bf16[131072]{0:T(1024)(128)(2,1)S(1)}, u32[]{:S(2)}, u32[]{:S(2)}) collective-permute-start(bf16[131072]{0:T(1024)(128)(2,1)S(1)} %add_convert_fusion.5), channel_id=1, source_target_pairs={{0,64},{64,0},{128,192},{192,128},{1,65},{65,1},{129,193},{193,129... | collective-permute-start | bytes 786440 | tf_op jit(solution)/shard_map/ppermute | solution.py:44
  210.9 57.7 %all-to-all-start.3 = ((bf16[64,2,16,512]{3,2,1,0:T(8,128)(2,1)}), bf16[64,2,16,512]{3,2,1,0:T(8,128)(2,1)}, u32[]{:S(2)}, u32[]{:S(2)}) async-start(bf16[64,2,16,512]{3,2,1,0:T(8,128)(2,1)} %copy.114), calls=%async_computation.3 | async-start | bytes 4194304 | tf_op jit(solution)/shard_map/all_to_all | solution.py:88
  229.9 2.0 copy-start.9
  230.7 1.7 copy-start.13
  268.7 1.8 copy-start.14
  270.5 5.7 %copy-start.16 = (bf16[1024,256]{1,0:T(8,128)(2,1)S(1)}, bf16[1024,256]{1,0:T(8,128)(2,1)}, u32[]{:S(2)}) copy-start(bf16[1024,256]{1,0:T(8,128)(2,1)} %param.6) | copy-start | bytes 1572868
  270.9 8.9 %collective-permute-start.9 = (bf16[1024,256]{1,0:T(8,128)(2,1)S(1)}, bf16[1024,256]{1,0:T(8,128)(2,1)S(1)}, u32[]{:S(2)}, u32[]{:S(2)}) collective-permute-start(bf16[1024,256]{1,0:T(8,128)(2,1)S(1)} %fusion.29), channel_id=1, source_target_pairs={{0,64},{64,0},{128,192},{192,128},{1,65},{65,1},{129,193},{193,129... | collective-permute-start | bytes 1572872 | tf_op jit(solution)/shard_map/ppermute | solution.py:39
  276.6 1.6 copy-start.17
  277.1 5.3 %collective-permute-start = (bf16[256,1024]{0,1:T(8,128)(2,1)S(1)}, bf16[256,1024]{0,1:T(8,128)(2,1)S(1)}, u32[]{:S(2)}, u32[]{:S(2)}) collective-permute-start(bf16[256,1024]{0,1:T(8,128)(2,1)S(1)} %fusion.32), channel_id=1, source_target_pairs={{0,64},{64,0},{128,192},{192,128},{1,65},{65,1},{129,193},{193,129... | collective-permute-start | bytes 1572872 | tf_op jit(solution)/shard_map/ppermute | solution.py:39
  281.6 8.1 %collective-permute-start.10 = (bf16[131072]{0:T(1024)(128)(2,1)S(1)}, bf16[131072]{0:T(1024)(128)(2,1)S(1)}, u32[]{:S(2)}, u32[]{:S(2)}) collective-permute-start(bf16[131072]{0:T(1024)(128)(2,1)S(1)} %dynamic-slice_reduce_fusion), channel_id=1, source_target_pairs={{0,128},{64,192},{128,0},{192,64},{1,129},{65,193},{129,1},{193,65... | collective-permute-start | bytes 786440 | tf_op jit(solution)/shard_map/ppermute | solution.py:42
  284.6 10.8 %collective-permute-start.1 = (bf16[131072]{0:T(1024)(128)(2,1)S(1)}, bf16[131072]{0:T(1024)(128)(2,1)S(1)}, u32[]{:S(2)}, u32[]{:S(2)}) collective-permute-start(bf16[131072]{0:T(1024)(128)(2,1)S(1)} %dynamic-slice_reduce_fusion.3), channel_id=1, source_target_pairs={{0,128},{64,192},{128,0},{192,64},{1,129},{65,193},{129,1},{193,65... | collective-permute-start | bytes 786440 | tf_op jit(solution)/shard_map/ppermute | solution.py:42
  289.9 7.1 %collective-permute-start.11 = (bf16[131072]{0:T(1024)(128)(2,1)S(1)}, bf16[131072]{0:T(1024)(128)(2,1)S(1)}, u32[]{:S(2)}, u32[]{:S(2)}) collective-permute-start(bf16[131072]{0:T(1024)(128)(2,1)S(1)} %add_convert_fusion.4), channel_id=1, source_target_pairs={{0,64},{64,0},{128,192},{192,128},{1,65},{65,1},{129,193},{193,129... | collective-permute-start | bytes 786440 | tf_op jit(solution)/shard_map/ppermute | solution.py:44
  295.7 5.6 %collective-permute-start.2 = (bf16[131072]{0:T(1024)(128)(2,1)S(1)}, bf16[131072]{0:T(1024)(128)(2,1)S(1)}, u32[]{:S(2)}, u32[]{:S(2)}) collective-permute-start(bf16[131072]{0:T(1024)(128)(2,1)S(1)} %add_convert_fusion.7), channel_id=1, source_target_pairs={{0,64},{64,0},{128,192},{192,128},{1,65},{65,1},{129,193},{193,129... | collective-permute-start | bytes 786440 | tf_op jit(solution)/shard_map/ppermute | solution.py:44
  301.3 4.3 %copy-start.1 = (bf16[4,256,256]{2,1,0:T(8,128)(2,1)S(1)}, bf16[4,256,256]{2,1,0:T(8,128)(2,1)}, u32[]{:S(2)}) copy-start(bf16[4,256,256]{2,1,0:T(8,128)(2,1)} %param.9) | copy-start | bytes 1572868
  (2 other events, 2.1 us)

commit v5 on v4

--- a/solution.py
+++ b/solution.py
@@ -37,13 +37,14 @@
     row_swap = [(i, i ^ 2) for i in range(size)]
     own = (grad * scale).astype(jnp.bfloat16)
     got = lax.ppermute(own, "dp", core_swap)
-    pair = (own.astype(jnp.float32) + got.astype(jnp.float32)).astype(jnp.bfloat16).reshape(2, -1)
+    pair = (own.astype(jnp.float32) + got.astype(jnp.float32)).astype(jnp.bfloat16)
+    pair = pair.reshape((2, grad.shape[0] // 2) + grad.shape[1:])
     mine = pick(pair, core)
     got = lax.ppermute(mine, "dp", row_swap)
     total = (mine.astype(jnp.float32) + got.astype(jnp.float32)).astype(jnp.bfloat16)
     got = lax.ppermute(total, "dp", core_swap)
     full = jnp.where(core == 0, jnp.stack([total, got]), jnp.stack([got, total]))
-    return full.reshape(grad.shape).astype(jnp.float32)
+    return full.astype(jnp.float32).reshape(grad.shape)
 
 
 def shards(tokens, cotangent, up_width, up_hidden, down_hidden, down_width):

time: 311 us -> 273 us (0.88); the launches traced: 306 us -> 272 us
  local copies, waits for them, and re-layouts: 54.3 us -> 38.2 us
  other arithmetic: 19.6 us -> 10.6 us
  waiting for transfers between devices: 142 us -> 133 us
    all_to_all x2, waiting for transfers between devices: 79.7 us -> 69 us  [shards(): recv = lax.all_to_all(send, 'block', 0, 0, tiled=True)]
    convert_element_type x5 -> x0, local copies, waits for them, and re-layouts: 10.1 us -> none  [the longest x4 9.93 us: dp_sum(): return full.reshape(grad.shape).astype(jnp.float32)]
    dynamic_slice x4 -> x0, local copies, waits for them, and re-layouts: 7.17 us -> none  [pick(): return lax.dynamic_index_in_dim(pair, index, axis=0, keepdims=False)]
    convert_element_type x4, other arithmetic: 10.6 us -> 4.32 us  [dp_sum(): return full.astype(jnp.float32).reshape(grad.shape)]
    all_to_all x2, waiting for transfers between devices: 39.2 us -> 33.8 us  [shards(): recv2 = lax.all_to_all(send2, 'block', 0, 0, tiled=True)]
    all_to_all x2, starting transfers between devices: 15.4 us -> 20.5 us  [shards(): recv2 = lax.all_to_all(send2, 'block', 0, 0, tiled=True)]
    ppermute x4, waiting for transfers between devices: 23.5 us -> 28.1 us  [dp_sum(): got = lax.ppermute(mine, 'dp', row_swap)]
  transfers between devices with their start and end apart: 16 -> 16, of which waited for: 8 -> 10; matrix products, arithmetic and copies ran while one was open for 23% -> 23% of each run, Pallas kernels for 0% -> 0%
where the time goes in v5:
time: 273 us; the launch traced here: 272 us
  waiting for transfers between devices  133 us (49%)
  starting transfers between devices  62.1 us (23%)
  local copies, waits for them, and re-layouts  38.2 us (14%)
  matrix products  27.2 us (10%)
  other arithmetic  10.6 us (4%)
    all_to_all x2, waiting for transfers between devices, shards(): recv = lax.all_to_all(send, 'block', 0, 0, tiled=True)  69 us
    all_to_all x2, waiting for transfers between devices, shards(): recv2 = lax.all_to_all(send2, 'block', 0, 0, tiled=True)  33.8 us
    ppermute x4, waiting for transfers between devices, dp_sum(): got = lax.ppermute(mine, 'dp', row_swap)  28.1 us
    dot_general x24, matrix products, dot(): lax.dot_general(left, right, ((left_dims, right_dims), batch), preferred_...  27.2 us
    all_to_all x2, starting transfers between devices, shards(): recv = lax.all_to_all(send, 'block', 0, 0, tiled=True)  24.7 us
    all_to_all x2, starting transfers between devices, shards(): recv2 = lax.all_to_all(send2, 'block', 0, 0, tiled=True)  20.5 us
    another operation x8, local copies, waits for them, and re-layouts, shards(): jnp.stack([back_t, tile_grad_t], axis=0)  16.6 us
    ppermute x4, starting transfers between devices, dp_sum(): got = lax.ppermute(own, 'dp', core_swap)  9.48 us
  transfers between devices with their start and end apart: 16, of which 10 were waited for; matrix products, arithmetic and copies ran while one was open for 23% of the time, Pallas kernels for 0%

profile of v5, /device:TPU:1, one launch (start us, length us, event | category | flops | bytes accessed | tf_op | source)
XLA Modules:
  0.0 272.3 jit_solution(11236633568844754022)
XLA Ops:
  0.7 1.7 convolution_convert_fusion.3
  5.3 15.2 %all-to-all-start = ((bf16[64,2,16,512]{3,2,1,0:T(8,128)(2,1)}), bf16[64,2,16,512]{3,2,1,0:T(8,128)(2,1)S(1)}, u32[]{:S(2)}, u32[]{:S(2)}) async-start(bf16[64,2,16,512]{3,2,1,0:T(8,128)(2,1)} %pad_maximum_fusion), calls=%async_computation | async-start | bytes 4194304 | tf_op jit(solution)/shard_map/all_to_all | solution.py:71
  25.1 44.5 %all-to-all-done = bf16[64,2,16,512]{3,2,1,0:T(8,128)(2,1)S(1)} async-done(((bf16[64,2,16,512]{3,2,1,0:T(8,128)(2,1)}), bf16[64,2,16,512]{3,2,1,0:T(8,128)(2,1)S(1)}, u32[]{:S(2)}, u32[]{:S(2)}) %all-to-all-start) | async-done | bytes 2097184 | tf_op jit(solution)/shard_map/all_to_all | solution.py:71
  69.6 9.5 %all-to-all-start.2 = ((bf16[64,2,16,512]{3,2,1,0:T(8,128)(2,1)}), bf16[64,2,16,512]{3,2,1,0:T(8,128)(2,1)}, u32[]{:S(2)}, u32[]{:S(2)}) async-start(bf16[64,2,16,512]{3,2,1,0:T(8,128)(2,1)} %pad_maximum_fusion.2), calls=%async_computation.2 | async-start | bytes 4194304 | tf_op jit(solution)/shard_map/all_to_all | solution.py:71
  80.4 1.8 copy.101
  83.0 2.0 fusion.17
  86.5 2.1 stack.81
  88.6 2.5 copy.104
  91.1 2.8 %fusion.5 = bf16[4,256,512]{1,2,0:T(8,128)(2,1)S(1)} fusion(f32[4,512,256]{2,1,0:T(8,128)} %get-tuple-element.17, bf16[4,256,256]{2,1,0:T(8,128)(2,1)S(1)} %copy-done.16, bf16[4,256,512]{2,0,1:T(4,128)(2,1)S(1)} %bitcast.190), kind=kOutput, calls=%fused_computation.7 | convolution fusion | flops 273678336 | bytes 4718592 | tf_op jit(solution)/shard_map/dot_general | solution.py:22
  96.3 2.1 stack.82
  100.2 2.5 copy.106
  102.7 24.5 %all-to-all-done.2 = bf16[64,2,16,512]{3,2,1,0:T(8,128)(2,1)} async-done(((bf16[64,2,16,512]{3,2,1,0:T(8,128)(2,1)}), bf16[64,2,16,512]{3,2,1,0:T(8,128)(2,1)}, u32[]{:S(2)}, u32[]{:S(2)}) %all-to-all-start.2) | async-done | bytes 2097184 | tf_op jit(solution)/shard_map/all_to_all | solution.py:71
  127.2 10.2 %all-to-all-start.1 = ((bf16[64,2,16,512]{3,2,1,0:T(8,128)(2,1)}), bf16[64,2,16,512]{3,2,1,0:T(8,128)(2,1)}, u32[]{:S(2)}, u32[]{:S(2)}) async-start(bf16[64,2,16,512]{3,2,1,0:T(8,128)(2,1)} %copy.106), calls=%async_computation.1 | async-start | bytes 4194304 | tf_op jit(solution)/shard_map/all_to_all | solution.py:89
  137.5 2.8 %copy.110 = bf16[64,2,16,512]{3,0,2,1:T(8,128)(2,1)S(1)} copy(bf16[64,2,16,512]{3,2,1,0:T(8,128)(2,1)} %all-to-all-done.2) | data formatting | bytes 4194304 | tf_op jit(solution)/shard_map/all_to_all | solution.py:71
  142.1 1.7 fusion.13
  147.7 2.1 stack.86
  149.9 2.5 copy.119
  153.8 2.1 stack.85
  157.7 2.5 copy.120
  162.3 1.8 collective-permute-start.3
  164.1 21.5 %all-to-all-done.1 = bf16[64,2,16,512]{3,2,1,0:T(8,128)(2,1)} async-done(((bf16[64,2,16,512]{3,2,1,0:T(8,128)(2,1)}), bf16[64,2,16,512]{3,2,1,0:T(8,128)(2,1)}, u32[]{:S(2)}, u32[]{:S(2)}) %all-to-all-start.1) | async-done | bytes 2097184 | tf_op jit(solution)/shard_map/all_to_all | solution.py:89
  185.6 10.3 %all-to-all-start.3 = ((bf16[64,2,16,512]{3,2,1,0:T(8,128)(2,1)}), bf16[64,2,16,512]{3,2,1,0:T(8,128)(2,1)}, u32[]{:S(2)}, u32[]{:S(2)}) async-start(bf16[64,2,16,512]{3,2,1,0:T(8,128)(2,1)} %copy.120), calls=%async_computation.3 | async-start | bytes 4194304 | tf_op jit(solution)/shard_map/all_to_all | solution.py:89
  198.1 1.9 collective-permute-start.6
  202.2 10.0 %collective-permute-done.4 = bf16[2,256,256]{2,1,0:T(8,128)(2,1)S(1)} collective-permute-done((bf16[2,256,256]{2,1,0:T(8,128)(2,1)S(1)}, bf16[2,256,256]{2,1,0:T(8,128)(2,1)S(1)}, u32[]{:S(2)}, u32[]{:S(2)}) %collective-permute-start.4) | collective-permute-done | bytes 262176 | tf_op jit(solution)/shard_map/ppermute | solution.py:43
  213.5 9.0 %collective-permute-done.7 = bf16[2,256,256]{2,1,0:T(8,128)(2,1)S(1)} collective-permute-done((bf16[2,256,256]{2,1,0:T(8,128)(2,1)S(1)}, bf16[2,256,256]{2,1,0:T(8,128)(2,1)S(1)}, u32[]{:S(2)}, u32[]{:S(2)}) %collective-permute-start.7) | collective-permute-done | bytes 262176 | tf_op jit(solution)/shard_map/ppermute | solution.py:43
  227.0 1.8 fusion.63
  231.5 12.3 %all-to-all-done.3 = bf16[64,2,16,512]{3,2,1,0:T(8,128)(2,1)} async-done(((bf16[64,2,16,512]{3,2,1,0:T(8,128)(2,1)}), bf16[64,2,16,512]{3,2,1,0:T(8,128)(2,1)}, u32[]{:S(2)}, u32[]{:S(2)}) %all-to-all-start.3) | async-done | bytes 2097184 | tf_op jit(solution)/shard_map/all_to_all | solution.py:89
  243.8 1.8 fusion.64
  246.1 5.3 %collective-permute-start.9 = (bf16[1024,256]{0,1:T(8,128)(2,1)S(1)}, bf16[1024,256]{0,1:T(8,128)(2,1)S(1)}, u32[]{:S(2)}, u32[]{:S(2)}) collective-permute-start(bf16[1024,256]{0,1:T(8,128)(2,1)S(1)} %fusion.29), channel_id=1, source_target_pairs={{0,64},{64,0},{128,192},{192,128},{1,65},{65,1},{129,193},{193,129... | collective-permute-start | bytes 1572872 | tf_op jit(solution)/shard_map/ppermute | solution.py:39
  257.2 6.0 %collective-permute-done.10 = bf16[512,256]{1,0:T(8,128)(2,1)S(1)} collective-permute-done((bf16[512,256]{1,0:T(8,128)(2,1)S(1)}, bf16[512,256]{1,0:T(8,128)(2,1)S(1)}, u32[]{:S(2)}, u32[]{:S(2)}) %collective-permute-start.10) | collective-permute-done | bytes 262176 | tf_op jit(solution)/shard_map/ppermute | solution.py:43
  263.3 1.5 collective-permute-start.11
  265.7 3.2 %collective-permute-done.1 = bf16[128,1024]{1,0:T(8,128)(2,1)S(1)} collective-permute-done((bf16[128,1024]{1,0:T(8,128)(2,1)S(1)}, bf16[128,1024]{1,0:T(8,128)(2,1)S(1)}, u32[]{:S(2)}, u32[]{:S(2)}) %collective-permute-start.1) | collective-permute-done | bytes 262176 | tf_op jit(solution)/shard_map/ppermute | solution.py:43
  (127 shorter events, 49.5 us)
Async XLA Ops:
  0.6 82.4 %copy-start = (bf16[4,256,256]{2,1,0:T(8,128)(2,1)S(1)}, bf16[4,256,256]{2,1,0:T(8,128)(2,1)}, u32[]{:S(2)}) copy-start(bf16[4,256,256]{2,1,0:T(8,128)(2,1)} %param.9) | copy-start | bytes 1572868
  0.6 1.7 copy-start.19
  5.3 15.2 %copy-start.17 = (bf16[1,256,1024]{2,1,0:T(8,128)(2,1)S(1)}, bf16[1,256,1024]{2,1,0:T(8,128)(2,1)}, u32[]{:S(2)}) copy-start(bf16[1,256,1024]{2,1,0:T(8,128)(2,1)} %param.8) | copy-start | bytes 1572868
  5.3 64.2 %all-to-all-start = ((bf16[64,2,16,512]{3,2,1,0:T(8,128)(2,1)}), bf16[64,2,16,512]{3,2,1,0:T(8,128)(2,1)S(1)}, u32[]{:S(2)}, u32[]{:S(2)}) async-start(bf16[64,2,16,512]{3,2,1,0:T(8,128)(2,1)} %pad_maximum_fusion), calls=%async_computation | async-start | bytes 4194304 | tf_op jit(solution)/shard_map/all_to_all | solution.py:71
  69.6 57.7 %all-to-all-start.2 = ((bf16[64,2,16,512]{3,2,1,0:T(8,128)(2,1)}), bf16[64,2,16,512]{3,2,1,0:T(8,128)(2,1)}, u32[]{:S(2)}, u32[]{:S(2)}) async-start(bf16[64,2,16,512]{3,2,1,0:T(8,128)(2,1)} %pad_maximum_fusion.2), calls=%async_computation.2 | async-start | bytes 4194304 | tf_op jit(solution)/shard_map/all_to_all | solution.py:71
  83.0 2.0 copy-start.16
  88.6 2.5 copy-start.6
  127.2 58.4 %all-to-all-start.1 = ((bf16[64,2,16,512]{3,2,1,0:T(8,128)(2,1)}), bf16[64,2,16,512]{3,2,1,0:T(8,128)(2,1)}, u32[]{:S(2)}, u32[]{:S(2)}) async-start(bf16[64,2,16,512]{3,2,1,0:T(8,128)(2,1)} %copy.106), calls=%async_computation.1 | async-start | bytes 4194304 | tf_op jit(solution)/shard_map/all_to_all | solution.py:89
  141.3 2.5 copy-start.10
  149.9 2.5 copy-start.2
  157.7 2.5 copy-start.9
  162.3 33.6 %copy-start.7 = (bf16[4,64,4,512]{3,0,2,1:T(4,128)(2,1)S(1)}, bf16[4,64,4,512]{3,0,2,1:T(4,128)(2,1)}, u32[]{:S(2)}) copy-start(bf16[4,64,4,512]{3,0,2,1:T(4,128)(2,1)} %copy.101) | copy-start | bytes 3145732
  162.3 37.7 %collective-permute-start.3 = (bf16[4,256,256]{2,1,0:T(8,128)(2,1)S(1)}, bf16[4,256,256]{2,1,0:T(8,128)(2,1)S(1)}, u32[]{:S(2)}, u32[]{:S(2)}) collective-permute-start(bf16[4,256,256]{2,1,0:T(8,128)(2,1)S(1)} %fusion.30), channel_id=1, source_target_pairs={{0,64},{64,0},{128,192},{192,128},{1,65},{65,1},{129,193},{193,129... | collective-permute-start | bytes 1572872 | tf_op jit(solution)/shard_map/ppermute | solution.py:39
  185.6 58.2 %all-to-all-start.3 = ((bf16[64,2,16,512]{3,2,1,0:T(8,128)(2,1)}), bf16[64,2,16,512]{3,2,1,0:T(8,128)(2,1)}, u32[]{:S(2)}, u32[]{:S(2)}) async-start(bf16[64,2,16,512]{3,2,1,0:T(8,128)(2,1)} %copy.120), calls=%async_computation.3 | async-start | bytes 4194304 | tf_op jit(solution)/shard_map/all_to_all | solution.py:89
  198.1 3.4 %collective-permute-start.6 = (bf16[4,256,256]{2,1,0:T(8,128)(2,1)S(1)}, bf16[4,256,256]{2,1,0:T(8,128)(2,1)S(1)}, u32[]{:S(2)}, u32[]{:S(2)}) collective-permute-start(bf16[4,256,256]{2,1,0:T(8,128)(2,1)S(1)} %fusion.31), channel_id=1, source_target_pairs={{0,64},{64,0},{128,192},{192,128},{1,65},{65,1},{129,193},{193,129... | collective-permute-start | bytes 1572872 | tf_op jit(solution)/shard_map/ppermute | solution.py:39
  200.1 12.0 %collective-permute-start.4 = (bf16[2,256,256]{2,1,0:T(8,128)(2,1)S(1)}, bf16[2,256,256]{2,1,0:T(8,128)(2,1)S(1)}, u32[]{:S(2)}, u32[]{:S(2)}) collective-permute-start(bf16[2,256,256]{2,1,0:T(8,128)(2,1)S(1)} %dynamic-slice_bitcast_fusion.2), channel_id=1, source_target_pairs={{0,128},{64,192},{128,0},{192,64},{1,129},{65,193},{129,1},{193,65... | collective-permute-start | bytes 786440 | tf_op jit(solution)/shard_map/ppermute | solution.py:43
  201.7 20.8 %collective-permute-start.7 = (bf16[2,256,256]{2,1,0:T(8,128)(2,1)S(1)}, bf16[2,256,256]{2,1,0:T(8,128)(2,1)S(1)}, u32[]{:S(2)}, u32[]{:S(2)}) collective-permute-start(bf16[2,256,256]{2,1,0:T(8,128)(2,1)S(1)} %dynamic-slice_bitcast_fusion.1), channel_id=1, source_target_pairs={{0,128},{64,192},{128,0},{192,64},{1,129},{65,193},{129,1},{193,65... | collective-permute-start | bytes 786440 | tf_op jit(solution)/shard_map/ppermute | solution.py:43
  212.2 11.3 %collective-permute-start.5 = (bf16[2,256,256]{2,1,0:T(8,128)(2,1)S(1)}, bf16[2,256,256]{2,1,0:T(8,128)(2,1)S(1)}, u32[]{:S(2)}, u32[]{:S(2)}) collective-permute-start(bf16[2,256,256]{2,1,0:T(8,128)(2,1)S(1)} %add_convert_fusion.6), channel_id=1, source_target_pairs={{0,64},{64,0},{128,192},{192,128},{1,65},{65,1},{129,193},{193,129... | collective-permute-start | bytes 786440 | tf_op jit(solution)/shard_map/ppermute | solution.py:45
  222.6 2.1 collective-permute-start.8
  227.0 1.8 copy-start.21
  228.8 1.7 copy-start.22
  243.8 1.8 copy-start.23
  245.6 5.8 %copy-start.25 = (bf16[1024,256]{1,0:T(8,128)(2,1)S(1)}, bf16[1024,256]{1,0:T(8,128)(2,1)}, u32[]{:S(2)}) copy-start(bf16[1024,256]{1,0:T(8,128)(2,1)} %param.6) | copy-start | bytes 1572868
  246.1 8.8 %collective-permute-start.9 = (bf16[1024,256]{0,1:T(8,128)(2,1)S(1)}, bf16[1024,256]{0,1:T(8,128)(2,1)S(1)}, u32[]{:S(2)}, u32[]{:S(2)}) collective-permute-start(bf16[1024,256]{0,1:T(8,128)(2,1)S(1)} %fusion.29), channel_id=1, source_target_pairs={{0,64},{64,0},{128,192},{192,128},{1,65},{65,1},{129,193},{193,129... | collective-permute-start | bytes 1572872 | tf_op jit(solution)/shard_map/ppermute | solution.py:39
  251.9 2.1 copy-start.27
  253.1 2.7 collective-permute-start
  255.1 9.7 %copy-start.26 = (bf16[512,256]{1,0:T(8,128)(2,1)S(1)}, bf16[512,256]{1,0:T(8,128)(2,1)}, u32[]{:S(2)}) copy-start(bf16[512,256]{1,0:T(8,128)(2,1)} %convolution_convert_fusion.8) | copy-start | bytes 786436
  255.3 7.9 %collective-permute-start.10 = (bf16[512,256]{1,0:T(8,128)(2,1)S(1)}, bf16[512,256]{1,0:T(8,128)(2,1)S(1)}, u32[]{:S(2)}, u32[]{:S(2)}) collective-permute-start(bf16[512,256]{1,0:T(8,128)(2,1)S(1)} %dynamic-slice_bitcast_fusion), channel_id=1, source_target_pairs={{0,128},{64,192},{128,0},{192,64},{1,129},{65,193},{129,1},{193,65... | collective-permute-start | bytes 786440 | tf_op jit(solution)/shard_map/ppermute | solution.py:43
  256.1 12.8 %collective-permute-start.1 = (bf16[128,1024]{1,0:T(8,128)(2,1)S(1)}, bf16[128,1024]{1,0:T(8,128)(2,1)S(1)}, u32[]{:S(2)}, u32[]{:S(2)}) collective-permute-start(bf16[128,1024]{1,0:T(8,128)(2,1)S(1)} %dynamic-slice_bitcast_fusion.3), channel_id=1, source_target_pairs={{0,128},{64,192},{128,0},{192,64},{1,129},{65,193},{129,1},{193,65... | collective-permute-start | bytes 786440 | tf_op jit(solution)/shard_map/ppermute | solution.py:43
  263.3 6.6 %collective-permute-start.11 = (bf16[512,256]{1,0:T(8,128)(2,1)S(1)}, bf16[512,256]{1,0:T(8,128)(2,1)S(1)}, u32[]{:S(2)}, u32[]{:S(2)}) collective-permute-start(bf16[512,256]{1,0:T(8,128)(2,1)S(1)} %add_convert_fusion.4), channel_id=1, source_target_pairs={{0,64},{64,0},{128,192},{192,128},{1,65},{65,1},{129,193},{193,129... | collective-permute-start | bytes 786440 | tf_op jit(solution)/shard_map/ppermute | solution.py:45
  268.9 2.2 collective-permute-start.2
  270.0 2.2 copy-start.1
  (12 other events, 16.0 us)

commit v6 on v5

--- a/solution.py
+++ b/solution.py
@@ -93,21 +93,19 @@
         outs.append(dot(rows_t, dw, (0,), (0,)).astype(jnp.bfloat16))
         tgrads.append(dot(rows_grad_t, uw, (0,), (1,)).astype(jnp.bfloat16))
         g_dw = dot(rows_t, c, (1,), (0,))
-        g_uw = dot(x, rows_grad_t, (0,), (1,))
+        g_uw = dot(rows_grad_t, x, (1,), (0,))
         dwg = g_dw if dwg is None else dwg + g_dw
         uwg = g_uw if uwg is None else uwg + g_uw
 
-    dhg = dp_sum(dhg, grad_scale)
-    uhg = dp_sum(uhg, grad_scale)
-    dwg = dp_sum(dwg, grad_scale)
-    uwg = dp_sum(uwg, grad_scale)
+    hidden_grads = dp_sum(jnp.stack([dhg, uhg]), grad_scale)
+    width_grads = dp_sum(jnp.stack([dwg, uwg]), grad_scale)
     return (
         jnp.concatenate(outs, axis=0),
         jnp.concatenate(tgrads, axis=0),
-        uwg[None],
-        uhg,
-        dhg,
-        dwg[None],
+        width_grads[1].T[None],
+        hidden_grads[1],
+        hidden_grads[0],
+        width_grads[0][None],
     )
 
 

time: 273 us -> 278 us (1.018)
  waiting for transfers between devices: 133 us -> 147 us
  starting transfers between devices: 62.1 us -> 54.3 us
  local copies, waits for them, and re-layouts: 38.2 us -> 42.7 us
  other arithmetic: 10.6 us -> 6.83 us
    all_to_all x2, waiting for transfers between devices: 33.8 us -> 59.4 us  [shards(): recv2 = lax.all_to_all(send2, 'block', 0, 0, tiled=True)]
    ppermute x4 -> x2, waiting for transfers between devices: 28.1 us -> 11.6 us  [dp_sum(): got = lax.ppermute(mine, 'dp', row_swap)]
    convert_element_type x4 -> x2, other arithmetic: 4.32 us -> 0.38 us  [dp_sum(): return full.astype(jnp.float32).reshape(grad.shape)]
    ppermute x4 -> x2, starting transfers between devices: 4.84 us -> 1.3 us  [dp_sum(): got = lax.ppermute(total, 'dp', core_swap)]
    unnamed x56 -> x61, local copies, waits for them, and re-layouts: 4.1 us -> 7.56 us
    ppermute x4 -> x2, starting transfers between devices: 9.48 us -> 7.42 us  [dp_sum(): got = lax.ppermute(own, 'dp', core_swap)]
  transfers between devices with their start and end apart: 16 -> 10, of which waited for: 10 -> 7; matrix products, arithmetic and copies ran while one was open for 23% -> 22% of each run, Pallas kernels for 0% -> 0%
where the time goes in v6:
time: 278 us; the launch traced here: 277 us
  waiting for transfers between devices  147 us (53%)
  starting transfers between devices  54.3 us (20%)
  local copies, waits for them, and re-layouts  42.7 us (15%)
  matrix products  24.9 us (9%)
  other arithmetic  6.83 us (2%)
    all_to_all x2, waiting for transfers between devices, shards(): recv = lax.all_to_all(send, 'block', 0, 0, tiled=True)  71.8 us
    all_to_all x2, waiting for transfers between devices, shards(): recv2 = lax.all_to_all(send2, 'block', 0, 0, tiled=True)  59.4 us
    dot_general x24, matrix products, dot(): lax.dot_general(left, right, ((left_dims, right_dims), batch), preferred_...  24.9 us
    all_to_all x2, starting transfers between devices, shards(): recv = lax.all_to_all(send, 'block', 0, 0, tiled=True)  24.6 us
    all_to_all x2, starting transfers between devices, shards(): recv2 = lax.all_to_all(send2, 'block', 0, 0, tiled=True)  20.1 us
    another operation x8, local copies, waits for them, and re-layouts, shards(): jnp.stack([back_t, tile_grad_t], axis=0)  16.5 us
    ppermute x2, waiting for transfers between devices, dp_sum(): got = lax.ppermute(mine, 'dp', row_swap)  11.6 us
    unnamed x61, local copies, waits for them, and re-layouts  7.56 us
  transfers between devices with their start and end apart: 10, of which 7 were waited for; matrix products, arithmetic and copies ran while one was open for 22% of the time, Pallas kernels for 0%

profile of v6, /device:TPU:1, one launch (start us, length us, event | category | flops | bytes accessed | tf_op | source)
XLA Modules:
  0.0 276.9 jit_solution(1902074865386577386)
XLA Ops:
  0.7 1.7 convolution_convert_fusion.3
  5.3 15.1 %all-to-all-start = ((bf16[64,2,16,512]{3,2,1,0:T(8,128)(2,1)}), bf16[64,2,16,512]{3,2,1,0:T(8,128)(2,1)S(1)}, u32[]{:S(2)}, u32[]{:S(2)}) async-start(bf16[64,2,16,512]{3,2,1,0:T(8,128)(2,1)} %pad_maximum_fusion), calls=%async_computation | async-start | bytes 4194304 | tf_op jit(solution)/shard_map/all_to_all | solution.py:71
  20.4 1.6 convolution_convert_fusion.1
  25.0 44.4 %all-to-all-done = bf16[64,2,16,512]{3,2,1,0:T(8,128)(2,1)S(1)} async-done(((bf16[64,2,16,512]{3,2,1,0:T(8,128)(2,1)}), bf16[64,2,16,512]{3,2,1,0:T(8,128)(2,1)S(1)}, u32[]{:S(2)}, u32[]{:S(2)}) %all-to-all-start) | async-done | bytes 2097184 | tf_op jit(solution)/shard_map/all_to_all | solution.py:71
  69.4 9.5 %all-to-all-start.2 = ((bf16[64,2,16,512]{3,2,1,0:T(8,128)(2,1)}), bf16[64,2,16,512]{3,2,1,0:T(8,128)(2,1)}, u32[]{:S(2)}, u32[]{:S(2)}) async-start(bf16[64,2,16,512]{3,2,1,0:T(8,128)(2,1)} %pad_maximum_fusion.2), calls=%async_computation.2 | async-start | bytes 4194304 | tf_op jit(solution)/shard_map/all_to_all | solution.py:71
  83.3 1.5 fusion.5
  87.3 2.1 stack.72
  89.4 2.4 copy.100
  93.3 2.1 stack.71
  95.4 1.5 copy.99
  97.2 2.5 copy.101
  99.7 27.4 %all-to-all-done.2 = bf16[64,2,16,512]{3,2,1,0:T(8,128)(2,1)} async-done(((bf16[64,2,16,512]{3,2,1,0:T(8,128)(2,1)}), bf16[64,2,16,512]{3,2,1,0:T(8,128)(2,1)}, u32[]{:S(2)}, u32[]{:S(2)}) %all-to-all-start.2) | async-done | bytes 2097184 | tf_op jit(solution)/shard_map/all_to_all | solution.py:71
  127.1 10.0 %all-to-all-start.1 = ((bf16[64,2,16,512]{3,2,1,0:T(8,128)(2,1)}), bf16[64,2,16,512]{3,2,1,0:T(8,128)(2,1)}, u32[]{:S(2)}, u32[]{:S(2)}) async-start(bf16[64,2,16,512]{3,2,1,0:T(8,128)(2,1)} %copy.101), calls=%async_computation.1 | async-start | bytes 4194304 | tf_op jit(solution)/shard_map/all_to_all | solution.py:89
  137.1 2.8 copy.105
  141.7 1.7 fusion.15
  143.4 1.5 fusion.11
  147.4 2.1 stack.76
  149.5 2.5 copy.114
  153.5 2.1 stack.75
  155.6 1.5 copy.113
  157.4 2.5 copy.115
  159.9 25.4 %all-to-all-done.1 = bf16[64,2,16,512]{3,2,1,0:T(8,128)(2,1)} async-done(((bf16[64,2,16,512]{3,2,1,0:T(8,128)(2,1)}), bf16[64,2,16,512]{3,2,1,0:T(8,128)(2,1)}, u32[]{:S(2)}, u32[]{:S(2)}) %all-to-all-start.1) | async-done | bytes 2097184 | tf_op jit(solution)/shard_map/all_to_all | solution.py:89
  185.3 10.0 %all-to-all-start.3 = ((bf16[64,2,16,512]{3,2,1,0:T(8,128)(2,1)}), bf16[64,2,16,512]{3,2,1,0:T(8,128)(2,1)}, u32[]{:S(2)}, u32[]{:S(2)}) async-start(bf16[64,2,16,512]{3,2,1,0:T(8,128)(2,1)} %copy.115), calls=%async_computation.3 | async-start | bytes 4194304 | tf_op jit(solution)/shard_map/all_to_all | solution.py:89
  195.3 2.0 fusion.42
  200.8 2.1 collective-permute-start.3
  202.9 2.3 collective-permute-done.3
  205.8 1.7 fusion.62
  209.5 34.0 %all-to-all-done.3 = bf16[64,2,16,512]{3,2,1,0:T(8,128)(2,1)} async-done(((bf16[64,2,16,512]{3,2,1,0:T(8,128)(2,1)}), bf16[64,2,16,512]{3,2,1,0:T(8,128)(2,1)}, u32[]{:S(2)}, u32[]{:S(2)}) %all-to-all-start.3) | async-done | bytes 2097184 | tf_op jit(solution)/shard_map/all_to_all | solution.py:89
  243.5 1.7 fusion.63
  247.3 5.3 %collective-permute-start = (bf16[2,1024,256]{2,1,0:T(8,128)(2,1)S(1)}, bf16[2,1024,256]{2,1,0:T(8,128)(2,1)S(1)}, u32[]{:S(2)}, u32[]{:S(2)}) collective-permute-start(bf16[2,1024,256]{2,1,0:T(8,128)(2,1)S(1)} %fusion.12), channel_id=1, source_target_pairs={{0,64},{64,0},{128,192},{192,128},{1,65},{65,1},{129,193},{193,129... | collective-permute-start | bytes 3145736 | tf_op jit(solution)/shard_map/ppermute | solution.py:39
  253.9 1.9 collective-permute-done.5
  259.4 11.6 %collective-permute-done.1 = bf16[1,1024,256]{2,1,0:T(8,128)(2,1)S(1)} collective-permute-done((bf16[1,1024,256]{2,1,0:T(8,128)(2,1)S(1)}, bf16[1,1024,256]{2,1,0:T(8,128)(2,1)S(1)}, u32[]{:S(2)}, u32[]{:S(2)}) %collective-permute-start.1) | collective-permute-done | bytes 524320 | tf_op jit(solution)/shard_map/ppermute | solution.py:43
  (108 shorter events, 39.0 us)
Async XLA Ops:
  0.6 81.3 %copy-start = (bf16[4,256,256]{2,1,0:T(8,128)(2,1)S(1)}, bf16[4,256,256]{2,1,0:T(8,128)(2,1)}, u32[]{:S(2)}) copy-start(bf16[4,256,256]{2,1,0:T(8,128)(2,1)} %param.9) | copy-start | bytes 1572868
  0.6 1.7 copy-start.24
  5.3 64.1 %all-to-all-start = ((bf16[64,2,16,512]{3,2,1,0:T(8,128)(2,1)}), bf16[64,2,16,512]{3,2,1,0:T(8,128)(2,1)S(1)}, u32[]{:S(2)}, u32[]{:S(2)}) async-start(bf16[64,2,16,512]{3,2,1,0:T(8,128)(2,1)} %pad_maximum_fusion), calls=%async_computation | async-start | bytes 4194304 | tf_op jit(solution)/shard_map/all_to_all | solution.py:71
  69.4 57.7 %all-to-all-start.2 = ((bf16[64,2,16,512]{3,2,1,0:T(8,128)(2,1)}), bf16[64,2,16,512]{3,2,1,0:T(8,128)(2,1)}, u32[]{:S(2)}, u32[]{:S(2)}) async-start(bf16[64,2,16,512]{3,2,1,0:T(8,128)(2,1)} %pad_maximum_fusion.2), calls=%async_computation.2 | async-start | bytes 4194304 | tf_op jit(solution)/shard_map/all_to_all | solution.py:71
  81.9 1.4 copy-start.23
  95.4 1.5 copy-start.21
  127.1 58.2 %all-to-all-start.1 = ((bf16[64,2,16,512]{3,2,1,0:T(8,128)(2,1)}), bf16[64,2,16,512]{3,2,1,0:T(8,128)(2,1)}, u32[]{:S(2)}, u32[]{:S(2)}) async-start(bf16[64,2,16,512]{3,2,1,0:T(8,128)(2,1)} %copy.101), calls=%async_computation.1 | async-start | bytes 4194304 | tf_op jit(solution)/shard_map/all_to_all | solution.py:89
  140.9 2.5 copy-start.2
  141.7 1.7 copy-start.19
  149.5 2.5 copy-start.4
  155.6 1.5 copy-start.22
  185.3 58.2 %all-to-all-start.3 = ((bf16[64,2,16,512]{3,2,1,0:T(8,128)(2,1)}), bf16[64,2,16,512]{3,2,1,0:T(8,128)(2,1)}, u32[]{:S(2)}, u32[]{:S(2)}) async-start(bf16[64,2,16,512]{3,2,1,0:T(8,128)(2,1)} %copy.115), calls=%async_computation.3 | async-start | bytes 4194304 | tf_op jit(solution)/shard_map/all_to_all | solution.py:89
  195.3 2.0 copy-start.5
  195.3 2.0 copy-start.20
  198.6 1.5 copy-start.18
  200.8 4.4 %collective-permute-start.3 = (bf16[2,4,256,256]{3,2,1,0:T(8,128)(2,1)S(1)}, bf16[2,4,256,256]{3,2,1,0:T(8,128)(2,1)S(1)}, u32[]{:S(2)}, u32[]{:S(2)}) collective-permute-start(bf16[2,4,256,256]{3,2,1,0:T(8,128)(2,1)S(1)} %fusion.13), channel_id=1, source_target_pairs={{0,64},{64,0},{128,192},{192,128},{1,65},{65,1},{129,193},{193,129... | collective-permute-start | bytes 3145736 | tf_op jit(solution)/shard_map/ppermute | solution.py:39
  205.3 2.3 copy-start.27
  205.4 47.3 %collective-permute-start.4 = (bf16[1,4,256,256]{3,2,1,0:T(8,128)(2,1)S(1)}, bf16[1,4,256,256]{3,2,1,0:T(8,128)(2,1)}, u32[]{:S(2)}, u32[]{:S(2)}) collective-permute-start(bf16[1,4,256,256]{3,2,1,0:T(8,128)(2,1)S(1)} %add_convert_fusion.1), channel_id=1, source_target_pairs={{0,128},{64,192},{128,0},{192,64},{1,129},{65,193},{129,1},{193,65... | collective-permute-start | bytes 1572872 | tf_op jit(solution)/shard_map/ppermute | solution.py:43
  207.6 1.4 copy-start.28
  245.2 1.9 copy-start.9
  245.2 1.9 copy-start.11
  245.2 1.4 copy-start.29
  247.3 10.2 %collective-permute-start = (bf16[2,1024,256]{2,1,0:T(8,128)(2,1)S(1)}, bf16[2,1024,256]{2,1,0:T(8,128)(2,1)S(1)}, u32[]{:S(2)}, u32[]{:S(2)}) collective-permute-start(bf16[2,1024,256]{2,1,0:T(8,128)(2,1)S(1)} %fusion.12), channel_id=1, source_target_pairs={{0,64},{64,0},{128,192},{192,128},{1,65},{65,1},{129,193},{193,129... | collective-permute-start | bytes 3145736 | tf_op jit(solution)/shard_map/ppermute | solution.py:39
  253.8 2.0 collective-permute-start.5
  256.0 2.1 copy-start.16
  256.0 2.1 copy-start.25
  257.5 1.4 copy-start.26
  257.6 13.3 %collective-permute-start.1 = (bf16[1,1024,256]{2,1,0:T(8,128)(2,1)S(1)}, bf16[1,1024,256]{2,1,0:T(8,128)(2,1)S(1)}, u32[]{:S(2)}, u32[]{:S(2)}) collective-permute-start(bf16[1,1024,256]{2,1,0:T(8,128)(2,1)S(1)} %add_convert_fusion.3), channel_id=1, source_target_pairs={{0,128},{64,192},{128,0},{192,64},{1,129},{65,193},{129,1},{193,65... | collective-permute-start | bytes 1572872 | tf_op jit(solution)/shard_map/ppermute | solution.py:43
  258.9 13.4 %copy-start.12 = (bf16[64,1,16,512]{3,2,1,0:T(8,128)(2,1)S(1)}, bf16[64,1,16,512]{3,2,1,0:T(8,128)(2,1)}, u32[]{:S(2)}) copy-start(bf16[64,1,16,512]{3,2,1,0:T(8,128)(2,1)} %copy-done.11) | copy-start | bytes 3145732
  259.4 13.4 %copy-start.10 = (bf16[64,1,16,512]{3,2,1,0:T(8,128)(2,1)S(1)}, bf16[64,1,16,512]{3,2,1,0:T(8,128)(2,1)}, u32[]{:S(2)}) copy-start(bf16[64,1,16,512]{3,2,1,0:T(8,128)(2,1)} %copy-done.9) | copy-start | bytes 3145732
  271.1 3.2 %collective-permute-start.2 = (bf16[1,1024,256]{2,1,0:T(8,128)(2,1)S(1)}, bf16[1,1024,256]{2,1,0:T(8,128)(2,1)S(1)}, u32[]{:S(2)}, u32[]{:S(2)}) collective-permute-start(bf16[1,1024,256]{2,1,0:T(8,128)(2,1)S(1)} %add_convert_fusion.2), channel_id=1, source_target_pairs={{0,64},{64,0},{128,192},{192,128},{1,65},{65,1},{129,193},{193,129... | collective-permute-start | bytes 1572872 | tf_op jit(solution)/shard_map/ppermute | solution.py:45
  274.5 2.4 copy-start.1
  (8 other events, 9.1 us)

commit v7 on v5

--- a/solution.py
+++ b/solution.py
@@ -28,7 +28,7 @@
     return lax.dynamic_index_in_dim(pair, index, axis=0, keepdims=False)
 
 
-def dp_sum(grad, scale):
+def dp_sum(grad, scale, tied=None):
     size = lax.axis_size("dp")
     index = lax.axis_index("dp")
     core = index % 2
@@ -38,13 +38,15 @@
     own = (grad * scale).astype(jnp.bfloat16)
     got = lax.ppermute(own, "dp", core_swap)
     pair = (own.astype(jnp.float32) + got.astype(jnp.float32)).astype(jnp.bfloat16)
+    if tied is not None:
+        pair, tied = lax.optimization_barrier((pair, tied))
     pair = pair.reshape((2, grad.shape[0] // 2) + grad.shape[1:])
     mine = pick(pair, core)
     got = lax.ppermute(mine, "dp", row_swap)
     total = (mine.astype(jnp.float32) + got.astype(jnp.float32)).astype(jnp.bfloat16)
     got = lax.ppermute(total, "dp", core_swap)
     full = jnp.where(core == 0, jnp.stack([total, got]), jnp.stack([got, total]))
-    return full.astype(jnp.float32).reshape(grad.shape)
+    return full.astype(jnp.float32).reshape(grad.shape), tied
 
 
 def shards(tokens, cotangent, up_width, up_hidden, down_hidden, down_width):
@@ -85,22 +87,54 @@
         uhg = g_uh if uhg is None else uhg + g_uh
 
         send2 = jnp.stack([back_t, tile_grad_t], axis=0).reshape(2, local_blocks, nb, expand, rows)
-        send2 = send2.transpose(2, 0, 1, 3, 4).reshape(nb, 2, chunk, rows)
-        recv2 = lax.all_to_all(send2, "block", 0, 0, tiled=True)
-        rows_t = recv2[:, 0].reshape(nb * chunk, rows)
-        rows_grad_t = recv2[:, 1].reshape(nb * chunk, rows)
+        send2 = send2.transpose(2, 0, 1, 3, 4)
+        if step < CHUNKS - 1:
+            recv2 = lax.all_to_all(send2.reshape(nb, 2, chunk, rows), "block", 0, 0, tiled=True)
+            rows_t = recv2[:, 0].reshape(nb * chunk, rows)
+            rows_grad_t = recv2[:, 1].reshape(nb * chunk, rows)
+            outs.append(dot(rows_t, dw, (0,), (0,)).astype(jnp.bfloat16))
+            tgrads.append(dot(rows_grad_t, uw, (0,), (1,)).astype(jnp.bfloat16))
+            g_dw = dot(rows_t, c, (1,), (0,))
+            g_uw = dot(rows_grad_t, x, (1,), (0,))
+            dwg = g_dw if dwg is None else dwg + g_dw
+            uwg = g_uw if uwg is None else uwg + g_uw
+            continue
+        dw4 = dw.reshape(nb, local_blocks, expand, block_size)
+        uw4 = uw.reshape(block_size, nb, local_blocks, expand)
+        dwg4 = dwg.reshape(nb, local_blocks * expand, block_size)
+        uwg4 = uwg.reshape(nb, local_blocks * expand, block_size)
+        out_acc = tg_acc = None
+        width_parts = []
+        tail_payload = send2[:, :, local_blocks - 1:].reshape(nb, 2, expand, rows)
+        for lo, hi in ((0, local_blocks - 1), (local_blocks - 1, local_blocks)):
+            span = (hi - lo) * expand
+            payload = send2[:, :, lo:hi].reshape(nb, 2, span, rows) if lo == 0 else tail_payload
+            recv2 = lax.all_to_all(payload, "block", 0, 0, tiled=True)
+            rows_t = recv2[:, 0].reshape(nb * span, rows)
+            rows_grad_t = recv2[:, 1].reshape(nb * span, rows)
+            dw_p = dw4[:, lo:hi].reshape(nb * span, block_size)
+            uw_p = uw4[:, :, lo:hi].reshape(block_size, nb * span)
+            part_out = dot(rows_t, dw_p, (0,), (0,))
+            part_tg = dot(rows_grad_t, uw_p, (0,), (1,))
+            out_acc = part_out if out_acc is None else out_acc + part_out
+            tg_acc = part_tg if tg_acc is None else tg_acc + part_tg
+            g_dw = dot(rows_t, c, (1,), (0,)).reshape(nb, span, block_size)
+            g_uw = dot(rows_grad_t, x, (1,), (0,)).reshape(nb, span, block_size)
+            g_dw = g_dw + dwg4[:, lo * expand:hi * expand]
+            g_uw = g_uw + uwg4[:, lo * expand:hi * expand]
+            if lo == 0:
+                summed_part, tail_payload = dp_sum(jnp.stack([g_dw, g_uw]), grad_scale, tail_payload)
+            else:
+                summed_part = dp_sum(jnp.stack([g_dw, g_uw]), grad_scale)[0]
+            width_parts.append(summed_part)
+        outs.append(out_acc.astype(jnp.bfloat16))
+        tgrads.append(tg_acc.astype(jnp.bfloat16))
 
-        outs.append(dot(rows_t, dw, (0,), (0,)).astype(jnp.bfloat16))
-        tgrads.append(dot(rows_grad_t, uw, (0,), (1,)).astype(jnp.bfloat16))
-        g_dw = dot(rows_t, c, (1,), (0,))
-        g_uw = dot(x, rows_grad_t, (0,), (1,))
-        dwg = g_dw if dwg is None else dwg + g_dw
-        uwg = g_uw if uwg is None else uwg + g_uw
-
-    dhg = dp_sum(dhg, grad_scale)
-    uhg = dp_sum(uhg, grad_scale)
-    dwg = dp_sum(dwg, grad_scale)
-    uwg = dp_sum(uwg, grad_scale)
+    dhg = dp_sum(dhg, grad_scale)[0]
+    uhg = dp_sum(uhg, grad_scale)[0]
+    width = jnp.concatenate(width_parts, axis=2)
+    dwg = width[0].reshape(nb * chunk, block_size)
+    uwg = width[1].reshape(nb * chunk, block_size).T
     return (
         jnp.concatenate(outs, axis=0),
         jnp.concatenate(tgrads, axis=0),

time: 273 us -> 301 us (1.10); the launches traced: 272 us -> 296 us
  local copies, waits for them, and re-layouts: 38.2 us -> 66 us
  waiting for transfers between devices: 133 us -> 109 us
  other arithmetic: 10.6 us -> 17.3 us
  matrix products: 27.2 us -> 33.5 us
  starting transfers between devices: 62.1 us -> 68.1 us
    ppermute x4, waiting for transfers between devices: 28.1 us -> 4.03 us  [dp_sum(): got = lax.ppermute(mine, 'dp', row_swap)]
    slice x0 -> x12, local copies, waits for them, and re-layouts: none -> 15.8 us  [the longest x2 13 us: shards(): rows_grad_t = recv2[:, 1].reshape(nb * span, rows)]
    another operation x8 -> x6, local copies, waits for them, and re-layouts: 16.6 us -> 8.36 us  [shards(): jnp.stack([back_t, tile_grad_t], axis=0)]
    all_to_all x2 -> x3, starting transfers between devices: 20.5 us -> 26.9 us  [the longest x2 17.7 us: shards(): recv2 = lax.all_to_all(payload, 'block', 0, 0, tiled=True)]
    dot_general x24 -> x28, matrix products: 27.2 us -> 33.5 us  [dot(): lax.dot_general(left, right, ((left_dims, right_dims), batch), preferred_...]
    another operation x0 -> x4, local copies, waits for them, and re-layouts: none -> 5.52 us  [the longest x1 2.12 us: shards(): rows_t = recv2[:, 0].reshape(nb * span, rows)]
    unnamed x56 -> x86, local copies, waits for them, and re-layouts: 4.1 us -> 9.57 us
    reshape x3 -> x5, local copies, waits for them, and re-layouts: 5.25 us -> 9.63 us  [the longest x1 3.98 us: shards(): send2.reshape(nb, 2, chunk, rows)]
  transfers between devices with their start and end apart: 16 -> 17, of which waited for: 10 -> 7; matrix products, arithmetic and copies ran while one was open for 23% -> 33% of each run, Pallas kernels for 0% -> 0%
where the time goes in v7:
time: 301 us; the launch traced here: 296 us
  waiting for transfers between devices  109 us (36%)
  starting transfers between devices  68.1 us (23%)
  local copies, waits for them, and re-layouts  66 us (22%)
  matrix products  33.5 us (11%)
  other arithmetic  17.3 us (6%)
    all_to_all x2, waiting for transfers between devices, shards(): recv = lax.all_to_all(send, 'block', 0, 0, tiled=True)  73.2 us
    dot_general x28, matrix products, dot(): lax.dot_general(left, right, ((left_dims, right_dims), batch), preferred_...  33.5 us
    all_to_all x2, starting transfers between devices, shards(): recv = lax.all_to_all(send, 'block', 0, 0, tiled=True)  24.9 us
    all_to_all x2, starting transfers between devices, shards(): recv2 = lax.all_to_all(payload, 'block', 0, 0, tiled=True)  17.7 us
    all_to_all x1, waiting for transfers between devices, shards(): lax.all_to_all(send2.reshape(nb, 2, chunk, rows), 'block', 0, 0, tiled=True)  17.6 us
    all_to_all x2, waiting for transfers between devices, shards(): recv2 = lax.all_to_all(payload, 'block', 0, 0, tiled=True)  14.2 us
    slice x2, local copies, waits for them, and re-layouts, shards(): rows_grad_t = recv2[:, 1].reshape(nb * span, rows)  13 us
    ppermute x4, starting transfers between devices, dp_sum(): got = lax.ppermute(own, 'dp', core_swap)  11.1 us
  transfers between devices with their start and end apart: 17, of which 7 were waited for; matrix products, arithmetic and copies ran while one was open for 33% of the time, Pallas kernels for 0%

profile of v7, /device:TPU:1, one launch (start us, length us, event | category | flops | bytes accessed | tf_op | source)
XLA Modules:
  0.0 296.2 jit_solution(6834052295166159577)
XLA Ops:
  0.7 1.7 convolution_convert_fusion.1
  5.3 15.2 %all-to-all-start.2 = ((bf16[64,2,16,512]{3,2,1,0:T(8,128)(2,1)}), bf16[64,2,16,512]{3,2,1,0:T(8,128)(2,1)S(1)}, u32[]{:S(2)}, u32[]{:S(2)}) async-start(bf16[64,2,16,512]{3,2,1,0:T(8,128)(2,1)} %pad_maximum_fusion.1), calls=%async_computation.2 | async-start | bytes 4194304 | tf_op jit(solution)/shard_map/all_to_all | solution.py:73
  25.1 44.5 %all-to-all-done.2 = bf16[64,2,16,512]{3,2,1,0:T(8,128)(2,1)S(1)} async-done(((bf16[64,2,16,512]{3,2,1,0:T(8,128)(2,1)}), bf16[64,2,16,512]{3,2,1,0:T(8,128)(2,1)S(1)}, u32[]{:S(2)}, u32[]{:S(2)}) %all-to-all-start.2) | async-done | bytes 2097184 | tf_op jit(solution)/shard_map/all_to_all | solution.py:73
  69.5 9.7 %all-to-all-start = ((bf16[64,2,16,512]{3,2,1,0:T(8,128)(2,1)}), bf16[64,2,16,512]{3,2,1,0:T(8,128)(2,1)}, u32[]{:S(2)}, u32[]{:S(2)}) async-start(bf16[64,2,16,512]{3,2,1,0:T(8,128)(2,1)} %pad_maximum_fusion), calls=%async_computation | async-start | bytes 4194304 | tf_op jit(solution)/shard_map/all_to_all | solution.py:73
  95.9 2.9 copy.239
  98.8 28.7 %all-to-all-done = bf16[64,2,16,512]{3,2,1,0:T(8,128)(2,1)} async-done(((bf16[64,2,16,512]{3,2,1,0:T(8,128)(2,1)}), bf16[64,2,16,512]{3,2,1,0:T(8,128)(2,1)}, u32[]{:S(2)}, u32[]{:S(2)}) %all-to-all-start) | async-done | bytes 2097184 | tf_op jit(solution)/shard_map/all_to_all | solution.py:73
  127.5 10.1 %all-to-all-start.3 = ((bf16[64,2,12,512]{3,1,2,0:T(2,128)(2,1)}), bf16[64,2,12,512]{3,1,2,0:T(2,128)(2,1)S(1)}, u32[]{:S(2)}, u32[]{:S(2)}) async-start(bf16[64,2,12,512]{3,1,2,0:T(2,128)(2,1)} %copy.239), calls=%async_computation.3 | async-start | bytes 3145728 | tf_op jit(solution)/shard_map/all_to_all | solution.py:112
  137.6 2.8 copy.217
  140.6 1.8 copy.222
  143.2 2.0 fusion.17
  147.7 2.1 stack.91
  149.8 3.2 %fusion.5 = bf16[4,256,512]{1,2,0:T(8,128)(2,1)S(1)} fusion(f32[4,512,256]{2,1,0:T(8,128)} %get-tuple-element.57, bf16[4,256,256]{2,1,0:T(8,128)(2,1)} %param.10, bf16[4,256,512]{2,0,1:T(4,128)(2,1)} %bitcast.220), kind=kOutput, calls=%fused_computation.7 | convolution fusion | flops 273678336 | bytes 4718592 | tf_op jit(solution)/shard_map/dot_general | solution.py:22
  155.5 2.1 stack.92
  157.6 3.1 %maximum_bitcast_fusion = bf16[64,2,4,4,512]{4,3,0,2,1:T(4,128)(2,1)S(1)} fusion(bf16[1,4,64,4,512]{4,3,2,1,0:T(4,128)(2,1)} %stack.92, bf16[1,4,64,4,512]{4,3,2,1,0:T(4,128)(2,1)} %stack.91), kind=kLoop, calls=%fused_computation.15 | loop fusion | flops 1048576 | bytes 4194304 | tf_op jit(solution)/shard_map/transpose | solution.py:90
  160.7 2.5 copy.225
  163.3 4.0 %reshape.170 = bf16[64,2,16,512]{3,2,1,0:T(8,128)(2,1)} reshape(bf16[64,2,4,4,512]{4,3,2,1,0:T(4,128)(2,1)} %copy.225) | data formatting | bytes 4194304 | tf_op jit(solution)/shard_map/reshape | solution.py:92
  167.2 7.8 %all-to-all-done.3 = bf16[64,2,12,512]{3,1,2,0:T(2,128)(2,1)S(1)} async-done(((bf16[64,2,12,512]{3,1,2,0:T(2,128)(2,1)}), bf16[64,2,12,512]{3,1,2,0:T(2,128)(2,1)S(1)}, u32[]{:S(2)}, u32[]{:S(2)}) %all-to-all-start.3) | async-done | bytes 1572896 | tf_op jit(solution)/shard_map/all_to_all | solution.py:112
  175.1 9.2 %all-to-all-start.1 = ((bf16[64,2,16,512]{3,2,1,0:T(8,128)(2,1)}), bf16[64,2,16,512]{3,2,1,0:T(8,128)(2,1)}, u32[]{:S(2)}, u32[]{:S(2)}) async-start(bf16[64,2,16,512]{3,2,1,0:T(8,128)(2,1)} %reshape.170), calls=%async_computation.1 | async-start | bytes 4194304 | tf_op jit(solution)/shard_map/all_to_all | solution.py:92
  184.4 2.1 fusion.49
  187.8 2.2 collective-permute-start.6
  203.0 11.8 %slice_reduce_fusion = (bf16[64,12,512]{2,1,0:T(8,128)(2,1)}, bf16[64,12,512]{2,1,0:T(8,128)(2,1)}, bf16[64,1,12,512]{3,1,2,0:T(2,128)(2,1)}, bf16[64,1,12,512]{3,1,2,0:T(2,128)(2,1)}) fusion(bf16[64,2,12,512]{3,1,2,0:T(2,128)(2,1)S(1)} %all-to-all-done.3), kind=kLoop, calls=%fused_computation.139 | loop fusion | bytes 4718592 | tf_op jit(solution)/shard_map/slice | solution.py:114
  214.7 17.6 %all-to-all-done.1 = bf16[64,2,16,512]{3,2,1,0:T(8,128)(2,1)} async-done(((bf16[64,2,16,512]{3,2,1,0:T(8,128)(2,1)}), bf16[64,2,16,512]{3,2,1,0:T(8,128)(2,1)}, u32[]{:S(2)}, u32[]{:S(2)}) %all-to-all-start.1) | async-done | bytes 2097184 | tf_op jit(solution)/shard_map/all_to_all | solution.py:92
  232.3 3.2 %fusion.75 = (bf16[64,1,16,512]{3,2,1,0:T(8,128)(2,1)}, bf16[64,16,512]{2,1,0:T(8,128)(2,1)S(1)}, bf16[64,16,512]{2,1,0:T(8,128)(2,1)S(1)}, bf16[64,1,16,512]{3,2,1,0:T(8,128)(2,1)}) fusion(bf16[64,2,16,512]{3,2,1,0:T(8,128)(2,1)} %all-to-all-done.1), kind=kLoop, calls=%fused_computation.142 | loop fusion | bytes 6291456 | tf_op jit(solution)/shard_map/slice | solution.py:94
  239.5 4.9 %collective-permute-start = (bf16[2,64,12,256]{3,1,2,0:T(8,128)(2,1)S(1)}, bf16[2,64,12,256]{3,1,2,0:T(8,128)(2,1)S(1)}, u32[]{:S(2)}, u32[]{:S(2)}) collective-permute-start(bf16[2,64,12,256]{3,1,2,0:T(8,128)(2,1)S(1)} %fusion.20), channel_id=1, source_target_pairs={{0,64},{64,0},{128,192},{192,128},{1,65},{65,1},{129,193},{193,129... | collective-permute-start | bytes 2359304 | tf_op jit(solution)/shard_map/ppermute | solution.py:39
  253.0 7.6 %all-to-all-start.4 = ((bf16[64,2,4,512]{3,2,1,0:T(4,128)(2,1)}), bf16[64,2,4,512]{3,2,1,0:T(4,128)(2,1)}, u32[]{:S(2)}, u32[]{:S(2)}) async-start(bf16[64,2,4,512]{3,2,1,0:T(4,128)(2,1)} %copy.246), calls=%async_computation.4 | async-start | bytes 1048576 | tf_op jit(solution)/shard_map/all_to_all | solution.py:112
  261.7 2.1 reshape_squeeze.27
  263.8 2.1 reshape_squeeze.24
  267.9 1.7 convolution_convert_fusion.8
  271.9 6.3 %all-to-all-done.4 = bf16[64,2,4,512]{3,2,1,0:T(4,128)(2,1)} async-done(((bf16[64,2,4,512]{3,2,1,0:T(4,128)(2,1)}), bf16[64,2,4,512]{3,2,1,0:T(4,128)(2,1)}, u32[]{:S(2)}, u32[]{:S(2)}) %all-to-all-start.4) | async-done | bytes 524320 | tf_op jit(solution)/shard_map/all_to_all | solution.py:112
  280.3 3.4 %collective-permute-start.3 = (bf16[2,64,4,256]{3,1,2,0:T(8,128)(2,1)S(1)}, bf16[2,64,4,256]{3,1,2,0:T(8,128)(2,1)S(1)}, u32[]{:S(2)}, u32[]{:S(2)}) collective-permute-start(bf16[2,64,4,256]{3,1,2,0:T(8,128)(2,1)S(1)} %fusion.51), channel_id=1, source_target_pairs={{0,64},{64,0},{128,192},{192,128},{1,65},{65,1},{129,193},{193,129... | collective-permute-start | bytes 786440 | tf_op jit(solution)/shard_map/ppermute | solution.py:39
  285.6 4.0 %collective-permute-done.4 = bf16[1,64,4,256]{3,1,2,0:T(8,128)(2,1)S(1)} collective-permute-done((bf16[1,64,4,256]{3,1,2,0:T(8,128)(2,1)S(1)}, bf16[1,64,4,256]{3,1,2,0:T(8,128)(2,1)S(1)}, u32[]{:S(2)}, u32[]{:S(2)}) %collective-permute-start.4) | collective-permute-done | bytes 131104 | tf_op jit(solution)/shard_map/ppermute | solution.py:45
  292.4 1.6 copy.264
  (179 shorter events, 70.4 us)
Async XLA Ops:
  0.6 81.6 %copy-start = (bf16[4,256,256]{2,1,0:T(8,128)(2,1)S(1)}, bf16[4,256,256]{2,1,0:T(8,128)(2,1)}, u32[]{:S(2)}) copy-start(bf16[4,256,256]{2,1,0:T(8,128)(2,1)} %param.9) | copy-start | bytes 1572868
  5.3 15.2 %copy-start.8 = (bf16[1,256,1024]{2,1,0:T(8,128)(2,1)S(1)}, bf16[1,256,1024]{2,1,0:T(8,128)(2,1)}, u32[]{:S(2)}) copy-start(bf16[1,256,1024]{2,1,0:T(8,128)(2,1)} %param.8) | copy-start | bytes 1572868
  5.3 64.2 %all-to-all-start.2 = ((bf16[64,2,16,512]{3,2,1,0:T(8,128)(2,1)}), bf16[64,2,16,512]{3,2,1,0:T(8,128)(2,1)S(1)}, u32[]{:S(2)}, u32[]{:S(2)}) async-start(bf16[64,2,16,512]{3,2,1,0:T(8,128)(2,1)} %pad_maximum_fusion.1), calls=%async_computation.2 | async-start | bytes 4194304 | tf_op jit(solution)/shard_map/all_to_all | solution.py:73
  69.5 58.0 %all-to-all-start = ((bf16[64,2,16,512]{3,2,1,0:T(8,128)(2,1)}), bf16[64,2,16,512]{3,2,1,0:T(8,128)(2,1)}, u32[]{:S(2)}, u32[]{:S(2)}) async-start(bf16[64,2,16,512]{3,2,1,0:T(8,128)(2,1)} %pad_maximum_fusion), calls=%async_computation | async-start | bytes 4194304 | tf_op jit(solution)/shard_map/all_to_all | solution.py:73
  127.5 47.6 %all-to-all-start.3 = ((bf16[64,2,12,512]{3,1,2,0:T(2,128)(2,1)}), bf16[64,2,12,512]{3,1,2,0:T(2,128)(2,1)S(1)}, u32[]{:S(2)}, u32[]{:S(2)}) async-start(bf16[64,2,12,512]{3,1,2,0:T(2,128)(2,1)} %copy.239), calls=%async_computation.3 | async-start | bytes 3145728 | tf_op jit(solution)/shard_map/all_to_all | solution.py:112
  175.1 57.3 %all-to-all-start.1 = ((bf16[64,2,16,512]{3,2,1,0:T(8,128)(2,1)}), bf16[64,2,16,512]{3,2,1,0:T(8,128)(2,1)}, u32[]{:S(2)}, u32[]{:S(2)}) async-start(bf16[64,2,16,512]{3,2,1,0:T(8,128)(2,1)} %reshape.170), calls=%async_computation.1 | async-start | bytes 4194304 | tf_op jit(solution)/shard_map/all_to_all | solution.py:92
  187.8 9.1 %collective-permute-start.6 = (bf16[4,256,256]{2,1,0:T(8,128)(2,1)}, bf16[4,256,256]{2,1,0:T(8,128)(2,1)}, u32[]{:S(2)}, u32[]{:S(2)}) collective-permute-start(bf16[4,256,256]{2,1,0:T(8,128)(2,1)} %fusion.27), channel_id=1, source_target_pairs={{0,64},{64,0},{128,192},{192,128},{1,65},{65,1},{129,193},{193,129... | collective-permute-start | bytes 1572872 | tf_op jit(solution)/shard_map/ppermute | solution.py:39
  192.1 7.4 %collective-permute-start.9 = (bf16[4,256,256]{2,1,0:T(8,128)(2,1)}, bf16[4,256,256]{2,1,0:T(8,128)(2,1)}, u32[]{:S(2)}, u32[]{:S(2)}) collective-permute-start(bf16[4,256,256]{2,1,0:T(8,128)(2,1)} %fusion.28), channel_id=1, source_target_pairs={{0,64},{64,0},{128,192},{192,128},{1,65},{65,1},{129,193},{193,129... | collective-permute-start | bytes 1572872 | tf_op jit(solution)/shard_map/ppermute | solution.py:39
  199.1 45.3 %collective-permute-start.7 = (bf16[2,256,256]{2,1,0:T(8,128)(2,1)}, bf16[2,256,256]{2,1,0:T(8,128)(2,1)}, u32[]{:S(2)}, u32[]{:S(2)}) collective-permute-start(bf16[2,256,256]{2,1,0:T(8,128)(2,1)} %dynamic-slice_bitcast_fusion.1), channel_id=1, source_target_pairs={{0,128},{64,192},{128,0},{192,64},{1,129},{65,193},{129,1},{193,65... | collective-permute-start | bytes 786440 | tf_op jit(solution)/shard_map/ppermute | solution.py:45
  201.6 45.0 %collective-permute-start.10 = (bf16[2,256,256]{2,1,0:T(8,128)(2,1)S(1)}, bf16[2,256,256]{2,1,0:T(8,128)(2,1)}, u32[]{:S(2)}, u32[]{:S(2)}) collective-permute-start(bf16[2,256,256]{2,1,0:T(8,128)(2,1)S(1)} %dynamic-slice_bitcast_fusion), channel_id=1, source_target_pairs={{0,128},{64,192},{128,0},{192,64},{1,129},{65,193},{129,1},{193,65... | collective-permute-start | bytes 786440 | tf_op jit(solution)/shard_map/ppermute | solution.py:45
  214.7 20.8 %copy-start.22 = (bf16[1024,256]{1,0:T(8,128)(2,1)S(1)}, bf16[1024,256]{1,0:T(8,128)(2,1)}, u32[]{:S(2)}) copy-start(bf16[1024,256]{1,0:T(8,128)(2,1)} %param.7) | copy-start | bytes 1572868
  238.7 5.7 %copy-start.35 = (bf16[4,256,256]{2,1,0:T(8,128)(2,1)S(1)}, bf16[4,256,256]{2,1,0:T(8,128)(2,1)}, u32[]{:S(2)}) copy-start(bf16[4,256,256]{2,1,0:T(8,128)(2,1)} %copy-done.34) | copy-start | bytes 1572868
  239.3 7.4 %copy-start.33 = (bf16[4,256,256]{2,1,0:T(8,128)(2,1)S(1)}, bf16[4,256,256]{2,1,0:T(8,128)(2,1)}, u32[]{:S(2)}) copy-start(bf16[4,256,256]{2,1,0:T(8,128)(2,1)} %copy-done.32) | copy-start | bytes 1572868
  239.5 8.8 %collective-permute-start = (bf16[2,64,12,256]{3,1,2,0:T(8,128)(2,1)S(1)}, bf16[2,64,12,256]{3,1,2,0:T(8,128)(2,1)S(1)}, u32[]{:S(2)}, u32[]{:S(2)}) collective-permute-start(bf16[2,64,12,256]{3,1,2,0:T(8,128)(2,1)S(1)} %fusion.20), channel_id=1, source_target_pairs={{0,64},{64,0},{128,192},{192,128},{1,65},{65,1},{129,193},{193,129... | collective-permute-start | bytes 2359304 | tf_op jit(solution)/shard_map/ppermute | solution.py:39
  245.4 2.8 collective-permute-start.8
  247.7 4.0 %collective-permute-start.11 = (bf16[2,256,256]{2,1,0:T(8,128)(2,1)S(1)}, bf16[2,256,256]{2,1,0:T(8,128)(2,1)S(1)}, u32[]{:S(2)}, u32[]{:S(2)}) collective-permute-start(bf16[2,256,256]{2,1,0:T(8,128)(2,1)S(1)} %add_convert_fusion.4), channel_id=1, source_target_pairs={{0,64},{64,0},{128,192},{192,128},{1,65},{65,1},{129,193},{193,129... | collective-permute-start | bytes 786440 | tf_op jit(solution)/shard_map/ppermute | solution.py:47
  250.2 15.7 %collective-permute-start.1 = (bf16[1,64,12,256]{3,1,2,0:T(8,128)(2,1)}, bf16[1,64,12,256]{3,1,2,0:T(8,128)(2,1)S(1)}, u32[]{:S(2)}, u32[]{:S(2)}) collective-permute-start(bf16[1,64,12,256]{3,1,2,0:T(8,128)(2,1)} %constant_dynamic-slice_fusion), channel_id=1, source_target_pairs={{0,128},{64,192},{128,0},{192,64},{1,129},{65,193},{129,1},{193,65... | collective-permute-start | bytes 1179656 | tf_op jit(solution)/shard_map/ppermute | solution.py:45
  253.0 25.2 %all-to-all-start.4 = ((bf16[64,2,4,512]{3,2,1,0:T(4,128)(2,1)}), bf16[64,2,4,512]{3,2,1,0:T(4,128)(2,1)}, u32[]{:S(2)}, u32[]{:S(2)}) async-start(bf16[64,2,4,512]{3,2,1,0:T(4,128)(2,1)} %copy.246), calls=%async_computation.4 | async-start | bytes 1048576 | tf_op jit(solution)/shard_map/all_to_all | solution.py:112
  263.8 5.8 %copy-start.12 = (bf16[1,1024,256]{2,1,0:T(8,128)(2,1)S(1)}, bf16[1,1024,256]{2,1,0:T(8,128)(2,1)}, u32[]{:S(2)}) copy-start(bf16[1,1024,256]{2,1,0:T(8,128)(2,1)} %param.11) | copy-start | bytes 1572868
  267.1 3.7 %collective-permute-start.2 = (bf16[1,64,12,256]{3,1,2,0:T(8,128)(2,1)S(1)}, bf16[1,64,12,256]{3,1,2,0:T(8,128)(2,1)S(1)}, u32[]{:S(2)}, u32[]{:S(2)}) collective-permute-start(bf16[1,64,12,256]{3,1,2,0:T(8,128)(2,1)S(1)} %add_convert_fusion.3), channel_id=1, source_target_pairs={{0,64},{64,0},{128,192},{192,128},{1,65},{65,1},{129,193},{193,129... | collective-permute-start | bytes 1179656 | tf_op jit(solution)/shard_map/ppermute | solution.py:47
  269.6 9.7 %copy-start.23 = (bf16[1024,256]{1,0:T(8,128)(2,1)S(1)}, bf16[1024,256]{1,0:T(8,128)(2,1)}, u32[]{:S(2)}) copy-start(bf16[1024,256]{1,0:T(8,128)(2,1)} %param.7) | copy-start | bytes 1572868
  270.8 8.8 %copy-start.25 = (bf16[1024,256]{1,0:T(8,128)(2,1)S(1)}, bf16[1024,256]{1,0:T(8,128)(2,1)}, u32[]{:S(2)}) copy-start(bf16[1024,256]{1,0:T(8,128)(2,1)} %param.6) | copy-start | bytes 1572868
  270.8 9.1 %slice-start = ((bf16[256,64,4,4]{0,3,2,1:T(4,128)(2,1)}), bf16[256,64,1,4]{0,3,2,1:T(4,128)(2,1)S(1)}, s32[]{:S(2)}) async-start(bf16[256,64,4,4]{0,3,2,1:T(4,128)(2,1)} %copy-done.36), calls=%async_computation.5 | async-start | bytes 262144 | tf_op jit(solution)/shard_map/slice | solution.py:116
  279.6 4.3 %copy-start.27 = (bf16[768,512]{1,0:T(8,128)(2,1)S(1)}, bf16[768,512]{1,0:T(8,128)(2,1)}, u32[]{:S(2)}) copy-start(bf16[768,512]{1,0:T(8,128)(2,1)} %reshape_squeeze.27) | copy-start | bytes 2359300
  279.6 4.3 %copy-start.39 = (bf16[256,768]{0,1:T(8,128)(2,1)S(1)}, bf16[256,768]{0,1:T(8,128)(2,1)}, u32[]{:S(2)}) copy-start(bf16[256,768]{0,1:T(8,128)(2,1)} %reshape.179) | copy-start | bytes 1179652
  280.2 5.0 %copy-start.26 = (bf16[768,512]{1,0:T(8,128)(2,1)S(1)}, bf16[768,512]{1,0:T(8,128)(2,1)}, u32[]{:S(2)}) copy-start(bf16[768,512]{1,0:T(8,128)(2,1)} %reshape_squeeze.24) | copy-start | bytes 2359300
  280.2 5.0 %copy-start.38 = (bf16[768,256]{1,0:T(8,128)(2,1)S(1)}, bf16[768,256]{1,0:T(8,128)(2,1)}, u32[]{:S(2)}) copy-start(bf16[768,256]{1,0:T(8,128)(2,1)} %reshape.175) | copy-start | bytes 1179652
  280.3 4.6 %collective-permute-start.3 = (bf16[2,64,4,256]{3,1,2,0:T(8,128)(2,1)S(1)}, bf16[2,64,4,256]{3,1,2,0:T(8,128)(2,1)S(1)}, u32[]{:S(2)}, u32[]{:S(2)}) collective-permute-start(bf16[2,64,4,256]{3,1,2,0:T(8,128)(2,1)S(1)} %fusion.51), channel_id=1, source_target_pairs={{0,64},{64,0},{128,192},{192,128},{1,65},{65,1},{129,193},{193,129... | collective-permute-start | bytes 786440 | tf_op jit(solution)/shard_map/ppermute | solution.py:39
  284.0 7.0 %copy-start.41 = (bf16[512,256]{1,0:T(8,128)(2,1)S(1)}, bf16[512,256]{1,0:T(8,128)(2,1)}, u32[]{:S(2)}) copy-start(bf16[512,256]{1,0:T(8,128)(2,1)} %convolution_convert_fusion.9) | copy-start | bytes 786436
  284.9 7.2 %copy-start.28 = (bf16[2,64,12,256]{3,1,2,0:T(8,128)(2,1)S(1)}, bf16[2,64,12,256]{3,1,2,0:T(8,128)(2,1)}, u32[]{:S(2)}) copy-start(bf16[2,64,12,256]{3,1,2,0:T(8,128)(2,1)} %maximum_select_fusion) | copy-start | bytes 2359300
  284.9 4.8 %collective-permute-start.4 = (bf16[1,64,4,256]{3,1,2,0:T(8,128)(2,1)S(1)}, bf16[1,64,4,256]{3,1,2,0:T(8,128)(2,1)S(1)}, u32[]{:S(2)}, u32[]{:S(2)}) collective-permute-start(bf16[1,64,4,256]{3,1,2,0:T(8,128)(2,1)S(1)} %add_convert_fusion.7), channel_id=1, source_target_pairs={{0,128},{64,192},{128,0},{192,64},{1,129},{65,193},{129,1},{193,65... | collective-permute-start | bytes 393224 | tf_op jit(solution)/shard_map/ppermute | solution.py:45
  289.7 2.4 collective-permute-start.5
  (29 other events, 59.0 us)

commit v8 on v5

--- a/solution.py
+++ b/solution.py
@@ -97,8 +97,9 @@
         dwg = g_dw if dwg is None else dwg + g_dw
         uwg = g_uw if uwg is None else uwg + g_uw
 
-    dhg = dp_sum(dhg, grad_scale)
-    uhg = dp_sum(uhg, grad_scale)
+    hidden_grads = dp_sum(jnp.stack([dhg, uhg]), grad_scale)
+    dhg = hidden_grads[0]
+    uhg = hidden_grads[1]
     dwg = dp_sum(dwg, grad_scale)
     uwg = dp_sum(uwg, grad_scale)
     return (

time: 273 us -> 272 us (level)
  local copies, waits for them, and re-layouts: 38.2 us -> 33.3 us
  waiting for transfers between devices: 133 us -> 137 us
    another operation x8, local copies, waits for them, and re-layouts: 16.6 us -> 12.3 us  [shards(): jnp.stack([back_t, tile_grad_t], axis=0)]
    all_to_all x2, waiting for transfers between devices: 33.8 us -> 37.8 us  [shards(): recv2 = lax.all_to_all(send2, 'block', 0, 0, tiled=True)]
    ppermute x4 -> x3, starting transfers between devices: 9.48 us -> 7.1 us  [dp_sum(): got = lax.ppermute(own, 'dp', core_swap)]
    ppermute x4 -> x3, starting transfers between devices: 4.84 us -> 6.79 us  [dp_sum(): got = lax.ppermute(total, 'dp', core_swap)]
    ppermute x4 -> x3, waiting for transfers between devices: 28.1 us -> 28.8 us  [dp_sum(): got = lax.ppermute(mine, 'dp', row_swap)]
  transfers between devices with their start and end apart: 16 -> 13, of which waited for: 10 -> 8; matrix products, arithmetic and copies ran while one was open for 23% -> 23% of each run, Pallas kernels for 0% -> 0%
where the time goes in v8:
time: 272 us; the launch traced here: 271 us
  waiting for transfers between devices  137 us (50%)
  starting transfers between devices  60.9 us (22%)
  local copies, waits for them, and re-layouts  33.3 us (12%)
  matrix products  26.7 us (10%)
  other arithmetic  11.9 us (4%)
    all_to_all x2, waiting for transfers between devices, shards(): recv = lax.all_to_all(send, 'block', 0, 0, tiled=True)  68.9 us
    all_to_all x2, waiting for transfers between devices, shards(): recv2 = lax.all_to_all(send2, 'block', 0, 0, tiled=True)  37.8 us
    ppermute x3, waiting for transfers between devices, dp_sum(): got = lax.ppermute(mine, 'dp', row_swap)  28.8 us
    dot_general x24, matrix products, dot(): lax.dot_general(left, right, ((left_dims, right_dims), batch), preferred_...  26.7 us
    all_to_all x2, starting transfers between devices, shards(): recv = lax.all_to_all(send, 'block', 0, 0, tiled=True)  24.7 us
    all_to_all x2, starting transfers between devices, shards(): recv2 = lax.all_to_all(send2, 'block', 0, 0, tiled=True)  20.2 us
    another operation x8, local copies, waits for them, and re-layouts, shards(): jnp.stack([back_t, tile_grad_t], axis=0)  12.3 us
    ppermute x3, starting transfers between devices, dp_sum(): got = lax.ppermute(own, 'dp', core_swap)  7.1 us
  transfers between devices with their start and end apart: 13, of which 8 were waited for; matrix products, arithmetic and copies ran while one was open for 23% of the time, Pallas kernels for 0%

profile of v8, /device:TPU:1, one launch (start us, length us, event | category | flops | bytes accessed | tf_op | source)
XLA Modules:
  0.0 271.3 jit_solution(6529222211379466163)
XLA Ops:
  0.7 1.7 convolution_convert_fusion.3
  3.8 1.5 pad_maximum_fusion
  5.3 15.2 %all-to-all-start = ((bf16[64,2,16,512]{3,2,1,0:T(8,128)(2,1)}), bf16[64,2,16,512]{3,2,1,0:T(8,128)(2,1)S(1)}, u32[]{:S(2)}, u32[]{:S(2)}) async-start(bf16[64,2,16,512]{3,2,1,0:T(8,128)(2,1)} %pad_maximum_fusion), calls=%async_computation | async-start | bytes 4194304 | tf_op jit(solution)/shard_map/all_to_all | solution.py:71
  23.5 1.5 pad_maximum_fusion.2
  25.1 44.5 %all-to-all-done = bf16[64,2,16,512]{3,2,1,0:T(8,128)(2,1)S(1)} async-done(((bf16[64,2,16,512]{3,2,1,0:T(8,128)(2,1)}), bf16[64,2,16,512]{3,2,1,0:T(8,128)(2,1)S(1)}, u32[]{:S(2)}, u32[]{:S(2)}) %all-to-all-start) | async-done | bytes 2097184 | tf_op jit(solution)/shard_map/all_to_all | solution.py:71
  69.5 9.5 %all-to-all-start.2 = ((bf16[64,2,16,512]{3,2,1,0:T(8,128)(2,1)}), bf16[64,2,16,512]{3,2,1,0:T(8,128)(2,1)}, u32[]{:S(2)}, u32[]{:S(2)}) async-start(bf16[64,2,16,512]{3,2,1,0:T(8,128)(2,1)} %pad_maximum_fusion.2), calls=%async_computation.2 | async-start | bytes 4194304 | tf_op jit(solution)/shard_map/all_to_all | solution.py:71
  80.4 1.8 copy.101
  83.0 2.0 fusion.18
  86.5 2.1 stack.76
  88.6 2.5 copy.104
  91.1 2.8 %fusion.5 = bf16[4,256,512]{1,2,0:T(8,128)(2,1)S(1)} fusion(f32[4,512,256]{2,1,0:T(8,128)} %get-tuple-element.19, bf16[4,256,256]{2,1,0:T(8,128)(2,1)S(1)} %copy-done.9, bf16[4,256,512]{2,0,1:T(4,128)(2,1)S(1)} %bitcast.180), kind=kOutput, calls=%fused_computation.7 | convolution fusion | flops 273678336 | bytes 4718592 | tf_op jit(solution)/shard_map/dot_general | solution.py:22
  96.3 2.1 stack.77
  98.5 1.5 copy.105
  100.2 2.5 copy.106
  102.8 24.5 %all-to-all-done.2 = bf16[64,2,16,512]{3,2,1,0:T(8,128)(2,1)} async-done(((bf16[64,2,16,512]{3,2,1,0:T(8,128)(2,1)}), bf16[64,2,16,512]{3,2,1,0:T(8,128)(2,1)}, u32[]{:S(2)}, u32[]{:S(2)}) %all-to-all-start.2) | async-done | bytes 2097184 | tf_op jit(solution)/shard_map/all_to_all | solution.py:71
  127.2 10.2 %all-to-all-start.1 = ((bf16[64,2,16,512]{3,2,1,0:T(8,128)(2,1)}), bf16[64,2,16,512]{3,2,1,0:T(8,128)(2,1)}, u32[]{:S(2)}, u32[]{:S(2)}) async-start(bf16[64,2,16,512]{3,2,1,0:T(8,128)(2,1)} %copy.106), calls=%async_computation.1 | async-start | bytes 4194304 | tf_op jit(solution)/shard_map/all_to_all | solution.py:89
  137.4 2.8 %copy.110 = bf16[64,2,16,512]{3,0,2,1:T(8,128)(2,1)S(1)} copy(bf16[64,2,16,512]{3,2,1,0:T(8,128)(2,1)} %all-to-all-done.2) | data formatting | bytes 4194304 | tf_op jit(solution)/shard_map/all_to_all | solution.py:71
  145.4 1.6 fusion.11
  148.7 1.8 collective-permute-start.3
  152.5 2.4 copy.119
  156.6 2.5 copy.120
  159.1 26.5 %all-to-all-done.1 = bf16[64,2,16,512]{3,2,1,0:T(8,128)(2,1)} async-done(((bf16[64,2,16,512]{3,2,1,0:T(8,128)(2,1)}), bf16[64,2,16,512]{3,2,1,0:T(8,128)(2,1)}, u32[]{:S(2)}, u32[]{:S(2)}) %all-to-all-start.1) | async-done | bytes 2097184 | tf_op jit(solution)/shard_map/all_to_all | solution.py:89
  185.6 10.0 %all-to-all-start.3 = ((bf16[64,2,16,512]{3,2,1,0:T(8,128)(2,1)}), bf16[64,2,16,512]{3,2,1,0:T(8,128)(2,1)S(1)}, u32[]{:S(2)}, u32[]{:S(2)}) async-start(bf16[64,2,16,512]{3,2,1,0:T(8,128)(2,1)} %copy.120), calls=%async_computation.3 | async-start | bytes 4194304 | tf_op jit(solution)/shard_map/all_to_all | solution.py:89
  197.4 20.8 %collective-permute-done.4 = bf16[1,4,256,256]{3,2,1,0:T(8,128)(2,1)S(1)} collective-permute-done((bf16[1,4,256,256]{3,2,1,0:T(8,128)(2,1)S(1)}, bf16[1,4,256,256]{3,2,1,0:T(8,128)(2,1)S(1)}, u32[]{:S(2)}, u32[]{:S(2)}) %collective-permute-start.4) | collective-permute-done | bytes 524320 | tf_op jit(solution)/shard_map/ppermute | solution.py:43
  218.3 3.0 %collective-permute-start.5 = (bf16[1,4,256,256]{3,2,1,0:T(8,128)(2,1)S(1)}, bf16[1,4,256,256]{3,2,1,0:T(8,128)(2,1)}, u32[]{:S(2)}, u32[]{:S(2)}) collective-permute-start(bf16[1,4,256,256]{3,2,1,0:T(8,128)(2,1)S(1)} %add_convert_fusion.1), channel_id=1, source_target_pairs={{0,64},{64,0},{128,192},{192,128},{1,65},{65,1},{129,193},{193,129... | collective-permute-start | bytes 1572872 | tf_op jit(solution)/shard_map/ppermute | solution.py:45
  221.4 1.7 collective-permute-done.5
  225.9 1.8 fusion.63
  232.3 11.4 %all-to-all-done.3 = bf16[64,2,16,512]{3,2,1,0:T(8,128)(2,1)S(1)} async-done(((bf16[64,2,16,512]{3,2,1,0:T(8,128)(2,1)}), bf16[64,2,16,512]{3,2,1,0:T(8,128)(2,1)S(1)}, u32[]{:S(2)}, u32[]{:S(2)}) %all-to-all-start.3) | async-done | bytes 2097184 | tf_op jit(solution)/shard_map/all_to_all | solution.py:89
  245.5 5.3 %collective-permute-start.6 = (bf16[1024,256]{0,1:T(8,128)(2,1)S(1)}, bf16[1024,256]{0,1:T(8,128)(2,1)S(1)}, u32[]{:S(2)}, u32[]{:S(2)}) collective-permute-start(bf16[1024,256]{0,1:T(8,128)(2,1)S(1)} %fusion.30), channel_id=1, source_target_pairs={{0,64},{64,0},{128,192},{192,128},{1,65},{65,1},{129,193},{193,129... | collective-permute-start | bytes 1572872 | tf_op jit(solution)/shard_map/ppermute | solution.py:39
  256.3 5.6 %collective-permute-done.7 = bf16[512,256]{1,0:T(8,128)(2,1)S(1)} collective-permute-done((bf16[512,256]{1,0:T(8,128)(2,1)S(1)}, bf16[512,256]{1,0:T(8,128)(2,1)S(1)}, u32[]{:S(2)}, u32[]{:S(2)}) %collective-permute-start.7) | collective-permute-done | bytes 262176 | tf_op jit(solution)/shard_map/ppermute | solution.py:43
  261.9 2.3 collective-permute-start.8
  265.1 2.4 collective-permute-done.1
  (104 shorter events, 42.4 us)
Async XLA Ops:
  0.6 82.4 %copy-start = (bf16[4,256,256]{2,1,0:T(8,128)(2,1)S(1)}, bf16[4,256,256]{2,1,0:T(8,128)(2,1)}, u32[]{:S(2)}) copy-start(bf16[4,256,256]{2,1,0:T(8,128)(2,1)} %param.9) | copy-start | bytes 1572868
  0.6 1.7 copy-start.12
  5.3 15.2 %copy-start.10 = (bf16[1,256,1024]{2,1,0:T(8,128)(2,1)S(1)}, bf16[1,256,1024]{2,1,0:T(8,128)(2,1)}, u32[]{:S(2)}) copy-start(bf16[1,256,1024]{2,1,0:T(8,128)(2,1)} %param.8) | copy-start | bytes 1572868
  5.3 64.2 %all-to-all-start = ((bf16[64,2,16,512]{3,2,1,0:T(8,128)(2,1)}), bf16[64,2,16,512]{3,2,1,0:T(8,128)(2,1)S(1)}, u32[]{:S(2)}, u32[]{:S(2)}) async-start(bf16[64,2,16,512]{3,2,1,0:T(8,128)(2,1)} %pad_maximum_fusion), calls=%async_computation | async-start | bytes 4194304 | tf_op jit(solution)/shard_map/all_to_all | solution.py:71
  20.6 1.5 copy-start.13
  69.5 57.7 %all-to-all-start.2 = ((bf16[64,2,16,512]{3,2,1,0:T(8,128)(2,1)}), bf16[64,2,16,512]{3,2,1,0:T(8,128)(2,1)}, u32[]{:S(2)}, u32[]{:S(2)}) async-start(bf16[64,2,16,512]{3,2,1,0:T(8,128)(2,1)} %pad_maximum_fusion.2), calls=%async_computation.2 | async-start | bytes 4194304 | tf_op jit(solution)/shard_map/all_to_all | solution.py:71
  83.0 2.0 copy-start.9
  88.6 2.5 copy-start.1
  98.5 1.5 copy-start.7
  127.2 58.4 %all-to-all-start.1 = ((bf16[64,2,16,512]{3,2,1,0:T(8,128)(2,1)}), bf16[64,2,16,512]{3,2,1,0:T(8,128)(2,1)}, u32[]{:S(2)}, u32[]{:S(2)}) async-start(bf16[64,2,16,512]{3,2,1,0:T(8,128)(2,1)} %copy.106), calls=%async_computation.1 | async-start | bytes 4194304 | tf_op jit(solution)/shard_map/all_to_all | solution.py:89
  140.4 1.7 copy-start.2
  148.7 47.0 %collective-permute-start.3 = (bf16[2,4,256,256]{3,2,1,0:T(8,128)(2,1)}, bf16[2,4,256,256]{3,2,1,0:T(8,128)(2,1)}, u32[]{:S(2)}, u32[]{:S(2)}) collective-permute-start(bf16[2,4,256,256]{3,2,1,0:T(8,128)(2,1)} %fusion.12), channel_id=1, source_target_pairs={{0,64},{64,0},{128,192},{192,128},{1,65},{65,1},{129,193},{193,129... | collective-permute-start | bytes 3145736 | tf_op jit(solution)/shard_map/ppermute | solution.py:39
  155.2 1.2 copy-start.8
  185.6 58.1 %all-to-all-start.3 = ((bf16[64,2,16,512]{3,2,1,0:T(8,128)(2,1)}), bf16[64,2,16,512]{3,2,1,0:T(8,128)(2,1)S(1)}, u32[]{:S(2)}, u32[]{:S(2)}) async-start(bf16[64,2,16,512]{3,2,1,0:T(8,128)(2,1)} %copy.120), calls=%async_computation.3 | async-start | bytes 4194304 | tf_op jit(solution)/shard_map/all_to_all | solution.py:89
  197.0 21.3 %collective-permute-start.4 = (bf16[1,4,256,256]{3,2,1,0:T(8,128)(2,1)S(1)}, bf16[1,4,256,256]{3,2,1,0:T(8,128)(2,1)S(1)}, u32[]{:S(2)}, u32[]{:S(2)}) collective-permute-start(bf16[1,4,256,256]{3,2,1,0:T(8,128)(2,1)S(1)} %add_convert_fusion.2), channel_id=1, source_target_pairs={{0,128},{64,192},{128,0},{192,64},{1,129},{65,193},{129,1},{193,65... | collective-permute-start | bytes 1572872 | tf_op jit(solution)/shard_map/ppermute | solution.py:43
  218.3 4.7 %collective-permute-start.5 = (bf16[1,4,256,256]{3,2,1,0:T(8,128)(2,1)S(1)}, bf16[1,4,256,256]{3,2,1,0:T(8,128)(2,1)}, u32[]{:S(2)}, u32[]{:S(2)}) collective-permute-start(bf16[1,4,256,256]{3,2,1,0:T(8,128)(2,1)S(1)} %add_convert_fusion.1), channel_id=1, source_target_pairs={{0,64},{64,0},{128,192},{192,128},{1,65},{65,1},{129,193},{193,129... | collective-permute-start | bytes 1572872 | tf_op jit(solution)/shard_map/ppermute | solution.py:45
  225.9 1.8 copy-start.14
  227.7 1.2 copy-start.11
  227.7 1.7 copy-start.16
  228.9 2.0 copy-start.18
  243.7 1.4 copy-start.17
  243.9 7.0 %copy-start.5 = (f32[1024,256]{0,1:T(8,128)S(1)}, f32[1024,256]{0,1:T(8,128)}, u32[]{:S(2)}) copy-start(f32[1024,256]{0,1:T(8,128)} %fusion.60) | copy-start | bytes 3145732
  243.9 6.9 %copy-start.19 = (bf16[1024,256]{1,0:T(8,128)(2,1)S(1)}, bf16[1024,256]{1,0:T(8,128)(2,1)}, u32[]{:S(2)}) copy-start(bf16[1024,256]{1,0:T(8,128)(2,1)} %param.6) | copy-start | bytes 1572868
  245.5 8.4 %collective-permute-start.6 = (bf16[1024,256]{0,1:T(8,128)(2,1)S(1)}, bf16[1024,256]{0,1:T(8,128)(2,1)S(1)}, u32[]{:S(2)}, u32[]{:S(2)}) collective-permute-start(bf16[1024,256]{0,1:T(8,128)(2,1)S(1)} %fusion.30), channel_id=1, source_target_pairs={{0,64},{64,0},{128,192},{192,128},{1,65},{65,1},{129,193},{193,129... | collective-permute-start | bytes 1572872 | tf_op jit(solution)/shard_map/ppermute | solution.py:39
  250.8 1.8 copy-start.15
  251.3 1.7 copy-start.21
  252.6 2.3 collective-permute-start
  254.1 10.1 %copy-start.20 = (bf16[512,256]{1,0:T(8,128)(2,1)S(1)}, bf16[512,256]{1,0:T(8,128)(2,1)}, u32[]{:S(2)}) copy-start(bf16[512,256]{1,0:T(8,128)(2,1)} %convolution_convert_fusion.8) | copy-start | bytes 786436
  254.4 7.5 %collective-permute-start.7 = (bf16[512,256]{1,0:T(8,128)(2,1)S(1)}, bf16[512,256]{1,0:T(8,128)(2,1)S(1)}, u32[]{:S(2)}, u32[]{:S(2)}) collective-permute-start(bf16[512,256]{1,0:T(8,128)(2,1)S(1)} %dynamic-slice_bitcast_fusion), channel_id=1, source_target_pairs={{0,128},{64,192},{128,0},{192,64},{1,129},{65,193},{129,1},{193,65... | collective-permute-start | bytes 786440 | tf_op jit(solution)/shard_map/ppermute | solution.py:43
  255.1 12.4 %collective-permute-start.1 = (bf16[128,1024]{1,0:T(8,128)(2,1)S(1)}, bf16[128,1024]{1,0:T(8,128)(2,1)S(1)}, u32[]{:S(2)}, u32[]{:S(2)}) collective-permute-start(bf16[128,1024]{1,0:T(8,128)(2,1)S(1)} %dynamic-slice_bitcast_fusion.1), channel_id=1, source_target_pairs={{0,128},{64,192},{128,0},{192,64},{1,129},{65,193},{129,1},{193,65... | collective-permute-start | bytes 786440 | tf_op jit(solution)/shard_map/ppermute | solution.py:43
  261.9 7.0 %collective-permute-start.8 = (bf16[512,256]{1,0:T(8,128)(2,1)S(1)}, bf16[512,256]{1,0:T(8,128)(2,1)S(1)}, u32[]{:S(2)}, u32[]{:S(2)}) collective-permute-start(bf16[512,256]{1,0:T(8,128)(2,1)S(1)} %add_convert_fusion.4), channel_id=1, source_target_pairs={{0,64},{64,0},{128,192},{192,128},{1,65},{65,1},{129,193},{193,129... | collective-permute-start | bytes 786440 | tf_op jit(solution)/shard_map/ppermute | solution.py:45
  267.6 2.6 collective-permute-start.2
  (3 other events, 3.4 us)

commit v9 on v8

--- a/solution.py
+++ b/solution.py
@@ -28,7 +28,7 @@
     return lax.dynamic_index_in_dim(pair, index, axis=0, keepdims=False)
 
 
-def dp_sum(grad, scale):
+def dp_sum(grad, scale, tied=None):
     size = lax.axis_size("dp")
     index = lax.axis_index("dp")
     core = index % 2
@@ -40,11 +40,15 @@
     pair = (own.astype(jnp.float32) + got.astype(jnp.float32)).astype(jnp.bfloat16)
     pair = pair.reshape((2, grad.shape[0] // 2) + grad.shape[1:])
     mine = pick(pair, core)
+    if tied is not None:
+        mine, tied = lax.optimization_barrier((mine, tied))
     got = lax.ppermute(mine, "dp", row_swap)
     total = (mine.astype(jnp.float32) + got.astype(jnp.float32)).astype(jnp.bfloat16)
     got = lax.ppermute(total, "dp", core_swap)
-    full = jnp.where(core == 0, jnp.stack([total, got]), jnp.stack([got, total]))
-    return full.astype(jnp.float32).reshape(grad.shape)
+    full = jnp.zeros((2,) + total.shape, jnp.float32)
+    full = lax.dynamic_update_index_in_dim(full, total.astype(jnp.float32), core, 0)
+    full = lax.dynamic_update_index_in_dim(full, got.astype(jnp.float32), 1 - core, 0)
+    return full.reshape(grad.shape), tied
 
 
 def shards(tokens, cotangent, up_width, up_hidden, down_hidden, down_width):
@@ -90,18 +94,21 @@
         rows_t = recv2[:, 0].reshape(nb * chunk, rows)
         rows_grad_t = recv2[:, 1].reshape(nb * chunk, rows)
 
-        outs.append(dot(rows_t, dw, (0,), (0,)).astype(jnp.bfloat16))
-        tgrads.append(dot(rows_grad_t, uw, (0,), (1,)).astype(jnp.bfloat16))
+        if step < CHUNKS - 1:
+            outs.append(dot(rows_t, dw, (0,), (0,)).astype(jnp.bfloat16))
+            tgrads.append(dot(rows_grad_t, uw, (0,), (1,)).astype(jnp.bfloat16))
         g_dw = dot(rows_t, c, (1,), (0,))
         g_uw = dot(x, rows_grad_t, (0,), (1,))
         dwg = g_dw if dwg is None else dwg + g_dw
         uwg = g_uw if uwg is None else uwg + g_uw
 
-    hidden_grads = dp_sum(jnp.stack([dhg, uhg]), grad_scale)
+    hidden_grads = dp_sum(jnp.stack([dhg, uhg]), grad_scale)[0]
     dhg = hidden_grads[0]
     uhg = hidden_grads[1]
-    dwg = dp_sum(dwg, grad_scale)
-    uwg = dp_sum(uwg, grad_scale)
+    dwg, rows_t = dp_sum(dwg, grad_scale, rows_t)
+    uwg, rows_grad_t = dp_sum(uwg, grad_scale, rows_grad_t)
+    outs.append(dot(rows_t, dw, (0,), (0,)).astype(jnp.bfloat16))
+    tgrads.append(dot(rows_grad_t, uw, (0,), (1,)).astype(jnp.bfloat16))
     return (
         jnp.concatenate(outs, axis=0),
         jnp.concatenate(tgrads, axis=0),

time: 272 us -> 274 us (level)
  local copies, waits for them, and re-layouts: 33.3 us -> 41.1 us
  other arithmetic: 11.9 us -> 5.57 us
  matrix products: 26.7 us -> 32.3 us
  waiting for transfers between devices: 137 us -> 132 us
    all_to_all x2, waiting for transfers between devices: 37.8 us -> 29.8 us  [shards(): recv2 = lax.all_to_all(send2, 'block', 0, 0, tiled=True)]
    dot_general x24, matrix products: 26.7 us -> 32.3 us  [dot(): lax.dot_general(left, right, ((left_dims, right_dims), batch), preferred_...]
    another operation x8, local copies, waits for them, and re-layouts: 12.3 us -> 16.6 us  [shards(): jnp.stack([back_t, tile_grad_t], axis=0)]
    convert_element_type x6 -> x0, other arithmetic: 3.78 us -> none  [the longest x3 3.52 us: dp_sum(): return full.astype(jnp.float32).reshape(grad.shape)]
  transfers between devices with their start and end apart: 13 -> 13, of which waited for: 8 -> 10; matrix products, arithmetic and copies ran while one was open for 23% -> 25% of each run, Pallas kernels for 0% -> 0%
where the time goes in v9:
time: 274 us; the launch traced here: 273 us
  waiting for transfers between devices  132 us (48%)
  starting transfers between devices  60.8 us (22%)
  local copies, waits for them, and re-layouts  41.1 us (15%)
  matrix products  32.3 us (12%)
  other arithmetic  5.57 us (2%)
    all_to_all x2, waiting for transfers between devices, shards(): recv = lax.all_to_all(send, 'block', 0, 0, tiled=True)  68.9 us
    dot_general x24, matrix products, dot(): lax.dot_general(left, right, ((left_dims, right_dims), batch), preferred_...  32.3 us
    all_to_all x2, waiting for transfers between devices, shards(): recv2 = lax.all_to_all(send2, 'block', 0, 0, tiled=True)  29.8 us
    ppermute x3, waiting for transfers between devices, dp_sum(): got = lax.ppermute(mine, 'dp', row_swap)  29.2 us
    all_to_all x2, starting transfers between devices, shards(): recv = lax.all_to_all(send, 'block', 0, 0, tiled=True)  24.6 us
    all_to_all x2, starting transfers between devices, shards(): recv2 = lax.all_to_all(send2, 'block', 0, 0, tiled=True)  20.3 us
    another operation x8, local copies, waits for them, and re-layouts, shards(): jnp.stack([back_t, tile_grad_t], axis=0)  16.6 us
    ppermute x3, starting transfers between devices, dp_sum(): got = lax.ppermute(own, 'dp', core_swap)  8.67 us
  transfers between devices with their start and end apart: 13, of which 10 were waited for; matrix products, arithmetic and copies ran while one was open for 25% of the time, Pallas kernels for 0%

profile of v9, /device:TPU:1, one launch (start us, length us, event | category | flops | bytes accessed | tf_op | source)
XLA Modules:
  0.0 272.7 jit_solution(1988717509447401146)
XLA Ops:
  0.7 1.7 convolution_convert_fusion.3
  5.3 15.1 %all-to-all-start = ((bf16[64,2,16,512]{3,2,1,0:T(8,128)(2,1)}), bf16[64,2,16,512]{3,2,1,0:T(8,128)(2,1)S(1)}, u32[]{:S(2)}, u32[]{:S(2)}) async-start(bf16[64,2,16,512]{3,2,1,0:T(8,128)(2,1)} %pad_maximum_fusion), calls=%async_computation | async-start | bytes 4194304 | tf_op jit(solution)/shard_map/all_to_all | solution.py:75
  25.0 44.4 %all-to-all-done = bf16[64,2,16,512]{3,2,1,0:T(8,128)(2,1)S(1)} async-done(((bf16[64,2,16,512]{3,2,1,0:T(8,128)(2,1)}), bf16[64,2,16,512]{3,2,1,0:T(8,128)(2,1)S(1)}, u32[]{:S(2)}, u32[]{:S(2)}) %all-to-all-start) | async-done | bytes 2097184 | tf_op jit(solution)/shard_map/all_to_all | solution.py:75
  69.4 9.5 %all-to-all-start.2 = ((bf16[64,2,16,512]{3,2,1,0:T(8,128)(2,1)}), bf16[64,2,16,512]{3,2,1,0:T(8,128)(2,1)}, u32[]{:S(2)}, u32[]{:S(2)}) async-start(bf16[64,2,16,512]{3,2,1,0:T(8,128)(2,1)} %pad_maximum_fusion.2), calls=%async_computation.2 | async-start | bytes 4194304 | tf_op jit(solution)/shard_map/all_to_all | solution.py:75
  80.3 1.8 copy.101
  82.9 2.0 fusion.18
  86.4 2.1 stack.34
  88.5 2.5 copy.104
  91.0 2.8 %fusion.5 = bf16[4,256,512]{1,2,0:T(8,128)(2,1)S(1)} fusion(f32[4,512,256]{2,1,0:T(8,128)} %get-tuple-element.31, bf16[4,256,256]{2,1,0:T(8,128)(2,1)S(1)} %copy-done.19, bf16[4,256,512]{2,0,1:T(4,128)(2,1)S(1)} %bitcast.176), kind=kOutput, calls=%fused_computation.7 | convolution fusion | flops 273678336 | bytes 4718592 | tf_op jit(solution)/shard_map/dot_general | solution.py:22
  96.2 2.1 stack.35
  100.1 2.5 copy.106
  102.6 24.5 %all-to-all-done.2 = bf16[64,2,16,512]{3,2,1,0:T(8,128)(2,1)} async-done(((bf16[64,2,16,512]{3,2,1,0:T(8,128)(2,1)}), bf16[64,2,16,512]{3,2,1,0:T(8,128)(2,1)}, u32[]{:S(2)}, u32[]{:S(2)}) %all-to-all-start.2) | async-done | bytes 2097184 | tf_op jit(solution)/shard_map/all_to_all | solution.py:75
  127.1 10.2 %all-to-all-start.1 = ((bf16[64,2,16,512]{3,2,1,0:T(8,128)(2,1)}), bf16[64,2,16,512]{3,2,1,0:T(8,128)(2,1)}, u32[]{:S(2)}, u32[]{:S(2)}) async-start(bf16[64,2,16,512]{3,2,1,0:T(8,128)(2,1)} %copy.106), calls=%async_computation.1 | async-start | bytes 4194304 | tf_op jit(solution)/shard_map/all_to_all | solution.py:93
  137.3 2.8 %copy.110 = bf16[64,2,16,512]{3,0,2,1:T(8,128)(2,1)S(1)} copy(bf16[64,2,16,512]{3,2,1,0:T(8,128)(2,1)} %all-to-all-done.2) | data formatting | bytes 4194304 | tf_op jit(solution)/shard_map/all_to_all | solution.py:75
  142.0 1.7 fusion.14
  147.6 2.1 stack.39
  149.8 2.5 copy.119
  153.7 2.1 stack.38
  157.6 2.5 copy.120
  164.5 21.0 %all-to-all-done.1 = bf16[64,2,16,512]{3,2,1,0:T(8,128)(2,1)} async-done(((bf16[64,2,16,512]{3,2,1,0:T(8,128)(2,1)}), bf16[64,2,16,512]{3,2,1,0:T(8,128)(2,1)}, u32[]{:S(2)}, u32[]{:S(2)}) %all-to-all-start.1) | async-done | bytes 2097184 | tf_op jit(solution)/shard_map/all_to_all | solution.py:93
  185.5 10.0 %all-to-all-start.3 = ((bf16[64,2,16,512]{3,2,1,0:T(8,128)(2,1)}), bf16[64,2,16,512]{3,2,1,0:T(8,128)(2,1)}, u32[]{:S(2)}, u32[]{:S(2)}) async-start(bf16[64,2,16,512]{3,2,1,0:T(8,128)(2,1)} %copy.120), calls=%async_computation.3 | async-start | bytes 4194304 | tf_op jit(solution)/shard_map/all_to_all | solution.py:93
  195.5 2.1 fusion.22
  197.9 2.1 collective-permute-start.4
  200.0 2.3 collective-permute-done.4
  202.9 21.0 %collective-permute-done.5 = bf16[1,4,256,256]{3,2,1,0:T(8,128)(2,1)S(1)} collective-permute-done((bf16[1,4,256,256]{3,2,1,0:T(8,128)(2,1)S(1)}, bf16[1,4,256,256]{3,2,1,0:T(8,128)(2,1)S(1)}, u32[]{:S(2)}, u32[]{:S(2)}) %collective-permute-start.5) | collective-permute-done | bytes 524320 | tf_op jit(solution)/shard_map/ppermute | solution.py:45
  224.3 2.8 %collective-permute-start.6 = (bf16[1,4,256,256]{3,2,1,0:T(8,128)(2,1)S(1)}, bf16[1,4,256,256]{3,2,1,0:T(8,128)(2,1)S(1)}, u32[]{:S(2)}, u32[]{:S(2)}) collective-permute-start(bf16[1,4,256,256]{3,2,1,0:T(8,128)(2,1)S(1)} %get-tuple-element.17), channel_id=1, source_target_pairs={{0,64},{64,0},{128,192},{192,128},{1,65},{65,1},{129,193},{193,129... | collective-permute-start | bytes 1572872 | tf_op jit(solution)/shard_map/ppermute | solution.py:47
  230.2 1.8 fusion.63
  234.9 8.8 %all-to-all-done.3 = bf16[64,2,16,512]{3,2,1,0:T(8,128)(2,1)} async-done(((bf16[64,2,16,512]{3,2,1,0:T(8,128)(2,1)}), bf16[64,2,16,512]{3,2,1,0:T(8,128)(2,1)}, u32[]{:S(2)}, u32[]{:S(2)}) %all-to-all-start.3) | async-done | bytes 2097184 | tf_op jit(solution)/shard_map/all_to_all | solution.py:93
  243.7 1.8 fusion.62
  246.0 5.3 %collective-permute-start = (bf16[1024,256]{1,0:T(8,128)(2,1)S(1)}, bf16[1024,256]{1,0:T(8,128)(2,1)S(1)}, u32[]{:S(2)}, u32[]{:S(2)}) collective-permute-start(bf16[1024,256]{1,0:T(8,128)(2,1)S(1)} %fusion.29), channel_id=1, source_target_pairs={{0,64},{64,0},{128,192},{192,128},{1,65},{65,1},{129,193},{193,129... | collective-permute-start | bytes 1572872 | tf_op jit(solution)/shard_map/ppermute | solution.py:39
  259.3 4.2 %collective-permute-done.7 = bf16[512,256]{1,0:T(8,128)(2,1)S(1)} collective-permute-done((bf16[512,256]{1,0:T(8,128)(2,1)S(1)}, bf16[512,256]{1,0:T(8,128)(2,1)S(1)}, u32[]{:S(2)}, u32[]{:S(2)}) %collective-permute-start.7) | collective-permute-done | bytes 262176 | tf_op jit(solution)/shard_map/ppermute | solution.py:45
  265.1 4.0 %collective-permute-done.2 = bf16[128,1024]{1,0:T(8,128)(2,1)S(1)} collective-permute-done((bf16[128,1024]{1,0:T(8,128)(2,1)S(1)}, bf16[128,1024]{1,0:T(8,128)(2,1)S(1)}, u32[]{:S(2)}, u32[]{:S(2)}) %collective-permute-start.2) | collective-permute-done | bytes 262176 | tf_op jit(solution)/shard_map/ppermute | solution.py:45
  (122 shorter events, 49.3 us)
Async XLA Ops:
  0.6 82.3 %copy-start = (bf16[4,256,256]{2,1,0:T(8,128)(2,1)S(1)}, bf16[4,256,256]{2,1,0:T(8,128)(2,1)}, u32[]{:S(2)}) copy-start(bf16[4,256,256]{2,1,0:T(8,128)(2,1)} %param.9) | copy-start | bytes 1572868
  0.6 1.7 copy-start.20
  5.3 64.1 %all-to-all-start = ((bf16[64,2,16,512]{3,2,1,0:T(8,128)(2,1)}), bf16[64,2,16,512]{3,2,1,0:T(8,128)(2,1)S(1)}, u32[]{:S(2)}, u32[]{:S(2)}) async-start(bf16[64,2,16,512]{3,2,1,0:T(8,128)(2,1)} %pad_maximum_fusion), calls=%async_computation | async-start | bytes 4194304 | tf_op jit(solution)/shard_map/all_to_all | solution.py:75
  69.4 57.7 %all-to-all-start.2 = ((bf16[64,2,16,512]{3,2,1,0:T(8,128)(2,1)}), bf16[64,2,16,512]{3,2,1,0:T(8,128)(2,1)}, u32[]{:S(2)}, u32[]{:S(2)}) async-start(bf16[64,2,16,512]{3,2,1,0:T(8,128)(2,1)} %pad_maximum_fusion.2), calls=%async_computation.2 | async-start | bytes 4194304 | tf_op jit(solution)/shard_map/all_to_all | solution.py:75
  82.9 2.0 copy-start.19
  88.5 2.5 copy-start.6
  127.1 58.4 %all-to-all-start.1 = ((bf16[64,2,16,512]{3,2,1,0:T(8,128)(2,1)}), bf16[64,2,16,512]{3,2,1,0:T(8,128)(2,1)}, u32[]{:S(2)}, u32[]{:S(2)}) async-start(bf16[64,2,16,512]{3,2,1,0:T(8,128)(2,1)} %copy.106), calls=%async_computation.1 | async-start | bytes 4194304 | tf_op jit(solution)/shard_map/all_to_all | solution.py:93
  141.1 2.5 copy-start.10
  149.7 2.5 copy-start.2
  157.6 2.5 copy-start.9
  164.5 31.1 %copy-start.3 = (bf16[4,256,512]{1,2,0:T(8,128)(2,1)S(1)}, bf16[4,256,512]{1,2,0:T(8,128)(2,1)}, u32[]{:S(2)}) copy-start(bf16[4,256,512]{1,2,0:T(8,128)(2,1)} %get-tuple-element.32) | copy-start | bytes 3145732
  185.5 58.2 %all-to-all-start.3 = ((bf16[64,2,16,512]{3,2,1,0:T(8,128)(2,1)}), bf16[64,2,16,512]{3,2,1,0:T(8,128)(2,1)}, u32[]{:S(2)}, u32[]{:S(2)}) async-start(bf16[64,2,16,512]{3,2,1,0:T(8,128)(2,1)} %copy.120), calls=%async_computation.3 | async-start | bytes 4194304 | tf_op jit(solution)/shard_map/all_to_all | solution.py:93
  197.9 4.4 %collective-permute-start.4 = (bf16[2,4,256,256]{3,2,1,0:T(8,128)(2,1)S(1)}, bf16[2,4,256,256]{3,2,1,0:T(8,128)(2,1)S(1)}, u32[]{:S(2)}, u32[]{:S(2)}) collective-permute-start(bf16[2,4,256,256]{3,2,1,0:T(8,128)(2,1)S(1)} %fusion.12), channel_id=1, source_target_pairs={{0,64},{64,0},{128,192},{192,128},{1,65},{65,1},{129,193},{193,129... | collective-permute-start | bytes 3145736 | tf_op jit(solution)/shard_map/ppermute | solution.py:39
  202.5 21.5 %collective-permute-start.5 = (bf16[1,4,256,256]{3,2,1,0:T(8,128)(2,1)S(1)}, bf16[1,4,256,256]{3,2,1,0:T(8,128)(2,1)S(1)}, u32[]{:S(2)}, u32[]{:S(2)}) collective-permute-start(bf16[1,4,256,256]{3,2,1,0:T(8,128)(2,1)S(1)} %add_convert_fusion.1), channel_id=1, source_target_pairs={{0,128},{64,192},{128,0},{192,64},{1,129},{65,193},{129,1},{193,65... | collective-permute-start | bytes 1572872 | tf_op jit(solution)/shard_map/ppermute | solution.py:45
  224.3 4.3 %collective-permute-start.6 = (bf16[1,4,256,256]{3,2,1,0:T(8,128)(2,1)S(1)}, bf16[1,4,256,256]{3,2,1,0:T(8,128)(2,1)S(1)}, u32[]{:S(2)}, u32[]{:S(2)}) collective-permute-start(bf16[1,4,256,256]{3,2,1,0:T(8,128)(2,1)S(1)} %get-tuple-element.17), channel_id=1, source_target_pairs={{0,64},{64,0},{128,192},{192,128},{1,65},{65,1},{129,193},{193,129... | collective-permute-start | bytes 1572872 | tf_op jit(solution)/shard_map/ppermute | solution.py:47
  230.2 1.8 copy-start.23
  243.7 1.9 copy-start.14
  245.5 6.2 %copy-start.17 = (bf16[64,1,16,512]{3,2,1,0:T(8,128)(2,1)}, bf16[64,1,16,512]{3,2,1,0:T(8,128)(2,1)S(1)}, u32[]{:S(2)}) copy-start(bf16[64,1,16,512]{3,2,1,0:T(8,128)(2,1)S(1)} %get-tuple-element.22) | copy-start | bytes 3145732
  245.5 5.8 %copy-start.13 = (f32[1024,256]{1,0:T(8,128)S(1)}, f32[1024,256]{1,0:T(8,128)}, u32[]{:S(2)}) copy-start(f32[1024,256]{1,0:T(8,128)} %fusion.59) | copy-start | bytes 3145732
  245.5 5.8 %copy-start.25 = (bf16[1024,256]{1,0:T(8,128)(2,1)S(1)}, bf16[1024,256]{1,0:T(8,128)(2,1)}, u32[]{:S(2)}) copy-start(bf16[1024,256]{1,0:T(8,128)(2,1)} %param.6) | copy-start | bytes 1572868
  246.0 7.0 %copy-start.21 = (bf16[1,1024,256]{2,1,0:T(8,128)(2,1)S(1)}, bf16[1,1024,256]{2,1,0:T(8,128)(2,1)}, u32[]{:S(2)}) copy-start(bf16[1,1024,256]{2,1,0:T(8,128)(2,1)} %param.11) | copy-start | bytes 1572868
  246.0 9.4 %collective-permute-start = (bf16[1024,256]{1,0:T(8,128)(2,1)S(1)}, bf16[1024,256]{1,0:T(8,128)(2,1)S(1)}, u32[]{:S(2)}, u32[]{:S(2)}) collective-permute-start(bf16[1024,256]{1,0:T(8,128)(2,1)S(1)} %fusion.29), channel_id=1, source_target_pairs={{0,64},{64,0},{128,192},{192,128},{1,65},{65,1},{129,193},{193,129... | collective-permute-start | bytes 1572872 | tf_op jit(solution)/shard_map/ppermute | solution.py:39
  251.3 2.9 %copy-start.22 = (bf16[1,256,1024]{2,1,0:T(8,128)(2,1)S(1)}, bf16[1,256,1024]{2,1,0:T(8,128)(2,1)}, u32[]{:S(2)}) copy-start(bf16[1,256,1024]{2,1,0:T(8,128)(2,1)} %param.8) | copy-start | bytes 1572868
  251.8 5.5 %collective-permute-start.1 = (bf16[256,1024]{0,1:T(8,128)(2,1)S(1)}, bf16[256,1024]{0,1:T(8,128)(2,1)S(1)}, u32[]{:S(2)}, u32[]{:S(2)}) collective-permute-start(bf16[256,1024]{0,1:T(8,128)(2,1)S(1)} %fusion.31), channel_id=1, source_target_pairs={{0,64},{64,0},{128,192},{192,128},{1,65},{65,1},{129,193},{193,129... | collective-permute-start | bytes 1572872 | tf_op jit(solution)/shard_map/ppermute | solution.py:39
  255.6 7.9 %collective-permute-start.7 = (bf16[512,256]{1,0:T(8,128)(2,1)S(1)}, bf16[512,256]{1,0:T(8,128)(2,1)S(1)}, u32[]{:S(2)}, u32[]{:S(2)}) collective-permute-start(bf16[512,256]{1,0:T(8,128)(2,1)S(1)} %dynamic-slice_bitcast_fusion.1), channel_id=1, source_target_pairs={{0,128},{64,192},{128,0},{192,64},{1,129},{65,193},{129,1},{193,65... | collective-permute-start | bytes 786440 | tf_op jit(solution)/shard_map/ppermute | solution.py:45
  257.6 11.5 %collective-permute-start.2 = (bf16[128,1024]{1,0:T(8,128)(2,1)S(1)}, bf16[128,1024]{1,0:T(8,128)(2,1)S(1)}, u32[]{:S(2)}, u32[]{:S(2)}) collective-permute-start(bf16[128,1024]{1,0:T(8,128)(2,1)S(1)} %dynamic-slice_bitcast_fusion), channel_id=1, source_target_pairs={{0,128},{64,192},{128,0},{192,64},{1,129},{65,193},{129,1},{193,65... | collective-permute-start | bytes 786440 | tf_op jit(solution)/shard_map/ppermute | solution.py:45
  263.6 6.7 %copy-start.28 = (bf16[512,256]{1,0:T(8,128)(2,1)S(1)}, bf16[512,256]{1,0:T(8,128)(2,1)}, u32[]{:S(2)}) copy-start(bf16[512,256]{1,0:T(8,128)(2,1)} %convolution_convert_fusion.11) | copy-start | bytes 786436
  263.6 6.7 %copy-start.29 = (bf16[512,256]{1,0:T(8,128)(2,1)S(1)}, bf16[512,256]{1,0:T(8,128)(2,1)}, u32[]{:S(2)}) copy-start(bf16[512,256]{1,0:T(8,128)(2,1)} %convolution_convert_fusion.9) | copy-start | bytes 786436
  263.6 6.7 %copy-start.30 = (bf16[512,256]{1,0:T(8,128)(2,1)S(1)}, bf16[512,256]{1,0:T(8,128)(2,1)}, u32[]{:S(2)}) copy-start(bf16[512,256]{1,0:T(8,128)(2,1)} %convolution_convert_fusion.10) | copy-start | bytes 786436
  263.7 7.7 %collective-permute-start.8 = (bf16[512,256]{1,0:T(8,128)(2,1)S(1)}, bf16[512,256]{1,0:T(8,128)(2,1)S(1)}, u32[]{:S(2)}, u32[]{:S(2)}) collective-permute-start(bf16[512,256]{1,0:T(8,128)(2,1)S(1)} %get-tuple-element.15), channel_id=1, source_target_pairs={{0,64},{64,0},{128,192},{192,128},{1,65},{65,1},{129,193},{193,129... | collective-permute-start | bytes 786440 | tf_op jit(solution)/shard_map/ppermute | solution.py:47
  269.2 3.5 %copy-start.1 = (bf16[4,256,256]{2,1,0:T(8,128)(2,1)S(1)}, bf16[4,256,256]{2,1,0:T(8,128)(2,1)}, u32[]{:S(2)}) copy-start(bf16[4,256,256]{2,1,0:T(8,128)(2,1)} %param.9) | copy-start | bytes 1572868
  269.3 2.1 collective-permute-start.3
  (12 other events, 15.9 us)

commit v10 on v9

--- a/solution.py
+++ b/solution.py
@@ -45,10 +45,8 @@
     got = lax.ppermute(mine, "dp", row_swap)
     total = (mine.astype(jnp.float32) + got.astype(jnp.float32)).astype(jnp.bfloat16)
     got = lax.ppermute(total, "dp", core_swap)
-    full = jnp.zeros((2,) + total.shape, jnp.float32)
-    full = lax.dynamic_update_index_in_dim(full, total.astype(jnp.float32), core, 0)
-    full = lax.dynamic_update_index_in_dim(full, got.astype(jnp.float32), 1 - core, 0)
-    return full.reshape(grad.shape), tied
+    full = jnp.where(core == 0, jnp.stack([total, got]), jnp.stack([got, total]))
+    return full.astype(jnp.float32).reshape(grad.shape), tied
 
 
 def shards(tokens, cotangent, up_width, up_hidden, down_hidden, down_width):

time: 274 us -> 273 us (level)
  transfers between devices with their start and end apart: 13 -> 13, of which waited for: 10 -> 9; matrix products, arithmetic and copies ran while one was open for 25% -> 25% of each run, Pallas kernels for 0% -> 0%
where the time goes in v10:
time: 273 us; the launch traced here: 272 us
  waiting for transfers between devices  131 us (48%)
  starting transfers between devices  60.9 us (22%)
  local copies, waits for them, and re-layouts  39.4 us (14%)
  matrix products  31.6 us (12%)
  other arithmetic  7.8 us (3%)
    all_to_all x2, waiting for transfers between devices, shards(): recv = lax.all_to_all(send, 'block', 0, 0, tiled=True)  69 us
    dot_general x24, matrix products, dot(): lax.dot_general(left, right, ((left_dims, right_dims), batch), preferred_...  31.6 us
    all_to_all x2, waiting for transfers between devices, shards(): recv2 = lax.all_to_all(send2, 'block', 0, 0, tiled=True)  30 us
    ppermute x3, waiting for transfers between devices, dp_sum(): got = lax.ppermute(mine, 'dp', row_swap)  28.2 us
    all_to_all x2, starting transfers between devices, shards(): recv = lax.all_to_all(send, 'block', 0, 0, tiled=True)  24.6 us
    all_to_all x2, starting transfers between devices, shards(): recv2 = lax.all_to_all(send2, 'block', 0, 0, tiled=True)  20.3 us
    another operation x8, local copies, waits for them, and re-layouts, shards(): jnp.stack([back_t, tile_grad_t], axis=0)  16.6 us
    ppermute x3, starting transfers between devices, dp_sum(): got = lax.ppermute(own, 'dp', core_swap)  8.67 us
  transfers between devices with their start and end apart: 13, of which 9 were waited for; matrix products, arithmetic and copies ran while one was open for 25% of the time, Pallas kernels for 0%

profile of v10, /device:TPU:1, one launch (start us, length us, event | category | flops | bytes accessed | tf_op | source)
XLA Modules:
  0.0 271.8 jit_solution(2531603834247629897)
XLA Ops:
  0.7 1.7 convolution_convert_fusion.3
  5.3 15.1 %all-to-all-start = ((bf16[64,2,16,512]{3,2,1,0:T(8,128)(2,1)}), bf16[64,2,16,512]{3,2,1,0:T(8,128)(2,1)S(1)}, u32[]{:S(2)}, u32[]{:S(2)}) async-start(bf16[64,2,16,512]{3,2,1,0:T(8,128)(2,1)} %pad_maximum_fusion), calls=%async_computation | async-start | bytes 4194304 | tf_op jit(solution)/shard_map/all_to_all | solution.py:73
  25.0 44.4 %all-to-all-done = bf16[64,2,16,512]{3,2,1,0:T(8,128)(2,1)S(1)} async-done(((bf16[64,2,16,512]{3,2,1,0:T(8,128)(2,1)}), bf16[64,2,16,512]{3,2,1,0:T(8,128)(2,1)S(1)}, u32[]{:S(2)}, u32[]{:S(2)}) %all-to-all-start) | async-done | bytes 2097184 | tf_op jit(solution)/shard_map/all_to_all | solution.py:73
  69.4 9.5 %all-to-all-start.2 = ((bf16[64,2,16,512]{3,2,1,0:T(8,128)(2,1)}), bf16[64,2,16,512]{3,2,1,0:T(8,128)(2,1)}, u32[]{:S(2)}, u32[]{:S(2)}) async-start(bf16[64,2,16,512]{3,2,1,0:T(8,128)(2,1)} %pad_maximum_fusion.2), calls=%async_computation.2 | async-start | bytes 4194304 | tf_op jit(solution)/shard_map/all_to_all | solution.py:73
  80.3 1.8 copy.101
  82.9 2.0 fusion.18
  86.3 2.1 stack.76
  88.5 2.5 copy.104
  91.0 2.8 %fusion.5 = bf16[4,256,512]{1,2,0:T(8,128)(2,1)S(1)} fusion(f32[4,512,256]{2,1,0:T(8,128)} %get-tuple-element.25, bf16[4,256,256]{2,1,0:T(8,128)(2,1)S(1)} %copy-done.19, bf16[4,256,512]{2,0,1:T(4,128)(2,1)S(1)} %bitcast.176), kind=kOutput, calls=%fused_computation.7 | convolution fusion | flops 273678336 | bytes 4718592 | tf_op jit(solution)/shard_map/dot_general | solution.py:22
  96.2 2.1 stack.77
  100.0 2.5 copy.106
  102.5 24.5 %all-to-all-done.2 = bf16[64,2,16,512]{3,2,1,0:T(8,128)(2,1)} async-done(((bf16[64,2,16,512]{3,2,1,0:T(8,128)(2,1)}), bf16[64,2,16,512]{3,2,1,0:T(8,128)(2,1)}, u32[]{:S(2)}, u32[]{:S(2)}) %all-to-all-start.2) | async-done | bytes 2097184 | tf_op jit(solution)/shard_map/all_to_all | solution.py:73
  127.1 10.2 %all-to-all-start.1 = ((bf16[64,2,16,512]{3,2,1,0:T(8,128)(2,1)}), bf16[64,2,16,512]{3,2,1,0:T(8,128)(2,1)}, u32[]{:S(2)}, u32[]{:S(2)}) async-start(bf16[64,2,16,512]{3,2,1,0:T(8,128)(2,1)} %copy.106), calls=%async_computation.1 | async-start | bytes 4194304 | tf_op jit(solution)/shard_map/all_to_all | solution.py:91
  137.3 2.8 %copy.110 = bf16[64,2,16,512]{3,0,2,1:T(8,128)(2,1)S(1)} copy(bf16[64,2,16,512]{3,2,1,0:T(8,128)(2,1)} %all-to-all-done.2) | data formatting | bytes 4194304 | tf_op jit(solution)/shard_map/all_to_all | solution.py:73
  141.9 1.7 fusion.14
  147.6 2.1 stack.81
  149.7 2.5 copy.119
  153.7 2.1 stack.80
  157.6 2.5 copy.120
  164.5 21.0 %all-to-all-done.1 = bf16[64,2,16,512]{3,2,1,0:T(8,128)(2,1)} async-done(((bf16[64,2,16,512]{3,2,1,0:T(8,128)(2,1)}), bf16[64,2,16,512]{3,2,1,0:T(8,128)(2,1)}, u32[]{:S(2)}, u32[]{:S(2)}) %all-to-all-start.1) | async-done | bytes 2097184 | tf_op jit(solution)/shard_map/all_to_all | solution.py:91
  185.5 10.0 %all-to-all-start.3 = ((bf16[64,2,16,512]{3,2,1,0:T(8,128)(2,1)}), bf16[64,2,16,512]{3,2,1,0:T(8,128)(2,1)}, u32[]{:S(2)}, u32[]{:S(2)}) async-start(bf16[64,2,16,512]{3,2,1,0:T(8,128)(2,1)} %copy.120), calls=%async_computation.3 | async-start | bytes 4194304 | tf_op jit(solution)/shard_map/all_to_all | solution.py:91
  195.5 2.1 fusion.22
  197.9 2.1 collective-permute-start.4
  200.0 2.3 collective-permute-done.4
  202.9 21.0 %collective-permute-done.5 = bf16[1,4,256,256]{3,2,1,0:T(8,128)(2,1)S(1)} collective-permute-done((bf16[1,4,256,256]{3,2,1,0:T(8,128)(2,1)S(1)}, bf16[1,4,256,256]{3,2,1,0:T(8,128)(2,1)S(1)}, u32[]{:S(2)}, u32[]{:S(2)}) %collective-permute-start.5) | collective-permute-done | bytes 524320 | tf_op jit(solution)/shard_map/ppermute | solution.py:45
  224.0 2.8 %collective-permute-start.6 = (bf16[1,4,256,256]{3,2,1,0:T(8,128)(2,1)S(1)}, bf16[1,4,256,256]{3,2,1,0:T(8,128)(2,1)S(1)}, u32[]{:S(2)}, u32[]{:S(2)}) collective-permute-start(bf16[1,4,256,256]{3,2,1,0:T(8,128)(2,1)S(1)} %add_convert_fusion), channel_id=1, source_target_pairs={{0,64},{64,0},{128,192},{192,128},{1,65},{65,1},{129,193},{193,129... | collective-permute-start | bytes 1572872 | tf_op jit(solution)/shard_map/ppermute | solution.py:47
  230.0 1.8 fusion.64
  234.7 9.0 %all-to-all-done.3 = bf16[64,2,16,512]{3,2,1,0:T(8,128)(2,1)} async-done(((bf16[64,2,16,512]{3,2,1,0:T(8,128)(2,1)}), bf16[64,2,16,512]{3,2,1,0:T(8,128)(2,1)}, u32[]{:S(2)}, u32[]{:S(2)}) %all-to-all-start.3) | async-done | bytes 2097184 | tf_op jit(solution)/shard_map/all_to_all | solution.py:91
  243.7 1.8 fusion.63
  246.0 5.3 %collective-permute-start = (bf16[1024,256]{1,0:T(8,128)(2,1)S(1)}, bf16[1024,256]{1,0:T(8,128)(2,1)S(1)}, u32[]{:S(2)}, u32[]{:S(2)}) collective-permute-start(bf16[1024,256]{1,0:T(8,128)(2,1)S(1)} %fusion.29), channel_id=1, source_target_pairs={{0,64},{64,0},{128,192},{192,128},{1,65},{65,1},{129,193},{193,129... | collective-permute-start | bytes 1572872 | tf_op jit(solution)/shard_map/ppermute | solution.py:39
  258.6 4.2 %collective-permute-done.7 = bf16[512,256]{1,0:T(8,128)(2,1)S(1)} collective-permute-done((bf16[512,256]{1,0:T(8,128)(2,1)S(1)}, bf16[512,256]{1,0:T(8,128)(2,1)S(1)}, u32[]{:S(2)}, u32[]{:S(2)}) %collective-permute-start.7) | collective-permute-done | bytes 262176 | tf_op jit(solution)/shard_map/ppermute | solution.py:45
  265.3 3.0 %collective-permute-done.2 = bf16[128,1024]{1,0:T(8,128)(2,1)S(1)} collective-permute-done((bf16[128,1024]{1,0:T(8,128)(2,1)S(1)}, bf16[128,1024]{1,0:T(8,128)(2,1)S(1)}, u32[]{:S(2)}, u32[]{:S(2)}) %collective-permute-start.2) | collective-permute-done | bytes 262176 | tf_op jit(solution)/shard_map/ppermute | solution.py:45
  (115 shorter events, 49.2 us)
Async XLA Ops:
  0.6 82.2 %copy-start = (bf16[4,256,256]{2,1,0:T(8,128)(2,1)S(1)}, bf16[4,256,256]{2,1,0:T(8,128)(2,1)}, u32[]{:S(2)}) copy-start(bf16[4,256,256]{2,1,0:T(8,128)(2,1)} %param.9) | copy-start | bytes 1572868
  0.6 1.7 copy-start.20
  5.3 64.1 %all-to-all-start = ((bf16[64,2,16,512]{3,2,1,0:T(8,128)(2,1)}), bf16[64,2,16,512]{3,2,1,0:T(8,128)(2,1)S(1)}, u32[]{:S(2)}, u32[]{:S(2)}) async-start(bf16[64,2,16,512]{3,2,1,0:T(8,128)(2,1)} %pad_maximum_fusion), calls=%async_computation | async-start | bytes 4194304 | tf_op jit(solution)/shard_map/all_to_all | solution.py:73
  69.4 57.7 %all-to-all-start.2 = ((bf16[64,2,16,512]{3,2,1,0:T(8,128)(2,1)}), bf16[64,2,16,512]{3,2,1,0:T(8,128)(2,1)}, u32[]{:S(2)}, u32[]{:S(2)}) async-start(bf16[64,2,16,512]{3,2,1,0:T(8,128)(2,1)} %pad_maximum_fusion.2), calls=%async_computation.2 | async-start | bytes 4194304 | tf_op jit(solution)/shard_map/all_to_all | solution.py:73
  82.9 2.0 copy-start.19
  88.5 2.5 copy-start.6
  127.1 58.4 %all-to-all-start.1 = ((bf16[64,2,16,512]{3,2,1,0:T(8,128)(2,1)}), bf16[64,2,16,512]{3,2,1,0:T(8,128)(2,1)}, u32[]{:S(2)}, u32[]{:S(2)}) async-start(bf16[64,2,16,512]{3,2,1,0:T(8,128)(2,1)} %copy.106), calls=%async_computation.1 | async-start | bytes 4194304 | tf_op jit(solution)/shard_map/all_to_all | solution.py:91
  141.1 2.5 copy-start.10
  141.9 1.7 copy-start.4
  149.7 2.5 copy-start.2
  157.6 2.5 copy-start.9
  164.4 31.1 %copy-start.3 = (bf16[4,256,512]{1,2,0:T(8,128)(2,1)S(1)}, bf16[4,256,512]{1,2,0:T(8,128)(2,1)}, u32[]{:S(2)}) copy-start(bf16[4,256,512]{1,2,0:T(8,128)(2,1)} %get-tuple-element.26) | copy-start | bytes 3145732
  185.5 58.2 %all-to-all-start.3 = ((bf16[64,2,16,512]{3,2,1,0:T(8,128)(2,1)}), bf16[64,2,16,512]{3,2,1,0:T(8,128)(2,1)}, u32[]{:S(2)}, u32[]{:S(2)}) async-start(bf16[64,2,16,512]{3,2,1,0:T(8,128)(2,1)} %copy.120), calls=%async_computation.3 | async-start | bytes 4194304 | tf_op jit(solution)/shard_map/all_to_all | solution.py:91
  197.9 4.4 %collective-permute-start.4 = (bf16[2,4,256,256]{3,2,1,0:T(8,128)(2,1)S(1)}, bf16[2,4,256,256]{3,2,1,0:T(8,128)(2,1)S(1)}, u32[]{:S(2)}, u32[]{:S(2)}) collective-permute-start(bf16[2,4,256,256]{3,2,1,0:T(8,128)(2,1)S(1)} %fusion.12), channel_id=1, source_target_pairs={{0,64},{64,0},{128,192},{192,128},{1,65},{65,1},{129,193},{193,129... | collective-permute-start | bytes 3145736 | tf_op jit(solution)/shard_map/ppermute | solution.py:39
  202.4 21.5 %collective-permute-start.5 = (bf16[1,4,256,256]{3,2,1,0:T(8,128)(2,1)S(1)}, bf16[1,4,256,256]{3,2,1,0:T(8,128)(2,1)S(1)}, u32[]{:S(2)}, u32[]{:S(2)}) collective-permute-start(bf16[1,4,256,256]{3,2,1,0:T(8,128)(2,1)S(1)} %add_convert_fusion.1), channel_id=1, source_target_pairs={{0,128},{64,192},{128,0},{192,64},{1,129},{65,193},{129,1},{193,65... | collective-permute-start | bytes 1572872 | tf_op jit(solution)/shard_map/ppermute | solution.py:45
  224.0 4.3 %collective-permute-start.6 = (bf16[1,4,256,256]{3,2,1,0:T(8,128)(2,1)S(1)}, bf16[1,4,256,256]{3,2,1,0:T(8,128)(2,1)S(1)}, u32[]{:S(2)}, u32[]{:S(2)}) collective-permute-start(bf16[1,4,256,256]{3,2,1,0:T(8,128)(2,1)S(1)} %add_convert_fusion), channel_id=1, source_target_pairs={{0,64},{64,0},{128,192},{192,128},{1,65},{65,1},{129,193},{193,129... | collective-permute-start | bytes 1572872 | tf_op jit(solution)/shard_map/ppermute | solution.py:47
  230.0 1.8 copy-start.23
  243.7 1.9 copy-start.14
  245.5 6.2 %copy-start.17 = (bf16[64,1,16,512]{3,2,1,0:T(8,128)(2,1)}, bf16[64,1,16,512]{3,2,1,0:T(8,128)(2,1)S(1)}, u32[]{:S(2)}) copy-start(bf16[64,1,16,512]{3,2,1,0:T(8,128)(2,1)S(1)} %get-tuple-element.16) | copy-start | bytes 3145732
  245.5 5.8 %copy-start.13 = (f32[1024,256]{1,0:T(8,128)S(1)}, f32[1024,256]{1,0:T(8,128)}, u32[]{:S(2)}) copy-start(f32[1024,256]{1,0:T(8,128)} %fusion.60) | copy-start | bytes 3145732
  245.5 5.8 %copy-start.25 = (bf16[1024,256]{1,0:T(8,128)(2,1)S(1)}, bf16[1024,256]{1,0:T(8,128)(2,1)}, u32[]{:S(2)}) copy-start(bf16[1024,256]{1,0:T(8,128)(2,1)} %param.6) | copy-start | bytes 1572868
  246.0 7.0 %copy-start.21 = (bf16[1,1024,256]{2,1,0:T(8,128)(2,1)S(1)}, bf16[1,1024,256]{2,1,0:T(8,128)(2,1)}, u32[]{:S(2)}) copy-start(bf16[1,1024,256]{2,1,0:T(8,128)(2,1)} %param.11) | copy-start | bytes 1572868
  246.0 8.7 %collective-permute-start = (bf16[1024,256]{1,0:T(8,128)(2,1)S(1)}, bf16[1024,256]{1,0:T(8,128)(2,1)S(1)}, u32[]{:S(2)}, u32[]{:S(2)}) collective-permute-start(bf16[1024,256]{1,0:T(8,128)(2,1)S(1)} %fusion.29), channel_id=1, source_target_pairs={{0,64},{64,0},{128,192},{192,128},{1,65},{65,1},{129,193},{193,129... | collective-permute-start | bytes 1572872 | tf_op jit(solution)/shard_map/ppermute | solution.py:39
  251.3 2.2 copy-start.22
  251.7 4.8 %collective-permute-start.1 = (bf16[256,1024]{0,1:T(8,128)(2,1)S(1)}, bf16[256,1024]{0,1:T(8,128)(2,1)S(1)}, u32[]{:S(2)}, u32[]{:S(2)}) collective-permute-start(bf16[256,1024]{0,1:T(8,128)(2,1)S(1)} %fusion.31), channel_id=1, source_target_pairs={{0,64},{64,0},{128,192},{192,128},{1,65},{65,1},{129,193},{193,129... | collective-permute-start | bytes 1572872 | tf_op jit(solution)/shard_map/ppermute | solution.py:39
  254.8 7.9 %collective-permute-start.7 = (bf16[512,256]{1,0:T(8,128)(2,1)S(1)}, bf16[512,256]{1,0:T(8,128)(2,1)S(1)}, u32[]{:S(2)}, u32[]{:S(2)}) collective-permute-start(bf16[512,256]{1,0:T(8,128)(2,1)S(1)} %dynamic-slice_bitcast_fusion.1), channel_id=1, source_target_pairs={{0,128},{64,192},{128,0},{192,64},{1,129},{65,193},{129,1},{193,65... | collective-permute-start | bytes 786440 | tf_op jit(solution)/shard_map/ppermute | solution.py:45
  256.9 7.4 %copy-start.26 = (bf16[512,256]{1,0:T(8,128)(2,1)S(1)}, bf16[512,256]{1,0:T(8,128)(2,1)}, u32[]{:S(2)}) copy-start(bf16[512,256]{1,0:T(8,128)(2,1)} %convolution_convert_fusion.9) | copy-start | bytes 786436
  256.9 7.4 %copy-start.27 = (bf16[512,256]{1,0:T(8,128)(2,1)S(1)}, bf16[512,256]{1,0:T(8,128)(2,1)}, u32[]{:S(2)}) copy-start(bf16[512,256]{1,0:T(8,128)(2,1)} %convolution_convert_fusion.10) | copy-start | bytes 786436
  256.9 11.4 %collective-permute-start.2 = (bf16[128,1024]{1,0:T(8,128)(2,1)S(1)}, bf16[128,1024]{1,0:T(8,128)(2,1)S(1)}, u32[]{:S(2)}, u32[]{:S(2)}) collective-permute-start(bf16[128,1024]{1,0:T(8,128)(2,1)S(1)} %dynamic-slice_bitcast_fusion), channel_id=1, source_target_pairs={{0,128},{64,192},{128,0},{192,64},{1,129},{65,193},{129,1},{193,65... | collective-permute-start | bytes 786440 | tf_op jit(solution)/shard_map/ppermute | solution.py:45
  262.8 6.6 %collective-permute-start.8 = (bf16[512,256]{1,0:T(8,128)(2,1)S(1)}, bf16[512,256]{1,0:T(8,128)(2,1)S(1)}, u32[]{:S(2)}, u32[]{:S(2)}) collective-permute-start(bf16[512,256]{1,0:T(8,128)(2,1)S(1)} %add_convert_fusion.4), channel_id=1, source_target_pairs={{0,64},{64,0},{128,192},{192,128},{1,65},{65,1},{129,193},{193,129... | collective-permute-start | bytes 786440 | tf_op jit(solution)/shard_map/ppermute | solution.py:47
  268.4 2.2 collective-permute-start.3
  269.5 2.2 copy-start.1
  (9 other events, 12.0 us)
